TPU v7x, 512 devices: a whole 4x8x8 slice. The times are simulated.
512 devices in a mesh: seq: 128 (over z, y, core), head: 4 (over x).
Axes of the slice: x: 4, y: 8, z: 8, core: 2. Of those that a mesh axis runs over, the one named last changes fastest.
Arguments:
- hidden: bfloat16 [16384, 1024], P('seq', 'head'), may hold values from -6 to 6
- queries: bfloat16 [16384, 1024], P('seq', 'head'), may hold values from -40 to 40
- suffix_keys: bfloat16 [16384, 1024], P('seq', 'head'), may hold values from -4 to 4
- suffix_values: bfloat16 [16384, 1024], P('seq', 'head'), may hold values from -6 to 6
- lengths: int32 [128], P('seq'), may hold values from 1 to 128, 10240 in all
- key_cache: bfloat16 [128, 32, 1024], P('seq', None, 'head'), may hold values from -6 to 6
- value_cache: bfloat16 [128, 32, 1024], P('seq', None, 'head'), may hold values from -6 to 6
- page_group: int32 [128], replicated, may hold values from 0 to 3, as said below
- out_weight: bfloat16 [1024, 1024], P('head'), may hold values from -0.1875 to 0.1875
- norm_gain: float32 [1024], replicated, may hold values from 0.1 to 1.9
- router_weight: bfloat16 [1024, 16], P('head'), may hold values from -0.1875 to 0.1875
- routes: int32 [16384, 2], P('seq'), may hold values from 0 to 15, all different within a row; in each aligned block of 16 rows (0 to 15, 16 to 31, ...) at most 2 rows name the same one
- gate_weight: bfloat16 [128, 1024, 2816], P('seq', None, 'head'), as said below
- up_weight: bfloat16 [128, 1024, 2816], P('seq', None, 'head'), as said below
- down_weight: bfloat16 [128, 1024, 2816], P('seq', None, 'head'), as said below
- destinations: int32 [128], replicated, may hold values from 0 to 127, as said below
Outputs:
- layer_output: bfloat16 [16384, 1024], P('seq', 'head')
Inputs may be any that keep to these rules, and one draw needn't show every extreme that they name: `lengths`: the largest length is 128. `page_group`: each of the 4 groups is named by exactly 32 entries. `routes`: each row names 2 different experts; in each aligned block of 16 rows no expert is named by more than 2 rows. `gate_weight`: copies h and h2 with h // 8 == h2 // 8 are equal. `up_weight`: copies h and h2 with h // 8 == h2 // 8 are equal. `down_weight`: copies h and h2 with h // 8 == h2 // 8 are equal. `destinations`: A permutation of the requests in which exactly 32 requests change place.
All inputs are finite; a program needn't handle non-finite values. No bound on the sum of `lengths` on one device may be relied on, other than what follows from the above.
Results may differ from a plain program's by a relative error of at most 0.0065.
Values may be sent and summed in bfloat16 or wider, within the bound.
No kernel may reach another device: no remote copies, remote signals or barrier semaphores. Data moves between devices by JAX's collectives and lax.ppermute only.
A program may use at most 64 MiB of HBM per device.

v0:
```python
import jax
import jax.numpy as jnp
from jax import lax
from jax.sharding import PartitionSpec as P

DH = 64
EXPERTS = 16
TOPK = 2
GROUPS = 4


norm_eps = 1e-06


def page_inverse(page_group, group_pages, groups):
    page_total = page_group.shape[0]
    onehot = (page_group[:, None] == jnp.arange(groups, dtype=jnp.int32)[None, :]).astype(jnp.int32)
    page_rank = jnp.sum((jnp.cumsum(onehot, axis=0) - 1) * onehot, axis=1)
    target = page_group * group_pages + page_rank
    return (
        jnp.zeros((page_total,), jnp.int32).at[target].set(jnp.arange(page_total, dtype=jnp.int32))
    )


def attend_rows(query_rows, key_rows, value_rows, prefix_keys, prefix_values, length, head_total):
    row_count = query_rows.shape[0]
    head_size = query_rows.shape[1] // head_total
    scale = head_size ** (-0.5)

    def heads_of(array):
        return array.reshape(array.shape[0], head_total, head_size)

    prefix_scores = (
        jnp.einsum(
            "qhd,khd->hqk",
            heads_of(query_rows),
            heads_of(prefix_keys),
            preferred_element_type=jnp.float32,
        )
        * scale
    )
    suffix_scores = (
        jnp.einsum(
            "qhd,khd->hqk",
            heads_of(query_rows),
            heads_of(key_rows),
            preferred_element_type=jnp.float32,
        )
        * scale
    )
    query_pos = jnp.arange(row_count, dtype=jnp.int32)[:, None]
    key_pos = jnp.arange(row_count, dtype=jnp.int32)[None, :]
    allowed = (key_pos <= query_pos) & (key_pos < length)
    suffix_scores = jnp.where(allowed[None], suffix_scores, -jnp.inf)
    row_max = jnp.maximum(jnp.max(prefix_scores, axis=2), jnp.max(suffix_scores, axis=2))[..., None]
    prefix_exp = jnp.exp(prefix_scores - row_max)
    suffix_exp = jnp.exp(suffix_scores - row_max)
    denominators = jnp.sum(prefix_exp, axis=2, keepdims=True) + jnp.sum(
        suffix_exp, axis=2, keepdims=True
    )
    prefix_probs = (prefix_exp / denominators).astype(jnp.bfloat16)
    suffix_probs = (suffix_exp / denominators).astype(jnp.bfloat16)
    mixed_heads = jnp.einsum(
        "hqk,khd->qhd", prefix_probs, heads_of(prefix_values), preferred_element_type=jnp.float32
    )
    mixed_heads = mixed_heads + jnp.einsum(
        "hqk,khd->qhd", suffix_probs, heads_of(value_rows), preferred_element_type=jnp.float32
    )
    return mixed_heads.reshape(row_count, head_total * head_size).astype(jnp.bfloat16)


def slot_table(route_rows, replicas, per_device, experts):
    row_count, topk_count = route_rows.shape
    sub_rows = row_count // replicas
    flat_routes = route_rows.reshape(replicas, sub_rows * topk_count)
    onehot = (flat_routes[..., None] == jnp.arange(experts, dtype=jnp.int32)).astype(jnp.int32)
    slot_rank = jnp.sum((jnp.cumsum(onehot, axis=1) - 1) * onehot, axis=2).reshape(-1)
    expert_flat = route_rows.reshape(-1)
    block_of = jnp.arange(row_count * topk_count, dtype=jnp.int32) // (sub_rows * topk_count)
    target_device = expert_flat // per_device * replicas + block_of
    local_slot = expert_flat % per_device
    return (target_device, local_slot, slot_rank)


def on_device(
    hidden,
    queries,
    suffix_keys,
    suffix_values,
    lengths,
    key_cache,
    value_cache,
    page_group,
    out_weight,
    norm_gain,
    router_weight,
    routes,
    gate_weight,
    up_weight,
    down_weight,
    destinations,
):
    seq_count = lax.axis_size("seq")
    head_count = lax.axis_size("head")
    seq_index = lax.axis_index("seq")
    head_index = lax.axis_index("head")
    row_count = hidden.shape[0]
    column_width = hidden.shape[1]
    features = queries.shape[1]
    local_heads = features // DH
    block_devices = seq_count // GROUPS
    page_local = key_cache.shape[0]
    page_rows = key_cache.shape[1]
    group_pages = page_local * block_devices
    replicas = max(1, seq_count // EXPERTS)
    per_device = max(1, EXPERTS // seq_count)
    capacity = 5 * row_count * TOPK // (4 * EXPERTS * replicas)
    inverse = page_inverse(page_group, group_pages, GROUPS)
    group_index = seq_index // block_devices
    half_width = page_rows * features
    local_pages = jnp.concatenate(
        [key_cache.reshape(page_local, half_width), value_cache.reshape(page_local, half_width)],
        axis=1,
    )
    all_pages = lax.all_gather(local_pages, "seq", axis=0, tiled=True)
    chosen = lax.dynamic_slice_in_dim(inverse, group_index * group_pages, group_pages, 0)
    held_pages = jnp.take(all_pages, chosen, axis=0)
    prefix_keys = held_pages[:, :half_width].reshape(group_pages * page_rows, features)
    prefix_values = held_pages[:, half_width:].reshape(group_pages * page_rows, features)
    length = lengths[0]
    attended = attend_rows(
        queries, suffix_keys, suffix_values, prefix_keys, prefix_values, length, local_heads
    )
    partial_proj = jnp.dot(attended, out_weight, preferred_element_type=jnp.float32)
    own_columns = lax.dynamic_slice_in_dim(
        partial_proj, head_index * column_width, column_width, 1
    ) + hidden.astype(jnp.float32)
    partial_proj = lax.dynamic_update_slice_in_dim(
        partial_proj, own_columns, head_index * column_width, 1
    )
    resid = lax.psum(partial_proj, "head")
    normed = (
        resid * lax.rsqrt(jnp.mean(resid * resid, axis=1, keepdims=True) + norm_eps) * norm_gain
    ).astype(jnp.bfloat16)
    normed_columns = lax.dynamic_slice_in_dim(normed, head_index * column_width, column_width, 1)
    logits = lax.psum(
        jnp.dot(normed_columns, router_weight, preferred_element_type=jnp.float32), "head"
    )
    chosen_logits = jnp.take_along_axis(logits, routes, axis=1)
    gate_first = jax.nn.sigmoid(chosen_logits[:, 0] - chosen_logits[:, 1])
    gate_second = jax.nn.sigmoid(chosen_logits[:, 1] - chosen_logits[:, 0])
    target_device, local_slot, slot_rank = slot_table(routes, replicas, per_device, EXPERTS)
    token_index = jnp.arange(row_count * TOPK, dtype=jnp.int32) // TOPK
    send_rows = jnp.zeros((seq_count, per_device, capacity, normed.shape[1]), jnp.bfloat16)
    send_rows = send_rows.at[target_device, local_slot, slot_rank].set(
        jnp.take(normed, token_index, axis=0)
    )
    slots = lax.all_to_all(send_rows, "seq", split_axis=0, concat_axis=0, tiled=True)
    gate_act = jnp.einsum("spnd,pdf->spnf", slots, gate_weight, preferred_element_type=jnp.float32)
    up_act = jnp.einsum("spnd,pdf->spnf", slots, up_weight, preferred_element_type=jnp.float32)
    expert_hidden = (jax.nn.gelu(gate_act, approximate=True) * up_act).astype(jnp.bfloat16)
    partial_out = jnp.einsum(
        "spnf,pdf->spnd", expert_hidden, down_weight, preferred_element_type=jnp.float32
    )
    part_dims = partial_out.shape
    split_part = partial_out.reshape(
        part_dims[0], part_dims[1], part_dims[2], head_count, part_dims[3] // head_count
    )
    arrived = lax.all_to_all(
        lax.all_to_all(
            split_part.astype(jnp.bfloat16), "seq", split_axis=0, concat_axis=0, tiled=True
        ),
        "head",
        split_axis=3,
        concat_axis=3,
        tiled=True,
    ).astype(split_part.dtype)
    returned = jnp.sum(arrived, axis=3).astype(jnp.bfloat16)
    picked = (
        returned[target_device, local_slot, slot_rank]
        .astype(jnp.float32)
        .reshape(row_count, TOPK, column_width)
    )
    resid_columns = lax.dynamic_slice_in_dim(resid, head_index * column_width, column_width, 1)
    layer = resid_columns + gate_first[:, None] * picked[:, 0] + gate_second[:, None] * picked[:, 1]
    layer = layer.astype(jnp.bfloat16)
    live_rows = jnp.arange(row_count, dtype=jnp.int32) < length
    layer = jnp.where(live_rows[:, None], layer, jnp.zeros_like(layer))
    out_pieces = layer.reshape(seq_count, row_count // seq_count, column_width)
    scattered = lax.all_to_all(out_pieces, "seq", split_axis=0, concat_axis=0, tiled=True)
    inverse_destination = (
        jnp.zeros((seq_count,), jnp.int32)
        .at[destinations]
        .set(jnp.arange(seq_count, dtype=jnp.int32))
    )
    reordered = jnp.take(scattered, inverse_destination, axis=0)
    settled = lax.all_to_all(reordered, "seq", split_axis=0, concat_axis=0, tiled=True)
    return settled.reshape(row_count, column_width)


def solution(mesh):
    return jax.shard_map(
        on_device,
        mesh=mesh,
        in_specs=(
            P("seq", "head"),
            P("seq", "head"),
            P("seq", "head"),
            P("seq", "head"),
            P("seq"),
            P("seq", None, "head"),
            P("seq", None, "head"),
            P(),
            P("head", None),
            P(),
            P("head", None),
            P("seq", None),
            P("seq", None, "head"),
            P("seq", None, "head"),
            P("seq", None, "head"),
            P(),
        ),
        out_specs=P("seq", "head"),
        check_vma=False,
    )
```

profile of v0, /device:TPU:1, one launch (start us, length us, event | category | flops | bytes accessed | tf_op | source)
XLA Modules:
  0.0 332.7 jit_solution(16132102906732446111)
XLA Ops:
  12.4 1.6 copy.116
  15.8 1.2 compare_select_fusion.6
  17.0 1.0 scatter_custom_fusion.1
  18.9 1.5 fusion.81
  20.4 83.8 %all-gather.3.cloned.1.call-done = bf16[128,1,16384]{2,1,0:T(2,128)(2,1)} async-done(((bf16[1,1,16384]{2,1,0:T(2,128)(2,1)}), bf16[128,1,16384]{2,1,0:T(2,128)(2,1)}) %all-gather.3.cloned.1.call-update) | async-done | bytes 4194320 | tf_op jit(solution)/shard_map/all_gather | solution.py:125
  104.2 9.9 %copy.185 = bf16[128,1,16384]{2,0,1:T(8,128)(2,1)} copy(bf16[128,1,16384]{2,1,0:T(2,128)(2,1)} %all-gather.3.cloned.1.call-done) | data formatting | bytes 8388608
  114.1 4.8 %gather_fusion = bf16[32,16384]{1,0:T(8,128)(2,1)S(1)} fusion(bf16[128,16384]{1,0:T(8,128)(2,1)} %bitcast.164, s32[1024]{0:T(1024)S(1)} %pad_clamp_fusion.2), kind=kCustom, calls=%fused_computation | custom fusion | bytes 2097280 | tf_op jit(solution)/shard_map/jit(_take)/gather | solution.py:127
  120.0 2.1 reshape_reshape.7
  122.1 1.7 bitcast_reduce_fusion
  125.4 3.3 reshape_reshape.6
  129.4 2.0 convolution_bitcast_fusion.1
  133.6 47.2 %all-reduce.2.cloned.1.call-done = f32[128,1024]{1,0:T(8,128)} async-done(((f32[128,1024]{1,0:T(8,128)}), f32[128,1024]{1,0:T(8,128)}) %all-reduce.2.cloned.1.call-update) | async-done | bytes 524304 | tf_op jit(solution)/shard_map/psum | solution.py:141
  180.8 1.2 multiply_reduce_fusion
  182.0 1.2 multiply_convert_fusion
  183.1 1.2 gather_fusion.1
  184.7 15.9 %scatter_fusion = bf16[128,2,1024]{2,1,0:T(2,128)(2,1)S(1)} fusion(bf16[128,2,1024]{2,1,0:T(2,128)(2,1)S(1)} %broadcast.370, s32[256]{0:T(256)S(1)} %bitcast.165, bf16[256,1024]{1,0:T(8,128)(2,1)S(1)} %broadcast_select_fusion.1), kind=kCustom, calls=%fused_computation.7 | custom fusion | bytes 1574912 | tf_op jit(solution)/shard_map/scatter | solution.py:155
  200.6 36.9 %all_to_all.25 = bf16[128,1,2,1024]{3,2,1,0:T(2,128)(2,1)S(1)} all-to-all(bf16[128,1,2,1024]{3,2,1,0:T(2,128)(2,1)S(1)} %bitcast.163), channel_id=1, replica_groups=mesh['seq'=128,'head'=4] {'seq'}, dimensions={0} | all-to-all | bytes 1048576 | tf_op jit(solution)/shard_map/all_to_all | solution.py:158
  237.5 2.0 fusion.42
  239.5 3.2 fusion.23
  243.1 1.0 copy.126
  244.1 5.4 %all-to-all-start.1 = ((bf16[128,1,2,4,256]{4,3,2,1,0:T(4,128)(2,1)}), bf16[128,1,2,4,256]{4,3,2,1,0:T(4,128)(2,1)S(1)}, u32[]{:S(2)}, u32[]{:S(2)}) async-start(bf16[128,1,2,4,256]{4,3,2,1,0:T(4,128)(2,1)} %copy.126), calls=%async_computation.1 | async-start | bytes 1048576 | tf_op jit(solution)/shard_map/all_to_all | solution.py:170
  249.7 1.1 scatter_custom_fusion
  251.0 8.1 %psum.15 = f32[128,16]{0,1:T(8,128)S(1)} all-reduce(f32[128,16]{0,1:T(8,128)S(1)} %fusion.65), channel_id=1, replica_groups=mesh['seq'=128,'head'=4] {'head'}, use_global_device_ids=true, to_apply=%region_10.11 | all-reduce | flops 2048 | bytes 16384 | tf_op jit(solution)/shard_map/psum | solution.py:146
  259.1 2.2 gather_fusion.4
  261.5 8.5 %all-to-all-done.1 = bf16[128,1,2,4,256]{4,3,2,1,0:T(4,128)(2,1)S(1)} async-done(((bf16[128,1,2,4,256]{4,3,2,1,0:T(4,128)(2,1)}), bf16[128,1,2,4,256]{4,3,2,1,0:T(4,128)(2,1)S(1)}, u32[]{:S(2)}, u32[]{:S(2)}) %all-to-all-start.1) | async-done | bytes 524320 | tf_op jit(solution)/shard_map/all_to_all | solution.py:170
  270.9 3.6 %all-to-all-start.2 = ((bf16[128,1,2,4,256]{4,0,2,1,3:T(8,128)(2,1)}), bf16[128,1,2,4,256]{4,0,2,1,3:T(8,128)(2,1)S(1)}, u32[]{:S(2)}, u32[]{:S(2)}) async-start(bf16[128,1,2,4,256]{4,0,2,1,3:T(8,128)(2,1)} %copy.127), calls=%async_computation.2 | async-start | bytes 1048576 | tf_op jit(solution)/shard_map/all_to_all | solution.py:169
  274.6 9.7 %all-to-all-done.2 = bf16[128,1,2,4,256]{4,0,2,1,3:T(8,128)(2,1)S(1)} async-done(((bf16[128,1,2,4,256]{4,0,2,1,3:T(8,128)(2,1)}), bf16[128,1,2,4,256]{4,0,2,1,3:T(8,128)(2,1)S(1)}, u32[]{:S(2)}, u32[]{:S(2)}) %all-to-all-start.2) | async-done | bytes 524320 | tf_op jit(solution)/shard_map/all_to_all | solution.py:169
  284.5 1.6 gather_fusion.2
  286.5 1.0 fusion.63
  289.5 5.8 %all-to-all-start.3 = ((bf16[128,2,128]{2,1,0:T(2,128)(2,1)}), bf16[128,2,128]{2,1,0:T(2,128)(2,1)S(1)}, u32[]{:S(2)}, u32[]{:S(2)}) async-start(bf16[128,2,128]{2,1,0:T(2,128)(2,1)} %reshape.393), calls=%async_computation.3 | async-start | bytes 131072 | tf_op jit(solution)/shard_map/all_to_all | solution.py:190
  295.3 11.5 %all-to-all-done.3 = bf16[128,2,128]{2,1,0:T(2,128)(2,1)S(1)} async-done(((bf16[128,2,128]{2,1,0:T(2,128)(2,1)}), bf16[128,2,128]{2,1,0:T(2,128)(2,1)S(1)}, u32[]{:S(2)}, u32[]{:S(2)}) %all-to-all-start.3) | async-done | bytes 65568 | tf_op jit(solution)/shard_map/all_to_all | solution.py:190
  308.5 16.7 %all_to_all.26 = bf16[128,2,128]{2,1,0:T(2,128)(2,1)S(1)} all-to-all(bf16[128,2,128]{2,1,0:T(2,128)(2,1)S(1)} %reshape.395), channel_id=1, replica_groups=mesh['seq'=128,'head'=4] {'seq'}, dimensions={0} | all-to-all | bytes 131072 | tf_op jit(solution)/shard_map/all_to_all | solution.py:197
  (102 shorter events, 20.4 us)
Async XLA Ops:
  6.5 233.0 %copy-start = (bf16[1,1024,704]{1,2,0:T(8,128)(2,1)S(1)}, bf16[1,1024,704]{1,2,0:T(8,128)(2,1)}, u32[]{:S(2)}) copy-start(bf16[1,1024,704]{1,2,0:T(8,128)(2,1)} %param.30) | copy-start | bytes 4325380
  6.5 97.7 %all-gather.3.cloned.1.call-start = ((), (), s32[]{:S(2)}) async-start(), calls=%async_computation.6 | async-start | bytes 8454144 | tf_op jit(solution)/shard_map/all_gather | solution.py:125
  8.9 171.9 %all-reduce.2.cloned.1.call-start = ((), (), s32[]{:S(2)}) async-start(), calls=%async_computation.5 | async-start | bytes 1048576 | tf_op jit(solution)/shard_map/psum | solution.py:141
  10.8 103.3 %copy-start.4 = (bf16[128,256]{0,1:T(8,128)(2,1)}, bf16[128,256]{0,1:T(8,128)(2,1)S(1)}, u32[]{:S(2)}) copy-start(bf16[128,256]{0,1:T(8,128)(2,1)S(1)} %copy.111) | copy-start | bytes 196612
  18.0 96.1 %copy-start.14 = (pred[128]{0:T(512)(128)(4,1)}, pred[128]{0:T(512)(128)(4,1)S(1)}, u32[]{:S(2)}) copy-start(pred[128]{0:T(512)(128)(4,1)S(1)} %iota_compare_fusion.4) | copy-start | bytes 388
  122.1 1.7 copy-start.11
  122.1 2.7 copy-start.2
  123.8 1.6 copy-start.8
  129.4 2.0 copy-start.3
  129.4 2.0 copy-start.7
  129.4 2.1 copy-start.9
  129.4 2.3 copy-start.5
  131.4 0.8 copy-start.6
  131.4 1.7 copy-start.10
  131.4 50.6 %copy-start.13 = (f32[1024]{0:T(1024)S(1)}, f32[1024]{0:T(1024)}, u32[]{:S(2)}) copy-start(f32[1024]{0:T(1024)} %param.25) | copy-start | bytes 12292
  132.3 0.8 copy-start.1
  242.7 8.2 %copy-start.12 = (bf16[256,16]{0,1:T(8,128)(2,1)S(1)}, bf16[256,16]{0,1:T(8,128)(2,1)}, u32[]{:S(2)}) copy-start(bf16[256,16]{0,1:T(8,128)(2,1)} %param.26) | copy-start | bytes 24580
  244.1 26.0 %all-to-all-start.1 = ((bf16[128,1,2,4,256]{4,3,2,1,0:T(4,128)(2,1)}), bf16[128,1,2,4,256]{4,3,2,1,0:T(4,128)(2,1)S(1)}, u32[]{:S(2)}, u32[]{:S(2)}) async-start(bf16[128,1,2,4,256]{4,3,2,1,0:T(4,128)(2,1)} %copy.126), calls=%async_computation.1 | async-start | bytes 1048576 | tf_op jit(solution)/shard_map/all_to_all | solution.py:170
  270.9 15.5 %copy-start.15 = (pred[128]{0:T(512)(128)(4,1)S(1)}, pred[128]{0:T(512)(128)(4,1)}, u32[]{:S(2)}) copy-start(pred[128]{0:T(512)(128)(4,1)} %copy-done.14) | copy-start | bytes 388
  270.9 13.3 %all-to-all-start.2 = ((bf16[128,1,2,4,256]{4,0,2,1,3:T(8,128)(2,1)}), bf16[128,1,2,4,256]{4,0,2,1,3:T(8,128)(2,1)S(1)}, u32[]{:S(2)}, u32[]{:S(2)}) async-start(bf16[128,1,2,4,256]{4,0,2,1,3:T(8,128)(2,1)} %copy.127), calls=%async_computation.2 | async-start | bytes 1048576 | tf_op jit(solution)/shard_map/all_to_all | solution.py:169
  289.5 17.3 %all-to-all-start.3 = ((bf16[128,2,128]{2,1,0:T(2,128)(2,1)}), bf16[128,2,128]{2,1,0:T(2,128)(2,1)S(1)}, u32[]{:S(2)}, u32[]{:S(2)}) async-start(bf16[128,2,128]{2,1,0:T(2,128)(2,1)} %reshape.393), calls=%async_computation.3 | async-start | bytes 131072 | tf_op jit(solution)/shard_map/all_to_all | solution.py:190
Sparse Core Ops, SparseCore 0:
  10.5 93.6 all-gather.2
  133.2 47.5 all-reduce.1
where the time goes:
time: 334 us; the launch traced here: 333 us
  waiting for transfers between devices  161 us (48%)
  blocking collectives  61.7 us (18%)
  local copies, waits for them, and re-layouts  57.8 us (17%)
  starting transfers between devices  14.8 us (4%)
  between operations  14.6 us (4%)
  other arithmetic  12.1 us (4%)
  matrix products  10.9 us (3%)
    all_gather x1, waiting for transfers between devices, on_device(): all_pages = lax.all_gather(local_pages, 'seq', axis=0, tiled=True)  83.8 us
    psum x1, waiting for transfers between devices, on_device(): resid = lax.psum(partial_proj, 'head')  47.2 us
    all_to_all x1, blocking collectives, on_device(): lax.all_to_all(send_rows, 'seq', split_axis=0, concat_axis=0, tiled=True)  36.9 us
    unnamed x45, local copies, waits for them, and re-layouts  18.3 us
    all_to_all x1, blocking collectives, on_device(): lax.all_to_all(reordered, 'seq', split_axis=0, concat_axis=0, tiled=True)  16.7 us
    scatter x1, local copies, waits for them, and re-layouts, on_device(): send_rows.at[target_device, local_slot, slot_rank]  15.9 us
    all_to_all x1, waiting for transfers between devices, on_device(): lax.all_to_all(out_pieces, 'seq', split_axis=0, concat_axis=0, tiled=True)  11.5 us
    all_to_all x1, waiting for transfers between devices, on_device(): lax.all_to_all(lax.all_to_all(split_part.astype(jnp.bfloat16), 'seq', spl...  9.7 us
  transfers between devices with their start and end apart: 5, of which 5 were waited for; matrix products, arithmetic and copies ran while one was open for 5% of the time, Pallas kernels for 0%

commit v1 on v0

--- a/solution.py
+++ b/solution.py
@@ -123,6 +123,9 @@
         axis=1,
     )
     all_pages = lax.all_gather(local_pages, "seq", axis=0, tiled=True)
+    full_weight = lax.all_gather(out_weight, "head", axis=0, tiled=True)
+    full_hidden = lax.all_gather(hidden, "head", axis=1, tiled=True)
+    full_router = lax.all_gather(router_weight, "head", axis=0, tiled=True)
     chosen = lax.dynamic_slice_in_dim(inverse, group_index * group_pages, group_pages, 0)
     held_pages = jnp.take(all_pages, chosen, axis=0)
     prefix_keys = held_pages[:, :half_width].reshape(group_pages * page_rows, features)
@@ -131,29 +134,28 @@
     attended = attend_rows(
         queries, suffix_keys, suffix_values, prefix_keys, prefix_values, length, local_heads
     )
-    partial_proj = jnp.dot(attended, out_weight, preferred_element_type=jnp.float32)
-    own_columns = lax.dynamic_slice_in_dim(
-        partial_proj, head_index * column_width, column_width, 1
-    ) + hidden.astype(jnp.float32)
-    partial_proj = lax.dynamic_update_slice_in_dim(
-        partial_proj, own_columns, head_index * column_width, 1
-    )
-    resid = lax.psum(partial_proj, "head")
+    full_attended = lax.all_gather(attended, "head", axis=1, tiled=True)
+    resid = full_hidden.astype(jnp.float32) + jnp.dot(
+        full_attended, full_weight, preferred_element_type=jnp.float32
+    )
     normed = (
         resid * lax.rsqrt(jnp.mean(resid * resid, axis=1, keepdims=True) + norm_eps) * norm_gain
     ).astype(jnp.bfloat16)
-    normed_columns = lax.dynamic_slice_in_dim(normed, head_index * column_width, column_width, 1)
-    logits = lax.psum(
-        jnp.dot(normed_columns, router_weight, preferred_element_type=jnp.float32), "head"
-    )
+    logits = jnp.dot(normed, full_router, preferred_element_type=jnp.float32)
     chosen_logits = jnp.take_along_axis(logits, routes, axis=1)
     gate_first = jax.nn.sigmoid(chosen_logits[:, 0] - chosen_logits[:, 1])
     gate_second = jax.nn.sigmoid(chosen_logits[:, 1] - chosen_logits[:, 0])
     target_device, local_slot, slot_rank = slot_table(routes, replicas, per_device, EXPERTS)
-    token_index = jnp.arange(row_count * TOPK, dtype=jnp.int32) // TOPK
-    send_rows = jnp.zeros((seq_count, per_device, capacity, normed.shape[1]), jnp.bfloat16)
-    send_rows = send_rows.at[target_device, local_slot, slot_rank].set(
-        jnp.take(normed, token_index, axis=0)
+    slot_flat = (target_device * per_device + local_slot) * capacity + slot_rank
+    slot_total = seq_count * per_device * capacity
+    pair_count = row_count * TOPK
+    slot_pair = (
+        jnp.zeros((slot_total,), jnp.int32)
+        .at[slot_flat]
+        .set(jnp.arange(pair_count, dtype=jnp.int32), mode="drop")
+    )
+    send_rows = jnp.take(normed, slot_pair // TOPK, axis=0).reshape(
+        seq_count, per_device, capacity, normed.shape[1]
     )
     slots = lax.all_to_all(send_rows, "seq", split_axis=0, concat_axis=0, tiled=True)
     gate_act = jnp.einsum("spnd,pdf->spnf", slots, gate_weight, preferred_element_type=jnp.float32)
@@ -165,17 +167,10 @@
     part_dims = partial_out.shape
     split_part = partial_out.reshape(
         part_dims[0], part_dims[1], part_dims[2], head_count, part_dims[3] // head_count
-    )
-    arrived = lax.all_to_all(
-        lax.all_to_all(
-            split_part.astype(jnp.bfloat16), "seq", split_axis=0, concat_axis=0, tiled=True
-        ),
-        "head",
-        split_axis=3,
-        concat_axis=3,
-        tiled=True,
-    ).astype(split_part.dtype)
-    returned = jnp.sum(arrived, axis=3).astype(jnp.bfloat16)
+    ).astype(jnp.bfloat16)
+    by_head = lax.all_to_all(split_part, "head", split_axis=3, concat_axis=3, tiled=True)
+    summed = jnp.sum(by_head.astype(jnp.float32), axis=3).astype(jnp.bfloat16)
+    returned = lax.all_to_all(summed, "seq", split_axis=0, concat_axis=0, tiled=True)
     picked = (
         returned[target_device, local_slot, slot_rank]
         .astype(jnp.float32)

time: 334 us -> 269 us (0.81)
  waiting for transfers between devices: 161 us -> 115 us
  local copies, waits for them, and re-layouts: 57.8 us -> 39.1 us
  starting transfers between devices: 14.8 us -> 29.5 us
  blocking collectives: 61.7 us -> 49.9 us
  other arithmetic: 12.1 us -> 8.53 us
    psum x1 -> x0, waiting for transfers between devices: 47.2 us -> none  [on_device(): resid = lax.psum(partial_proj, 'head')]
    all_to_all x1 -> x0, blocking collectives: 36.9 us -> none  [on_device(): lax.all_to_all(send_rows, 'seq', split_axis=0, concat_axis=0, tiled=True)]
    all_gather x0 -> x3, blocking collectives: none -> 33.2 us  [the longest x1 12.7 us: on_device(): full_attended = lax.all_gather(attended, 'head', axis=1, tiled=True)]
    all_to_all x2 -> x3, starting transfers between devices: 9 us -> 23.7 us  [the longest x1 14.5 us: on_device(): lax.all_to_all(send_rows, 'seq', split_axis=0, concat_axis=0, tiled=True)]
    scatter x1, local copies, waits for them, and re-layouts: 15.9 us -> 1.58 us  [on_device(): slot_pair = jnp.zeros((slot_total,), jnp.int32).at[slot_flat].set(jnp.ara...]
    all_gather x1, waiting for transfers between devices: 83.8 us -> 70.7 us  [on_device(): all_pages = lax.all_gather(local_pages, 'seq', axis=0, tiled=True)]
    all_to_all x2 -> x3, waiting for transfers between devices: 18.2 us -> 29.7 us  [the longest x1 12.8 us: on_device(): lax.all_to_all(summed, 'seq', split_axis=0, concat_axis=0, tiled=True)]
    psum x1 -> x0, blocking collectives: 8.12 us -> none  [on_device(): lax.psum(jnp.dot(normed_columns, router_weight, preferred_element_type=jn...]
  transfers between devices with their start and end apart: 5 -> 6, of which waited for: 5 -> 6; matrix products, arithmetic and copies ran while one was open for 5% -> 14% of each run, Pallas kernels for 0% -> 0%
where the time goes in v1:
time: 269 us; the launch traced here: 268 us
  waiting for transfers between devices  115 us (43%)
  blocking collectives  49.9 us (19%)
  local copies, waits for them, and re-layouts  39.1 us (15%)
  starting transfers between devices  29.5 us (11%)
  between operations  14.6 us (5%)
  matrix products  11 us (4%)
  other arithmetic  8.53 us (3%)
    all_gather x1, waiting for transfers between devices, on_device(): all_pages = lax.all_gather(local_pages, 'seq', axis=0, tiled=True)  70.7 us
    unnamed x31, local copies, waits for them, and re-layouts  17.3 us
    all_to_all x1, blocking collectives, on_device(): lax.all_to_all(reordered, 'seq', split_axis=0, concat_axis=0, tiled=True)  16.7 us
    all_to_all x1, starting transfers between devices, on_device(): lax.all_to_all(send_rows, 'seq', split_axis=0, concat_axis=0, tiled=True)  14.5 us
    all_to_all x1, waiting for transfers between devices, on_device(): lax.all_to_all(summed, 'seq', split_axis=0, concat_axis=0, tiled=True)  12.8 us
    all_gather x1, blocking collectives, on_device(): full_attended = lax.all_gather(attended, 'head', axis=1, tiled=True)  12.7 us
    all_to_all x1, waiting for transfers between devices, on_device(): lax.all_to_all(out_pieces, 'seq', split_axis=0, concat_axis=0, tiled=True)  11.5 us
    all_gather x1, blocking collectives, on_device(): full_hidden = lax.all_gather(hidden, 'head', axis=1, tiled=True)  10.7 us
  transfers between devices with their start and end apart: 6, of which 6 were waited for; matrix products, arithmetic and copies ran while one was open for 14% of the time, Pallas kernels for 0%

profile of v1, /device:TPU:1, one launch (start us, length us, event | category | flops | bytes accessed | tf_op | source)
XLA Modules:
  0.0 267.6 jit_solution(6575203713692141235)
XLA Ops:
  13.5 1.0 scatter_custom_fusion.1
  14.6 1.0 copy.111
  15.6 1.0 copy.113
  17.3 1.6 copy.116
  18.9 10.7 %all_gather.15 = bf16[128,1024]{1,0:T(8,128)(2,1)S(1)} all-gather(bf16[128,256]{1,0:T(8,128)(2,1)} %param.16), channel_id=1, replica_groups=mesh['seq'=128,'head'=4] {'head'}, dimensions={1}, use_global_device_ids=true | all-gather | bytes 327680 | tf_op jit(solution)/shard_map/all_gather | solution.py:127
  30.9 1.6 scatter_custom_fusion.2
  33.6 70.7 %all-gather.6.cloned.1.call-done = bf16[128,1,16384]{2,1,0:T(2,128)(2,1)} async-done(((bf16[1,1,16384]{2,1,0:T(2,128)(2,1)}), bf16[128,1,16384]{2,1,0:T(2,128)(2,1)}) %all-gather.6.cloned.1.call-update) | async-done | bytes 4194320 | tf_op jit(solution)/shard_map/all_gather | solution.py:125
  104.2 9.9 %copy.186 = bf16[128,1,16384]{2,0,1:T(8,128)(2,1)} copy(bf16[128,1,16384]{2,1,0:T(2,128)(2,1)} %all-gather.6.cloned.1.call-done) | data formatting | bytes 8388608
  114.1 4.8 %gather_fusion = bf16[32,16384]{1,0:T(8,128)(2,1)S(1)} fusion(bf16[128,16384]{1,0:T(8,128)(2,1)} %bitcast.159, s32[1024]{0:T(1024)S(1)} %pad_clamp_fusion.2), kind=kCustom, calls=%fused_computation | custom fusion | bytes 2097280 | tf_op jit(solution)/shard_map/jit(_take)/gather | solution.py:130
  119.2 2.1 reshape_reshape.6
  121.3 1.1 reshape_reshape.7
  122.5 1.4 bitcast_reduce_fusion
  125.3 12.7 %all_gather.17 = bf16[128,1024]{0,1:T(8,128)(2,1)S(1)} all-gather(bf16[128,256]{0,1:T(8,128)(2,1)S(1)} %bitcast.169), channel_id=1, replica_groups=mesh['seq'=128,'head'=4] {'head'}, dimensions={1}, use_global_device_ids=true | all-gather | bytes 327680 | tf_op jit(solution)/shard_map/all_gather | solution.py:137
  138.1 2.4 all-gather.4.cloned.1.call-done
  140.4 2.1 multiply_reduce_fusion
  142.7 1.2 gather_fusion.1
  144.1 1.4 fusion.44
  145.5 14.5 %all-to-all-start = ((bf16[128,1,2,1024]{3,2,1,0:T(2,128)(2,1)}), bf16[128,1,2,1024]{3,2,1,0:T(2,128)(2,1)S(1)}, u32[]{:S(2)}, u32[]{:S(2)}) async-start(bf16[128,1,2,1024]{3,2,1,0:T(2,128)(2,1)} %fusion.44), calls=%async_computation | async-start | bytes 1048576 | tf_op jit(solution)/shard_map/all_to_all | solution.py:160
  160.3 1.0 scatter_custom_fusion
  161.3 9.8 %all_gather.19 = bf16[1024,16]{0,1:T(8,128)(2,1)S(1)} all-gather(bf16[256,16]{0,1:T(8,128)(2,1)S(1)} %copy-done.6), channel_id=1, replica_groups=mesh['seq'=128,'head'=4] {'head'}, dimensions={0}, use_global_device_ids=true | all-gather | bytes 40960 | tf_op jit(solution)/shard_map/all_gather | solution.py:128
  171.1 9.5 %all-to-all-done = bf16[128,1,2,1024]{3,2,1,0:T(2,128)(2,1)S(1)} async-done(((bf16[128,1,2,1024]{3,2,1,0:T(2,128)(2,1)}), bf16[128,1,2,1024]{3,2,1,0:T(2,128)(2,1)S(1)}, u32[]{:S(2)}, u32[]{:S(2)}) %all-to-all-start) | async-done | bytes 524320 | tf_op jit(solution)/shard_map/all_to_all | solution.py:160
  180.5 2.9 %fusion.41 = f32[128,1,2,704]{0,3,2,1:T(8,128)} fusion(bf16[1,1024,704]{1,2,0:T(8,128)(2,1)} %param.28, bf16[128,1,2,1024]{3,2,1,0:T(2,128)(2,1)S(1)} %all-to-all-done), kind=kOutput, calls=%fused_computation.47 | convolution fusion | flops 370540544 | bytes 2686976 | tf_op jit(solution)/shard_map/spnd,pdf->spnf/dot_general | solution.py:161
  183.4 3.3 %fusion.8 = bf16[128,2,1024]{2,0,1:T(8,128)(2,1)S(1)} fusion(bf16[1,1024,704]{1,2,0:T(8,128)(2,1)S(1)} %copy-done, f32[128,1,2,704]{0,3,2,1:T(8,128)} %fusion.41, bf16[1,1024,704]{1,2,0:T(8,128)(2,1)} %param.29, bf16[128,1,2,1024]{3,2,1,0:T(2,128)(2,1)S(1)} %all-to-all-done), kind=kOutput, calls=%fused_computation.20 | convolution fusion | flops 738820096 | bytes 4653056 | tf_op jit(solution)/shard_map/spnf,pdf->spnd/dot_general | solution.py:164
  187.6 3.5 %all-to-all-start.1 = ((bf16[128,1,2,4,256]{4,0,2,1,3:T(8,128)(2,1)}), bf16[128,1,2,4,256]{4,0,2,1,3:T(8,128)(2,1)S(1)}, u32[]{:S(2)}, u32[]{:S(2)}) async-start(bf16[128,1,2,4,256]{4,0,2,1,3:T(8,128)(2,1)} %bitcast.163), calls=%async_computation.1 | async-start | bytes 1048576 | tf_op jit(solution)/shard_map/all_to_all | solution.py:171
  191.2 2.0 gather_fusion.4
  193.4 7.4 %all-to-all-done.1 = bf16[128,1,2,4,256]{4,0,2,1,3:T(8,128)(2,1)S(1)} async-done(((bf16[128,1,2,4,256]{4,0,2,1,3:T(8,128)(2,1)}), bf16[128,1,2,4,256]{4,0,2,1,3:T(8,128)(2,1)S(1)}, u32[]{:S(2)}, u32[]{:S(2)}) %all-to-all-start.1) | async-done | bytes 524320 | tf_op jit(solution)/shard_map/all_to_all | solution.py:171
  201.7 5.8 %all-to-all-start.2 = ((bf16[128,1,2,256]{3,2,1,0:T(2,128)(2,1)}), bf16[128,1,2,256]{3,2,1,0:T(2,128)(2,1)S(1)}, u32[]{:S(2)}, u32[]{:S(2)}) async-start(bf16[128,1,2,256]{3,2,1,0:T(2,128)(2,1)} %bitcast.155), calls=%async_computation.2 | async-start | bytes 262144 | tf_op jit(solution)/shard_map/all_to_all | solution.py:173
  207.5 12.8 %all-to-all-done.2 = bf16[128,1,2,256]{3,2,1,0:T(2,128)(2,1)S(1)} async-done(((bf16[128,1,2,256]{3,2,1,0:T(2,128)(2,1)}), bf16[128,1,2,256]{3,2,1,0:T(2,128)(2,1)S(1)}, u32[]{:S(2)}, u32[]{:S(2)}) %all-to-all-start.2) | async-done | bytes 131104 | tf_op jit(solution)/shard_map/all_to_all | solution.py:173
  220.3 1.6 gather_fusion.2
  224.3 5.8 %all-to-all-start.3 = ((bf16[128,2,128]{2,1,0:T(2,128)(2,1)}), bf16[128,2,128]{2,1,0:T(2,128)(2,1)S(1)}, u32[]{:S(2)}, u32[]{:S(2)}) async-start(bf16[128,2,128]{2,1,0:T(2,128)(2,1)} %reshape.406), calls=%async_computation.3 | async-start | bytes 131072 | tf_op jit(solution)/shard_map/all_to_all | solution.py:185
  230.2 11.5 %all-to-all-done.3 = bf16[128,2,128]{2,1,0:T(2,128)(2,1)S(1)} async-done(((bf16[128,2,128]{2,1,0:T(2,128)(2,1)}), bf16[128,2,128]{2,1,0:T(2,128)(2,1)S(1)}, u32[]{:S(2)}, u32[]{:S(2)}) %all-to-all-start.3) | async-done | bytes 65568 | tf_op jit(solution)/shard_map/all_to_all | solution.py:185
  243.4 16.7 %all_to_all.25 = bf16[128,2,128]{2,1,0:T(2,128)(2,1)S(1)} all-to-all(bf16[128,2,128]{2,1,0:T(2,128)(2,1)S(1)} %reshape.408), channel_id=1, replica_groups=mesh['seq'=128,'head'=4] {'seq'}, dimensions={0} | all-to-all | bytes 131072 | tf_op jit(solution)/shard_map/all_to_all | solution.py:192
  (91 shorter events, 18.6 us)
Async XLA Ops:
  6.5 176.9 %copy-start = (bf16[1,1024,704]{1,2,0:T(8,128)(2,1)S(1)}, bf16[1,1024,704]{1,2,0:T(8,128)(2,1)}, u32[]{:S(2)}) copy-start(bf16[1,1024,704]{1,2,0:T(8,128)(2,1)} %param.30) | copy-start | bytes 4325380
  6.5 97.7 %all-gather.6.cloned.1.call-start = ((), (), s32[]{:S(2)}) async-start(), calls=%async_computation.6 | async-start | bytes 8454144 | tf_op jit(solution)/shard_map/all_gather | solution.py:125
  8.9 131.5 %all-gather.4.cloned.1.call-start = ((), (), s32[]{:S(2)}) async-start(), calls=%async_computation.5 | async-start | bytes 2621440 | tf_op jit(solution)/shard_map/all_gather | solution.py:126
  15.6 98.6 %copy-start.2 = (bf16[128,256]{0,1:T(8,128)(2,1)}, bf16[128,256]{0,1:T(8,128)(2,1)S(1)}, u32[]{:S(2)}) copy-start(bf16[128,256]{0,1:T(8,128)(2,1)S(1)} %copy.111) | copy-start | bytes 196612
  122.5 1.8 copy-start.1
  124.3 0.8 copy-start.4
  125.2 17.4 %copy-start.7 = (f32[1024]{0:T(1024)S(1)}, f32[1024]{0:T(1024)}, u32[]{:S(2)}) copy-start(f32[1024]{0:T(1024)} %param.25) | copy-start | bytes 12292
  142.7 1.4 copy-start.3
  143.9 16.1 %copy-start.5 = (s32[128,2]{0,1:T(2,128)S(1)}, s32[128,2]{0,1:T(2,128)}, u32[]{:S(2)}) copy-start(s32[128,2]{0,1:T(2,128)} %param.27) | copy-start | bytes 3076
  143.9 16.4 %copy-start.8 = (s32[128]{0:T(128)S(1)}, s32[128]{0:T(128)}, u32[]{:S(2)}) copy-start(s32[128]{0:T(128)} %param.31) | copy-start | bytes 1540
  143.9 17.4 %copy-start.6 = (bf16[256,16]{0,1:T(8,128)(2,1)S(1)}, bf16[256,16]{0,1:T(8,128)(2,1)}, u32[]{:S(2)}) copy-start(bf16[256,16]{0,1:T(8,128)(2,1)} %param.26) | copy-start | bytes 24580
  145.5 35.0 %all-to-all-start = ((bf16[128,1,2,1024]{3,2,1,0:T(2,128)(2,1)}), bf16[128,1,2,1024]{3,2,1,0:T(2,128)(2,1)S(1)}, u32[]{:S(2)}, u32[]{:S(2)}) async-start(bf16[128,1,2,1024]{3,2,1,0:T(2,128)(2,1)} %fusion.44), calls=%async_computation | async-start | bytes 1048576 | tf_op jit(solution)/shard_map/all_to_all | solution.py:160
  187.6 13.3 %all-to-all-start.1 = ((bf16[128,1,2,4,256]{4,0,2,1,3:T(8,128)(2,1)}), bf16[128,1,2,4,256]{4,0,2,1,3:T(8,128)(2,1)S(1)}, u32[]{:S(2)}, u32[]{:S(2)}) async-start(bf16[128,1,2,4,256]{4,0,2,1,3:T(8,128)(2,1)} %bitcast.163), calls=%async_computation.1 | async-start | bytes 1048576 | tf_op jit(solution)/shard_map/all_to_all | solution.py:171
  201.7 18.6 %all-to-all-start.2 = ((bf16[128,1,2,256]{3,2,1,0:T(2,128)(2,1)}), bf16[128,1,2,256]{3,2,1,0:T(2,128)(2,1)S(1)}, u32[]{:S(2)}, u32[]{:S(2)}) async-start(bf16[128,1,2,256]{3,2,1,0:T(2,128)(2,1)} %bitcast.155), calls=%async_computation.2 | async-start | bytes 262144 | tf_op jit(solution)/shard_map/all_to_all | solution.py:173
  224.3 17.3 %all-to-all-start.3 = ((bf16[128,2,128]{2,1,0:T(2,128)(2,1)}), bf16[128,2,128]{2,1,0:T(2,128)(2,1)S(1)}, u32[]{:S(2)}, u32[]{:S(2)}) async-start(bf16[128,2,128]{2,1,0:T(2,128)(2,1)} %reshape.406), calls=%async_computation.3 | async-start | bytes 131072 | tf_op jit(solution)/shard_map/all_to_all | solution.py:185
Sparse Core Ops, SparseCore 0:
  10.5 93.7 all-gather.5
  106.3 34.0 all-gather.3

commit v2 on v1

--- a/solution.py
+++ b/solution.py
@@ -116,25 +116,49 @@
     per_device = max(1, EXPERTS // seq_count)
     capacity = 5 * row_count * TOPK // (4 * EXPERTS * replicas)
     inverse = page_inverse(page_group, group_pages, GROUPS)
-    group_index = seq_index // block_devices
-    half_width = page_rows * features
-    local_pages = jnp.concatenate(
-        [key_cache.reshape(page_local, half_width), value_cache.reshape(page_local, half_width)],
-        axis=1,
-    )
-    all_pages = lax.all_gather(local_pages, "seq", axis=0, tiled=True)
-    full_weight = lax.all_gather(out_weight, "head", axis=0, tiled=True)
-    full_hidden = lax.all_gather(hidden, "head", axis=1, tiled=True)
-    full_router = lax.all_gather(router_weight, "head", axis=0, tiled=True)
+    inverse_destination = (
+        jnp.zeros((seq_count,), jnp.int32)
+        .at[destinations]
+        .set(jnp.arange(seq_count, dtype=jnp.int32))
+    )
+    own_request = inverse_destination[seq_index]
+    group_index = own_request // block_devices
+    local_pages = jnp.concatenate([key_cache, value_cache], axis=2).reshape(
+        page_local * page_rows, 2 * features
+    )
+    all_pages = lax.all_gather(local_pages, "seq", axis=0, tiled=False).reshape(
+        seq_count * page_local, page_rows, 2 * features
+    )
+    extra = jnp.zeros((row_count, 128), jnp.bfloat16)
+    extra = extra.at[:, 0:TOPK].set(routes.astype(jnp.bfloat16))
+    extra = extra.at[:, TOPK].set(lengths[0].astype(jnp.bfloat16))
+    packed = jnp.concatenate([queries, suffix_keys, suffix_values, hidden, extra], axis=1)
+    pieces = packed.reshape(seq_count, row_count // seq_count, packed.shape[1])
+    spread = lax.all_to_all(pieces, "seq", split_axis=0, concat_axis=0, tiled=True)
+    spread = jnp.take(spread, inverse_destination, axis=0)
+    moved = lax.all_to_all(spread, "seq", split_axis=0, concat_axis=0, tiled=True).reshape(
+        row_count, packed.shape[1]
+    )
+    queries = moved[:, 0:features]
+    suffix_keys = moved[:, features : 2 * features]
+    suffix_values = moved[:, 2 * features : 3 * features]
+    hidden = moved[:, 3 * features : 3 * features + column_width]
+    tail = 3 * features + column_width
+    routes = moved[:, tail : tail + TOPK].astype(jnp.int32)
+    length = moved[0, tail + TOPK].astype(jnp.int32)
     chosen = lax.dynamic_slice_in_dim(inverse, group_index * group_pages, group_pages, 0)
     held_pages = jnp.take(all_pages, chosen, axis=0)
-    prefix_keys = held_pages[:, :half_width].reshape(group_pages * page_rows, features)
-    prefix_values = held_pages[:, half_width:].reshape(group_pages * page_rows, features)
-    length = lengths[0]
+    prefix_keys = held_pages[:, :, :features].reshape(group_pages * page_rows, features)
+    prefix_values = held_pages[:, :, features:].reshape(group_pages * page_rows, features)
     attended = attend_rows(
         queries, suffix_keys, suffix_values, prefix_keys, prefix_values, length, local_heads
     )
-    full_attended = lax.all_gather(attended, "head", axis=1, tiled=True)
+    stacked = jnp.concatenate([attended, hidden, router_weight.T], axis=0)
+    gathered = lax.all_gather(stacked, "head", axis=1, tiled=True)
+    full_attended = gathered[:row_count]
+    full_hidden = gathered[row_count : 2 * row_count]
+    full_router = gathered[2 * row_count :].T
+    full_weight = lax.all_gather(out_weight, "head", axis=0, tiled=True)
     resid = full_hidden.astype(jnp.float32) + jnp.dot(
         full_attended, full_weight, preferred_element_type=jnp.float32
     )
@@ -180,17 +204,7 @@
     layer = resid_columns + gate_first[:, None] * picked[:, 0] + gate_second[:, None] * picked[:, 1]
     layer = layer.astype(jnp.bfloat16)
     live_rows = jnp.arange(row_count, dtype=jnp.int32) < length
-    layer = jnp.where(live_rows[:, None], layer, jnp.zeros_like(layer))
-    out_pieces = layer.reshape(seq_count, row_count // seq_count, column_width)
-    scattered = lax.all_to_all(out_pieces, "seq", split_axis=0, concat_axis=0, tiled=True)
-    inverse_destination = (
-        jnp.zeros((seq_count,), jnp.int32)
-        .at[destinations]
-        .set(jnp.arange(seq_count, dtype=jnp.int32))
-    )
-    reordered = jnp.take(scattered, inverse_destination, axis=0)
-    settled = lax.all_to_all(reordered, "seq", split_axis=0, concat_axis=0, tiled=True)
-    return settled.reshape(row_count, column_width)
+    return jnp.where(live_rows[:, None], layer, jnp.zeros_like(layer))
 
 
 def solution(mesh):

time: 269 us -> 229 us (0.85)
  blocking collectives: 49.9 us -> 12.7 us
  starting transfers between devices: 29.5 us -> 45.5 us
  waiting for transfers between devices: 115 us -> 99.6 us
  local copies, waits for them, and re-layouts: 39.1 us -> 28.5 us
  between operations: 14.6 us -> 18.5 us
    all_gather x1, waiting for transfers between devices: 70.7 us -> 17 us  [on_device(): lax.all_gather(local_pages, 'seq', axis=0, tiled=False)]
    all_gather x3 -> x1, blocking collectives: 33.2 us -> 12.7 us  [on_device(): gathered = lax.all_gather(stacked, 'head', axis=1, tiled=True)]
    all_to_all x1 -> x2, starting transfers between devices: 5.8 us -> 24 us  [the longest x1 18.4 us: on_device(): lax.all_to_all(pieces, 'seq', split_axis=0, concat_axis=0, tiled=True)]
    all_to_all x1 -> x0, blocking collectives: 16.7 us -> none  [on_device(): lax.all_to_all(reordered, 'seq', split_axis=0, concat_axis=0, tiled=True)]
    all_to_all x1 -> x2, waiting for transfers between devices: 11.5 us -> 26.6 us  [the longest x1 14.8 us: on_device(): lax.all_to_all(pieces, 'seq', split_axis=0, concat_axis=0, tiled=True)]
    all_gather x1, waiting for transfers between devices: 2.35 us -> 15.6 us  [on_device(): full_weight = lax.all_gather(out_weight, 'head', axis=0, tiled=True)]
    all_to_all x1, waiting for transfers between devices: 9.45 us -> 20.6 us  [on_device(): lax.all_to_all(send_rows, 'seq', split_axis=0, concat_axis=0, tiled=True)]
    unnamed x31 -> x39, local copies, waits for them, and re-layouts: 17.3 us -> 6.72 us
  transfers between devices with their start and end apart: 6 -> 7, of which waited for: 6 -> 7; matrix products, arithmetic and copies ran while one was open for 14% -> 15% of each run, Pallas kernels for 0% -> 0%
where the time goes in v2:
time: 229 us; the launch traced here: 228 us
  waiting for transfers between devices  99.6 us (43%)
  starting transfers between devices  45.5 us (20%)
  local copies, waits for them, and re-layouts  28.5 us (12%)
  between operations  18.5 us (8%)
  matrix products  12.9 us (6%)
  blocking collectives  12.7 us (6%)
  other arithmetic  10.2 us (4%)
    all_to_all x1, waiting for transfers between devices, on_device(): lax.all_to_all(send_rows, 'seq', split_axis=0, concat_axis=0, tiled=True)  20.6 us
    all_to_all x1, starting transfers between devices, on_device(): lax.all_to_all(pieces, 'seq', split_axis=0, concat_axis=0, tiled=True)  18.4 us
    all_gather x1, waiting for transfers between devices, on_device(): lax.all_gather(local_pages, 'seq', axis=0, tiled=False)  17 us
    all_gather x1, waiting for transfers between devices, on_device(): full_weight = lax.all_gather(out_weight, 'head', axis=0, tiled=True)  15.6 us
    all_to_all x1, waiting for transfers between devices, on_device(): lax.all_to_all(pieces, 'seq', split_axis=0, concat_axis=0, tiled=True)  14.8 us
    all_to_all x1, waiting for transfers between devices, on_device(): lax.all_to_all(summed, 'seq', split_axis=0, concat_axis=0, tiled=True)  12.8 us
    all_gather x1, blocking collectives, on_device(): gathered = lax.all_gather(stacked, 'head', axis=1, tiled=True)  12.7 us
    all_to_all x1, starting transfers between devices, on_device(): lax.all_to_all(send_rows, 'seq', split_axis=0, concat_axis=0, tiled=True)  12.2 us
  transfers between devices with their start and end apart: 7, of which 7 were waited for; matrix products, arithmetic and copies ran while one was open for 15% of the time, Pallas kernels for 0%

profile of v2, /device:TPU:1, one launch (start us, length us, event | category | flops | bytes accessed | tf_op | source)
XLA Modules:
  0.0 227.8 jit_solution(12553757369360897242)
XLA Ops:
  6.5 1.5 pad_maximum_fusion.1
  17.0 1.1 reshape.446
  18.1 18.4 %all-to-all-start = ((bf16[128,2,576]{2,1,0:T(2,128)(2,1)}), bf16[128,2,576]{2,1,0:T(2,128)(2,1)S(1)}, u32[]{:S(2)}, u32[]{:S(2)}) async-start(bf16[128,2,576]{2,1,0:T(2,128)(2,1)} %reshape.446), calls=%async_computation | async-start | bytes 655360 | tf_op jit(solution)/shard_map/all_to_all | solution.py:137
  37.3 1.0 scatter_custom_fusion
  38.3 14.8 %all-to-all-done = bf16[128,2,576]{2,1,0:T(2,128)(2,1)S(1)} async-done(((bf16[128,2,576]{2,1,0:T(2,128)(2,1)}), bf16[128,2,576]{2,1,0:T(2,128)(2,1)S(1)}, u32[]{:S(2)}, u32[]{:S(2)}) %all-to-all-start) | async-done | bytes 294944 | tf_op jit(solution)/shard_map/all_to_all | solution.py:137
  55.4 1.1 reshape.448
  56.5 5.6 %all-to-all-start.1 = ((bf16[128,2,576]{2,1,0:T(2,128)(2,1)}), bf16[128,2,576]{2,1,0:T(2,128)(2,1)S(1)}, u32[]{:S(2)}, u32[]{:S(2)}) async-start(bf16[128,2,576]{2,1,0:T(2,128)(2,1)} %reshape.448), calls=%async_computation.1 | async-start | bytes 655360 | tf_op jit(solution)/shard_map/all_to_all | solution.py:139
  65.7 1.0 scatter_custom_fusion.1
  66.8 11.8 %all-to-all-done.1 = bf16[128,2,576]{2,1,0:T(2,128)(2,1)S(1)} async-done(((bf16[128,2,576]{2,1,0:T(2,128)(2,1)}), bf16[128,2,576]{2,1,0:T(2,128)(2,1)S(1)}, u32[]{:S(2)}, u32[]{:S(2)}) %all-to-all-start.1) | async-done | bytes 294944 | tf_op jit(solution)/shard_map/all_to_all | solution.py:139
  83.5 1.6 scatter_custom_fusion.2
  86.0 0.9 fusion.83
  87.0 17.0 %all-gather.3.cloned.1.call-done = bf16[128,32,512]{2,1,0:T(8,128)(2,1)} async-done(((bf16[1,32,512]{2,1,0:T(8,128)(2,1)}), bf16[128,32,512]{2,1,0:T(8,128)(2,1)}) %all-gather.3.cloned.1.call-update) | async-done | bytes 4194320 | tf_op jit(solution)/shard_map/all_gather | solution.py:129
  103.9 2.8 %gather_fusion.1 = bf16[32,32,512]{2,1,0:T(8,128)(2,1)S(1)} fusion(bf16[128,32,512]{2,1,0:T(8,128)(2,1)} %all-gather.3.cloned.1.call-done, s32[1024]{0:T(1024)S(1)} %pad_clamp_fusion.1), kind=kCustom, calls=%fused_computation.1 | custom fusion | bytes 2097280 | tf_op jit(solution)/shard_map/jit(_take)/gather | solution.py:150
  107.5 1.4 reshape_reshape.6
  108.9 1.5 multiply_reduce_fusion
  111.0 1.0 fusion.28
  112.4 12.7 %all_gather.10 = bf16[272,1024]{1,0:T(8,128)(2,1)S(1)} all-gather(bf16[272,256]{1,0:T(8,128)(2,1)S(1)} %pad_maximum_fusion), channel_id=1, replica_groups=mesh['seq'=128,'head'=4] {'head'}, dimensions={1}, use_global_device_ids=true | all-gather | bytes 696320 | tf_op jit(solution)/shard_map/all_gather | solution.py:157
  125.1 15.6 %all-gather.5.cloned.1.call-done = bf16[1024,1024]{1,0:T(8,128)(2,1)} async-done(((bf16[256,1024]{1,0:T(8,128)(2,1)}), bf16[1024,1024]{1,0:T(8,128)(2,1)}) %all-gather.5.cloned.1.call-update) | async-done | bytes 2097168 | tf_op jit(solution)/shard_map/all_gather | solution.py:161
  140.7 2.1 multiply_reduce_fusion.1
  143.0 1.2 gather_fusion.2
  144.3 1.4 fusion.43
  145.7 12.2 %all-to-all-start.2 = ((bf16[128,1,2,1024]{3,2,1,0:T(2,128)(2,1)}), bf16[128,1,2,1024]{3,2,1,0:T(2,128)(2,1)S(1)}, u32[]{:S(2)}, u32[]{:S(2)}) async-start(bf16[128,1,2,1024]{3,2,1,0:T(2,128)(2,1)} %fusion.43), calls=%async_computation.2 | async-start | bytes 1048576 | tf_op jit(solution)/shard_map/all_to_all | solution.py:184
  157.9 20.6 %all-to-all-done.2 = bf16[128,1,2,1024]{3,2,1,0:T(2,128)(2,1)S(1)} async-done(((bf16[128,1,2,1024]{3,2,1,0:T(2,128)(2,1)}), bf16[128,1,2,1024]{3,2,1,0:T(2,128)(2,1)S(1)}, u32[]{:S(2)}, u32[]{:S(2)}) %all-to-all-start.2) | async-done | bytes 524320 | tf_op jit(solution)/shard_map/all_to_all | solution.py:184
  178.5 2.9 %fusion.40 = f32[128,1,2,704]{0,3,2,1:T(8,128)} fusion(bf16[1,1024,704]{1,2,0:T(8,128)(2,1)} %param.32, bf16[128,1,2,1024]{3,2,1,0:T(2,128)(2,1)S(1)} %all-to-all-done.2), kind=kOutput, calls=%fused_computation.44 | convolution fusion | flops 370540544 | bytes 2686976 | tf_op jit(solution)/shard_map/spnd,pdf->spnf/dot_general | solution.py:185
  181.4 3.3 %fusion.7 = bf16[128,2,1024]{2,0,1:T(8,128)(2,1)S(1)} fusion(bf16[1,1024,704]{1,2,0:T(8,128)(2,1)S(1)} %copy-done, f32[128,1,2,704]{0,3,2,1:T(8,128)} %fusion.40, bf16[1,1024,704]{1,2,0:T(8,128)(2,1)} %param.33, bf16[128,1,2,1024]{3,2,1,0:T(2,128)(2,1)S(1)} %all-to-all-done.2), kind=kOutput, calls=%fused_computation.18 | convolution fusion | flops 738820096 | bytes 4653056 | tf_op jit(solution)/shard_map/spnf,pdf->spnd/dot_general | solution.py:188
  185.5 3.5 %all-to-all-start.3 = ((bf16[128,1,2,4,256]{4,0,2,1,3:T(8,128)(2,1)}), bf16[128,1,2,4,256]{4,0,2,1,3:T(8,128)(2,1)S(1)}, u32[]{:S(2)}, u32[]{:S(2)}) async-start(bf16[128,1,2,4,256]{4,0,2,1,3:T(8,128)(2,1)} %bitcast.134), calls=%async_computation.3 | async-start | bytes 1048576 | tf_op jit(solution)/shard_map/all_to_all | solution.py:195
  189.3 0.9 fusion.64
  190.2 2.0 gather_fusion.4
  192.4 6.4 %all-to-all-done.3 = bf16[128,1,2,4,256]{4,0,2,1,3:T(8,128)(2,1)S(1)} async-done(((bf16[128,1,2,4,256]{4,0,2,1,3:T(8,128)(2,1)}), bf16[128,1,2,4,256]{4,0,2,1,3:T(8,128)(2,1)S(1)}, u32[]{:S(2)}, u32[]{:S(2)}) %all-to-all-start.3) | async-done | bytes 524320 | tf_op jit(solution)/shard_map/all_to_all | solution.py:195
  199.6 5.8 %all-to-all-start.4 = ((bf16[128,1,2,256]{3,2,1,0:T(2,128)(2,1)}), bf16[128,1,2,256]{3,2,1,0:T(2,128)(2,1)S(1)}, u32[]{:S(2)}, u32[]{:S(2)}) async-start(bf16[128,1,2,256]{3,2,1,0:T(2,128)(2,1)} %bitcast.130), calls=%async_computation.4 | async-start | bytes 262144 | tf_op jit(solution)/shard_map/all_to_all | solution.py:197
  205.5 12.8 %all-to-all-done.4 = bf16[128,1,2,256]{3,2,1,0:T(2,128)(2,1)S(1)} async-done(((bf16[128,1,2,256]{3,2,1,0:T(2,128)(2,1)}), bf16[128,1,2,256]{3,2,1,0:T(2,128)(2,1)S(1)}, u32[]{:S(2)}, u32[]{:S(2)}) %all-to-all-start.4) | async-done | bytes 131104 | tf_op jit(solution)/shard_map/all_to_all | solution.py:197
  218.3 1.6 gather_fusion.3
  (118 shorter events, 22.2 us)
Async XLA Ops:
  6.5 174.8 %copy-start = (bf16[1,1024,704]{1,2,0:T(8,128)(2,1)S(1)}, bf16[1,1024,704]{1,2,0:T(8,128)(2,1)}, u32[]{:S(2)}) copy-start(bf16[1,1024,704]{1,2,0:T(8,128)(2,1)} %param.34) | copy-start | bytes 4325380
  6.5 30.7 %copy-start.13 = (s32[128]{0:T(128)S(1)}, s32[128]{0:T(128)}, u32[]{:S(2)}) copy-start(s32[128]{0:T(128)} %param.35) | copy-start | bytes 1540
  6.5 97.4 %all-gather.3.cloned.1.call-start = ((), (), s32[]{:S(2)}) async-start(), calls=%async_computation.5 | async-start | bytes 4227072 | tf_op jit(solution)/shard_map/all_gather | solution.py:129
  18.1 35.0 %all-to-all-start = ((bf16[128,2,576]{2,1,0:T(2,128)(2,1)}), bf16[128,2,576]{2,1,0:T(2,128)(2,1)S(1)}, u32[]{:S(2)}, u32[]{:S(2)}) async-start(bf16[128,2,576]{2,1,0:T(2,128)(2,1)} %reshape.446), calls=%async_computation | async-start | bytes 655360 | tf_op jit(solution)/shard_map/all_to_all | solution.py:137
  36.5 104.2 %all-gather.5.cloned.1.call-start = ((), (), s32[]{:S(2)}) async-start(), calls=%async_computation.6 | async-start | bytes 2621440 | tf_op jit(solution)/shard_map/all_gather | solution.py:161
  53.6 8.5 %copy-start.10 = (s32[128]{0:T(128)S(1)}, s32[128]{0:T(128)}, u32[]{:S(2)}) copy-start(s32[128]{0:T(128)} %param.27) | copy-start | bytes 1540
  56.5 22.1 %all-to-all-start.1 = ((bf16[128,2,576]{2,1,0:T(2,128)(2,1)}), bf16[128,2,576]{2,1,0:T(2,128)(2,1)S(1)}, u32[]{:S(2)}, u32[]{:S(2)}) async-start(bf16[128,2,576]{2,1,0:T(2,128)(2,1)} %reshape.448), calls=%async_computation.1 | async-start | bytes 655360 | tf_op jit(solution)/shard_map/all_to_all | solution.py:139
  82.1 4.9 %copy-start.4 = (bf16[128,256]{0,1:T(8,128)(2,1)}, bf16[128,256]{0,1:T(8,128)(2,1)S(1)}, u32[]{:S(2)}) copy-start(bf16[128,256]{0,1:T(8,128)(2,1)S(1)} %copy.78) | copy-start | bytes 196612
  85.9 1.1 copy-start.11
  107.5 2.9 %copy-start.3 = (f32[4,128,128]{1,2,0:T(8,128)S(1)}, f32[4,128,128]{1,2,0:T(8,128)}, u32[]{:S(2)}) copy-start(f32[4,128,128]{1,2,0:T(8,128)} %get-tuple-element.48) | copy-start | bytes 786436
  108.9 2.1 copy-start.2
  111.0 1.1 copy-start.7
  111.0 1.4 copy-start.5
  111.0 1.4 copy-start.8
  112.3 30.6 %copy-start.9 = (f32[1024]{0:T(1024)S(1)}, f32[1024]{0:T(1024)}, u32[]{:S(2)}) copy-start(f32[1024]{0:T(1024)} %param.29) | copy-start | bytes 12292
  125.1 17.7 %copy-start.1 = (bf16[272,1024]{1,0:T(8,128)(2,1)}, bf16[272,1024]{1,0:T(8,128)(2,1)S(1)}, u32[]{:S(2)}) copy-start(bf16[272,1024]{1,0:T(8,128)(2,1)S(1)} %all_gather.10) | copy-start | bytes 1671172
  142.9 1.4 copy-start.6
  145.7 32.8 %all-to-all-start.2 = ((bf16[128,1,2,1024]{3,2,1,0:T(2,128)(2,1)}), bf16[128,1,2,1024]{3,2,1,0:T(2,128)(2,1)S(1)}, u32[]{:S(2)}, u32[]{:S(2)}) async-start(bf16[128,1,2,1024]{3,2,1,0:T(2,128)(2,1)} %fusion.43), calls=%async_computation.2 | async-start | bytes 1048576 | tf_op jit(solution)/shard_map/all_to_all | solution.py:184
  185.5 13.3 %all-to-all-start.3 = ((bf16[128,1,2,4,256]{4,0,2,1,3:T(8,128)(2,1)}), bf16[128,1,2,4,256]{4,0,2,1,3:T(8,128)(2,1)S(1)}, u32[]{:S(2)}, u32[]{:S(2)}) async-start(bf16[128,1,2,4,256]{4,0,2,1,3:T(8,128)(2,1)} %bitcast.134), calls=%async_computation.3 | async-start | bytes 1048576 | tf_op jit(solution)/shard_map/all_to_all | solution.py:195
  192.2 28.0 %copy-start.12 = (pred[128]{0:T(512)(128)(4,1)S(1)}, pred[128]{0:T(512)(128)(4,1)}, u32[]{:S(2)}) copy-start(pred[128]{0:T(512)(128)(4,1)} %copy-done.11) | copy-start | bytes 388
  199.6 18.6 %all-to-all-start.4 = ((bf16[128,1,2,256]{3,2,1,0:T(2,128)(2,1)}), bf16[128,1,2,256]{3,2,1,0:T(2,128)(2,1)S(1)}, u32[]{:S(2)}, u32[]{:S(2)}) async-start(bf16[128,1,2,256]{3,2,1,0:T(2,128)(2,1)} %bitcast.130), calls=%async_computation.4 | async-start | bytes 262144 | tf_op jit(solution)/shard_map/all_to_all | solution.py:197
Sparse Core Ops, SparseCore 0:
  10.5 93.4 all-gather.2
  106.0 34.5 all-gather.4

commit v3 on v2

--- a/solution.py
+++ b/solution.py
@@ -1,7 +1,7 @@
 import jax
 import jax.numpy as jnp
 from jax import lax
-from jax.sharding import PartitionSpec as P
+from jax.sharding import Mesh, PartitionSpec as P
 
 DH = 64
 EXPERTS = 16
@@ -100,9 +100,11 @@
     down_weight,
     destinations,
 ):
-    seq_count = lax.axis_size("seq")
+    expert_count = lax.axis_size("ex")
+    replica_count = lax.axis_size("rep")
+    seq_count = expert_count * replica_count
     head_count = lax.axis_size("head")
-    seq_index = lax.axis_index("seq")
+    seq_index = lax.axis_index("ex") * replica_count + lax.axis_index("rep")
     head_index = lax.axis_index("head")
     row_count = hidden.shape[0]
     column_width = hidden.shape[1]
@@ -112,9 +114,16 @@
     page_local = key_cache.shape[0]
     page_rows = key_cache.shape[1]
     group_pages = page_local * block_devices
-    replicas = max(1, seq_count // EXPERTS)
-    per_device = max(1, EXPERTS // seq_count)
-    capacity = 5 * row_count * TOPK // (4 * EXPERTS * replicas)
+    capacity = row_count * TOPK // expert_count
+    ring = [
+        lax.ppermute(
+            out_weight,
+            "head",
+            [(source, (source + shift) % head_count) for source in range(head_count)],
+        )
+        for shift in range(1, head_count)
+    ]
+    rotated_weight = jnp.concatenate([out_weight] + ring, axis=0)
     inverse = page_inverse(page_group, group_pages, GROUPS)
     inverse_destination = (
         jnp.zeros((seq_count,), jnp.int32)
@@ -126,7 +135,7 @@
     local_pages = jnp.concatenate([key_cache, value_cache], axis=2).reshape(
         page_local * page_rows, 2 * features
     )
-    all_pages = lax.all_gather(local_pages, "seq", axis=0, tiled=False).reshape(
+    all_pages = lax.all_gather(local_pages, SEQ, axis=0, tiled=False).reshape(
         seq_count * page_local, page_rows, 2 * features
     )
     extra = jnp.zeros((row_count, 128), jnp.bfloat16)
@@ -134,9 +143,9 @@
     extra = extra.at[:, TOPK].set(lengths[0].astype(jnp.bfloat16))
     packed = jnp.concatenate([queries, suffix_keys, suffix_values, hidden, extra], axis=1)
     pieces = packed.reshape(seq_count, row_count // seq_count, packed.shape[1])
-    spread = lax.all_to_all(pieces, "seq", split_axis=0, concat_axis=0, tiled=True)
+    spread = lax.all_to_all(pieces, SEQ, split_axis=0, concat_axis=0, tiled=True)
     spread = jnp.take(spread, inverse_destination, axis=0)
-    moved = lax.all_to_all(spread, "seq", split_axis=0, concat_axis=0, tiled=True).reshape(
+    moved = lax.all_to_all(spread, SEQ, split_axis=0, concat_axis=0, tiled=True).reshape(
         row_count, packed.shape[1]
     )
     queries = moved[:, 0:features]
@@ -158,9 +167,12 @@
     full_attended = gathered[:row_count]
     full_hidden = gathered[row_count : 2 * row_count]
     full_router = gathered[2 * row_count :].T
-    full_weight = lax.all_gather(out_weight, "head", axis=0, tiled=True)
+    source_head = (head_index - jnp.arange(head_count, dtype=jnp.int32)) % head_count
+    rotated_attended = jnp.take(
+        full_attended.reshape(row_count, head_count, features), source_head, axis=1
+    ).reshape(row_count, head_count * features)
     resid = full_hidden.astype(jnp.float32) + jnp.dot(
-        full_attended, full_weight, preferred_element_type=jnp.float32
+        rotated_attended, rotated_weight, preferred_element_type=jnp.float32
     )
     normed = (
         resid * lax.rsqrt(jnp.mean(resid * resid, axis=1, keepdims=True) + norm_eps) * norm_gain
@@ -169,36 +181,34 @@
     chosen_logits = jnp.take_along_axis(logits, routes, axis=1)
     gate_first = jax.nn.sigmoid(chosen_logits[:, 0] - chosen_logits[:, 1])
     gate_second = jax.nn.sigmoid(chosen_logits[:, 1] - chosen_logits[:, 0])
-    target_device, local_slot, slot_rank = slot_table(routes, replicas, per_device, EXPERTS)
-    slot_flat = (target_device * per_device + local_slot) * capacity + slot_rank
-    slot_total = seq_count * per_device * capacity
     pair_count = row_count * TOPK
+    expert_flat = routes.reshape(-1)
+    onehot = (expert_flat[:, None] == jnp.arange(expert_count, dtype=jnp.int32)).astype(jnp.int32)
+    slot_rank = jnp.sum((jnp.cumsum(onehot, axis=0) - 1) * onehot, axis=1)
+    slot_flat = expert_flat * capacity + slot_rank
     slot_pair = (
-        jnp.zeros((slot_total,), jnp.int32)
+        jnp.zeros((expert_count * capacity,), jnp.int32)
         .at[slot_flat]
         .set(jnp.arange(pair_count, dtype=jnp.int32), mode="drop")
     )
     send_rows = jnp.take(normed, slot_pair // TOPK, axis=0).reshape(
-        seq_count, per_device, capacity, normed.shape[1]
-    )
-    slots = lax.all_to_all(send_rows, "seq", split_axis=0, concat_axis=0, tiled=True)
-    gate_act = jnp.einsum("spnd,pdf->spnf", slots, gate_weight, preferred_element_type=jnp.float32)
-    up_act = jnp.einsum("spnd,pdf->spnf", slots, up_weight, preferred_element_type=jnp.float32)
+        expert_count, capacity, normed.shape[1]
+    )
+    slots = lax.all_to_all(send_rows, "ex", split_axis=0, concat_axis=0, tiled=True)
+    gate_act = jnp.einsum("snd,df->snf", slots, gate_weight[0], preferred_element_type=jnp.float32)
+    up_act = jnp.einsum("snd,df->snf", slots, up_weight[0], preferred_element_type=jnp.float32)
     expert_hidden = (jax.nn.gelu(gate_act, approximate=True) * up_act).astype(jnp.bfloat16)
     partial_out = jnp.einsum(
-        "spnf,pdf->spnd", expert_hidden, down_weight, preferred_element_type=jnp.float32
-    )
-    part_dims = partial_out.shape
+        "snf,df->snd", expert_hidden, down_weight[0], preferred_element_type=jnp.float32
+    )
     split_part = partial_out.reshape(
-        part_dims[0], part_dims[1], part_dims[2], head_count, part_dims[3] // head_count
+        expert_count, capacity, head_count, column_width
     ).astype(jnp.bfloat16)
-    by_head = lax.all_to_all(split_part, "head", split_axis=3, concat_axis=3, tiled=True)
-    summed = jnp.sum(by_head.astype(jnp.float32), axis=3).astype(jnp.bfloat16)
-    returned = lax.all_to_all(summed, "seq", split_axis=0, concat_axis=0, tiled=True)
+    by_head = lax.all_to_all(split_part, "head", split_axis=2, concat_axis=2, tiled=True)
+    summed = jnp.sum(by_head.astype(jnp.float32), axis=2).astype(jnp.bfloat16)
+    returned = lax.all_to_all(summed, "ex", split_axis=0, concat_axis=0, tiled=True)
     picked = (
-        returned[target_device, local_slot, slot_rank]
-        .astype(jnp.float32)
-        .reshape(row_count, TOPK, column_width)
+        returned[expert_flat, slot_rank].astype(jnp.float32).reshape(row_count, TOPK, column_width)
     )
     resid_columns = lax.dynamic_slice_in_dim(resid, head_index * column_width, column_width, 1)
     layer = resid_columns + gate_first[:, None] * picked[:, 0] + gate_second[:, None] * picked[:, 1]
@@ -207,28 +217,36 @@
     return jnp.where(live_rows[:, None], layer, jnp.zeros_like(layer))
 
 
+SEQ = ("ex", "rep")
+
+
 def solution(mesh):
+    seq_count = mesh.shape["seq"]
+    fine = Mesh(
+        mesh.devices.reshape(EXPERTS, seq_count // EXPERTS, mesh.shape["head"]),
+        ("ex", "rep", "head"),
+    )
     return jax.shard_map(
         on_device,
-        mesh=mesh,
+        mesh=fine,
         in_specs=(
-            P("seq", "head"),
-            P("seq", "head"),
-            P("seq", "head"),
-            P("seq", "head"),
-            P("seq"),
-            P("seq", None, "head"),
-            P("seq", None, "head"),
+            P(SEQ, "head"),
+            P(SEQ, "head"),
+            P(SEQ, "head"),
+            P(SEQ, "head"),
+            P(SEQ),
+            P(SEQ, None, "head"),
+            P(SEQ, None, "head"),
             P(),
             P("head", None),
             P(),
             P("head", None),
-            P("seq", None),
-            P("seq", None, "head"),
-            P("seq", None, "head"),
-            P("seq", None, "head"),
+            P(SEQ, None),
+            P(SEQ, None, "head"),
+            P(SEQ, None, "head"),
+            P(SEQ, None, "head"),
             P(),
         ),
-        out_specs=P("seq", "head"),
+        out_specs=P(SEQ, "head"),
         check_vma=False,
     )

time: 229 us -> 217 us (0.948)
  the two profiles are of different devices: /device:TPU:1 before, /device:TPU:8 now
where the time goes in v3:
time: 217 us; the launch traced here: 216 us
  waiting for transfers between devices  67.7 us (31%)
  starting transfers between devices  51.2 us (24%)
  local copies, waits for them, and re-layouts  37 us (17%)
  between operations  18.6 us (9%)
  matrix products  14.5 us (7%)
  other arithmetic  14.2 us (7%)
  blocking collectives  12.9 us (6%)
    all_to_all x1, starting transfers between devices, on_device(): lax.all_to_all(pieces, SEQ, split_axis=0, concat_axis=0, tiled=True)  17.4 us
    all_to_all x1, waiting for transfers between devices, on_device(): lax.all_to_all(send_rows, 'ex', split_axis=0, concat_axis=0, tiled=True)  15.2 us
    all_to_all x1, waiting for transfers between devices, on_device(): lax.all_to_all(pieces, SEQ, split_axis=0, concat_axis=0, tiled=True)  14.7 us
    all_to_all x1, waiting for transfers between devices, on_device(): lax.all_to_all(spread, SEQ, split_axis=0, concat_axis=0, tiled=True)  13.8 us
    all_to_all x1, waiting for transfers between devices, on_device(): lax.all_to_all(summed, 'ex', split_axis=0, concat_axis=0, tiled=True)  13 us
    all_gather x1, blocking collectives, on_device(): gathered = lax.all_gather(stacked, 'head', axis=1, tiled=True)  12.9 us
    ppermute x3, starting transfers between devices, on_device(): lax.ppermute(out_weight, 'head', [(source, (source + shift) % head_count)...  11.4 us
    unnamed x43, local copies, waits for them, and re-layouts  7.8 us
  transfers between devices with their start and end apart: 9, of which 6 were waited for; matrix products, arithmetic and copies ran while one was open for 21% of the time, Pallas kernels for 0%

profile of v3, /device:TPU:8, one launch (start us, length us, event | category | flops | bytes accessed | tf_op | source)
XLA Modules:
  0.0 216.1 jit_solution(16326913949358408134)
XLA Ops:
  6.5 1.4 pad_maximum_fusion.1
  8.0 3.4 %collective-permute-start = (bf16[256,1024]{1,0:T(8,128)(2,1)}, bf16[256,1024]{1,0:T(8,128)(2,1)}, u32[]{:S(2)}, u32[]{:S(2)}) collective-permute-start(bf16[256,1024]{1,0:T(8,128)(2,1)} %param.28), channel_id=1, source_target_pairs={{0,1},{1,2},{2,3},{3,0},{4,5},{5,6},{6,7},{7,4},{8,9},{9,10},{10,1... | collective-permute-start | bytes 1572872 | tf_op jit(solution)/shard_map/ppermute | solution.py:119
  11.4 4.6 %collective-permute-start.1 = (bf16[256,1024]{1,0:T(8,128)(2,1)}, bf16[256,1024]{1,0:T(8,128)(2,1)}, u32[]{:S(2)}, u32[]{:S(2)}) collective-permute-start(bf16[256,1024]{1,0:T(8,128)(2,1)} %param.28), channel_id=1, source_target_pairs={{0,2},{1,3},{2,0},{3,1},{4,6},{5,7},{6,4},{7,5},{8,10},{9,11},{10,... | collective-permute-start | bytes 1572872 | tf_op jit(solution)/shard_map/ppermute | solution.py:119
  16.1 3.3 %collective-permute-start.2 = (bf16[256,1024]{1,0:T(8,128)(2,1)}, bf16[256,1024]{1,0:T(8,128)(2,1)}, u32[]{:S(2)}, u32[]{:S(2)}) collective-permute-start(bf16[256,1024]{1,0:T(8,128)(2,1)} %param.28), channel_id=1, source_target_pairs={{0,3},{1,0},{2,1},{3,2},{4,7},{5,4},{6,5},{7,6},{8,11},{9,8},{10,9... | collective-permute-start | bytes 1572872 | tf_op jit(solution)/shard_map/ppermute | solution.py:119
  29.5 17.4 %all-to-all-start = ((bf16[128,2,576]{2,1,0:T(2,128)(2,1)}), bf16[128,2,576]{2,1,0:T(2,128)(2,1)S(1)}, u32[]{:S(2)}, u32[]{:S(2)}) async-start(bf16[128,2,576]{2,1,0:T(2,128)(2,1)} %reshape.438), calls=%async_computation | async-start | bytes 655360 | tf_op jit(solution)/shard_map/all_to_all | solution.py:146
  48.3 14.7 %all-to-all-done = bf16[128,2,576]{2,1,0:T(2,128)(2,1)S(1)} async-done(((bf16[128,2,576]{2,1,0:T(2,128)(2,1)}), bf16[128,2,576]{2,1,0:T(2,128)(2,1)S(1)}, u32[]{:S(2)}, u32[]{:S(2)}) %all-to-all-start) | async-done | bytes 294944 | tf_op jit(solution)/shard_map/all_to_all | solution.py:146
  66.5 5.9 %all-to-all-start.1 = ((bf16[128,2,576]{2,1,0:T(2,128)(2,1)}), bf16[128,2,576]{2,1,0:T(2,128)(2,1)S(1)}, u32[]{:S(2)}, u32[]{:S(2)}) async-start(bf16[128,2,576]{2,1,0:T(2,128)(2,1)} %reshape.440), calls=%async_computation.1 | async-start | bytes 655360 | tf_op jit(solution)/shard_map/all_to_all | solution.py:148
  77.4 13.8 %all-to-all-done.1 = bf16[128,2,576]{2,1,0:T(2,128)(2,1)S(1)} async-done(((bf16[128,2,576]{2,1,0:T(2,128)(2,1)}), bf16[128,2,576]{2,1,0:T(2,128)(2,1)S(1)}, u32[]{:S(2)}, u32[]{:S(2)}) %all-to-all-start.1) | async-done | bytes 294944 | tf_op jit(solution)/shard_map/all_to_all | solution.py:148
  96.7 1.6 scatter_custom_fusion.2
  100.0 6.4 %all-gather.2.cloned.1.call-done = bf16[128,32,512]{2,1,0:T(8,128)(2,1)} async-done(((bf16[1,32,512]{2,1,0:T(8,128)(2,1)}), bf16[128,32,512]{2,1,0:T(8,128)(2,1)}) %all-gather.2.cloned.1.call-update) | async-done | bytes 4194320 | tf_op jit(solution)/shard_map/all_gather | solution.py:138
  106.4 2.8 %gather_fusion.1 = bf16[32,32,512]{2,1,0:T(8,128)(2,1)S(1)} fusion(bf16[128,32,512]{2,1,0:T(8,128)(2,1)} %all-gather.2.cloned.1.call-done, s32[1024]{0:T(1024)S(1)} %pad_clamp_fusion.2), kind=kCustom, calls=%fused_computation.1 | custom fusion | bytes 2097280 | tf_op jit(solution)/shard_map/jit(_take)/gather | solution.py:159
  110.3 1.4 reshape_reshape.7
  111.7 1.9 multiply_reduce_fusion
  113.6 1.1 fusion.8
  114.7 2.8 %reshape_reshape.6 = bf16[1024,4,64]{2,1,0:T(4,128)(2,1)} reshape(bf16[32,32,256]{2,1,0:T(8,128)(2,1)} %get-tuple-element.34) | data formatting | bytes 1048576 | tf_op jit(solution)/shard_map/reshape;reshape | solution.py:31
  118.1 2.1 fusion.33
  121.5 12.9 %all_gather.7 = bf16[272,1024]{1,0:T(8,128)(2,1)S(1)} all-gather(bf16[272,256]{1,0:T(8,128)(2,1)S(1)} %pad_maximum_fusion), channel_id=1, replica_groups=mesh['ex'=16,'rep'=8,'head'=4] {'head'}, dimensions={1}, use_global_device_ids=true | all-gather | bytes 696320 | tf_op jit(solution)/shard_map/all_gather | solution.py:166
  135.5 1.9 multiply_reduce_fusion.1
  138.3 1.3 gather_fusion.3
  140.5 7.6 %all-to-all-start.2 = ((bf16[16,16,1024]{2,1,0:T(8,128)(2,1)}), bf16[16,16,1024]{2,1,0:T(8,128)(2,1)}, u32[]{:S(2)}, u32[]{:S(2)}) async-start(bf16[16,16,1024]{2,1,0:T(8,128)(2,1)} %broadcast_select_fusion.1), calls=%async_computation.2 | async-start | bytes 1048576 | tf_op jit(solution)/shard_map/all_to_all | solution.py:197
  148.2 3.1 %dot_general.37 = bf16[4,256,704]{1,0,2:T(4,128)(2,1)S(1)} reshape(bf16[1,1024,704]{1,2,0:T(8,128)(2,1)} %param.34) | data formatting | bytes 2883584 | tf_op jit(solution)/shard_map/snf,df->snd/dot_general | solution.py:201
  151.2 15.2 %all-to-all-done.2 = bf16[16,16,1024]{2,1,0:T(8,128)(2,1)} async-done(((bf16[16,16,1024]{2,1,0:T(8,128)(2,1)}), bf16[16,16,1024]{2,1,0:T(8,128)(2,1)}, u32[]{:S(2)}, u32[]{:S(2)}) %all-to-all-start.2) | async-done | bytes 524320 | tf_op jit(solution)/shard_map/all_to_all | solution.py:197
  166.4 3.1 %fusion.45 = f32[16,16,704]{2,1,0:T(8,128)} fusion(bf16[16,16,1024]{2,1,0:T(8,128)(2,1)} %all-to-all-done.2, bf16[1,1024,704]{1,2,0:T(8,128)(2,1)} %param.32), kind=kOutput, calls=%fused_computation.49 | convolution fusion | flops 370540544 | bytes 2686976 | tf_op jit(solution)/shard_map/snd,df->snf/dot_general | solution.py:198
  169.5 3.4 %fusion.19 = bf16[16,16,4,256]{3,1,2,0:T(8,128)(2,1)} fusion(bf16[4,256,704]{1,0,2:T(4,128)(2,1)S(1)} %dot_general.37, f32[16,16,704]{2,1,0:T(8,128)} %fusion.45, bf16[16,16,1024]{2,1,0:T(8,128)(2,1)} %all-to-all-done.2, bf16[1,1024,704]{1,2,0:T(8,128)(2,1)S(1)} %copy-done), kind=kOutput, calls=%fused_computation.29 | convolution fusion | flops 738820096 | bytes 4653056 | tf_op jit(solution)/shard_map/snf,df->snd/dot_general | solution.py:201
  173.0 1.9 copy.106
  174.9 3.5 %all-to-all-start.3 = ((bf16[16,16,4,256]{3,1,0,2:T(8,128)(2,1)}), bf16[16,16,4,256]{3,1,0,2:T(8,128)(2,1)S(1)}, u32[]{:S(2)}, u32[]{:S(2)}) async-start(bf16[16,16,4,256]{3,1,0,2:T(8,128)(2,1)} %copy.106), calls=%async_computation.3 | async-start | bytes 1048576 | tf_op jit(solution)/shard_map/all_to_all | solution.py:207
  179.6 2.0 gather_fusion.5
  181.8 4.7 %all-to-all-done.3 = bf16[16,16,4,256]{3,1,0,2:T(8,128)(2,1)S(1)} async-done(((bf16[16,16,4,256]{3,1,0,2:T(8,128)(2,1)}), bf16[16,16,4,256]{3,1,0,2:T(8,128)(2,1)S(1)}, u32[]{:S(2)}, u32[]{:S(2)}) %all-to-all-start.3) | async-done | bytes 524320 | tf_op jit(solution)/shard_map/all_to_all | solution.py:207
  187.2 5.3 %all-to-all-start.4 = ((bf16[16,16,256]{2,1,0:T(8,128)(2,1)}), bf16[16,16,256]{2,1,0:T(8,128)(2,1)S(1)}, u32[]{:S(2)}, u32[]{:S(2)}) async-start(bf16[16,16,256]{2,1,0:T(8,128)(2,1)} %reduce_sum.65), calls=%async_computation.4 | async-start | bytes 262144 | tf_op jit(solution)/shard_map/all_to_all | solution.py:209
  192.6 13.0 %all-to-all-done.4 = bf16[16,16,256]{2,1,0:T(8,128)(2,1)S(1)} async-done(((bf16[16,16,256]{2,1,0:T(8,128)(2,1)}), bf16[16,16,256]{2,1,0:T(8,128)(2,1)S(1)}, u32[]{:S(2)}, u32[]{:S(2)}) %all-to-all-start.4) | async-done | bytes 131104 | tf_op jit(solution)/shard_map/all_to_all | solution.py:209
  205.6 1.7 gather_fusion.4
  207.6 1.7 fusion.56
  (133 shorter events, 30.6 us)
Async XLA Ops:
  6.5 163.0 %copy-start = (bf16[1,1024,704]{1,2,0:T(8,128)(2,1)S(1)}, bf16[1,1024,704]{1,2,0:T(8,128)(2,1)}, u32[]{:S(2)}) copy-start(bf16[1,1024,704]{1,2,0:T(8,128)(2,1)} %param.33) | copy-start | bytes 4325380
  6.5 40.3 %copy-start.9 = (s32[128]{0:T(128)S(1)}, s32[128]{0:T(128)}, u32[]{:S(2)}) copy-start(s32[128]{0:T(128)} %param.27) | copy-start | bytes 1540
  6.5 40.6 %copy-start.15 = (s32[128]{0:T(128)S(1)}, s32[128]{0:T(128)}, u32[]{:S(2)}) copy-start(s32[128]{0:T(128)} %param.35) | copy-start | bytes 1540
  6.5 99.8 %all-gather.2.cloned.1.call-start = ((), (), s32[]{:S(2)}) async-start(), calls=%async_computation.5 | async-start | bytes 4227072 | tf_op jit(solution)/shard_map/all_gather | solution.py:138
  8.0 127.5 %collective-permute-start = (bf16[256,1024]{1,0:T(8,128)(2,1)}, bf16[256,1024]{1,0:T(8,128)(2,1)}, u32[]{:S(2)}, u32[]{:S(2)}) collective-permute-start(bf16[256,1024]{1,0:T(8,128)(2,1)} %param.28), channel_id=1, source_target_pairs={{0,1},{1,2},{2,3},{3,0},{4,5},{5,6},{6,7},{7,4},{8,9},{9,10},{10,1... | collective-permute-start | bytes 1572872 | tf_op jit(solution)/shard_map/ppermute | solution.py:119
  11.4 124.1 %collective-permute-start.1 = (bf16[256,1024]{1,0:T(8,128)(2,1)}, bf16[256,1024]{1,0:T(8,128)(2,1)}, u32[]{:S(2)}, u32[]{:S(2)}) collective-permute-start(bf16[256,1024]{1,0:T(8,128)(2,1)} %param.28), channel_id=1, source_target_pairs={{0,2},{1,3},{2,0},{3,1},{4,6},{5,7},{6,4},{7,5},{8,10},{9,11},{10,... | collective-permute-start | bytes 1572872 | tf_op jit(solution)/shard_map/ppermute | solution.py:119
  16.1 119.5 %collective-permute-start.2 = (bf16[256,1024]{1,0:T(8,128)(2,1)}, bf16[256,1024]{1,0:T(8,128)(2,1)}, u32[]{:S(2)}, u32[]{:S(2)}) collective-permute-start(bf16[256,1024]{1,0:T(8,128)(2,1)} %param.28), channel_id=1, source_target_pairs={{0,3},{1,0},{2,1},{3,2},{4,7},{5,4},{6,5},{7,6},{8,11},{9,8},{10,9... | collective-permute-start | bytes 1572872 | tf_op jit(solution)/shard_map/ppermute | solution.py:119
  29.5 33.6 %all-to-all-start = ((bf16[128,2,576]{2,1,0:T(2,128)(2,1)}), bf16[128,2,576]{2,1,0:T(2,128)(2,1)S(1)}, u32[]{:S(2)}, u32[]{:S(2)}) async-start(bf16[128,2,576]{2,1,0:T(2,128)(2,1)} %reshape.438), calls=%async_computation | async-start | bytes 655360 | tf_op jit(solution)/shard_map/all_to_all | solution.py:146
  66.5 24.7 %all-to-all-start.1 = ((bf16[128,2,576]{2,1,0:T(2,128)(2,1)}), bf16[128,2,576]{2,1,0:T(2,128)(2,1)S(1)}, u32[]{:S(2)}, u32[]{:S(2)}) async-start(bf16[128,2,576]{2,1,0:T(2,128)(2,1)} %reshape.440), calls=%async_computation.1 | async-start | bytes 655360 | tf_op jit(solution)/shard_map/all_to_all | solution.py:148
  92.5 0.6 copy-start.10
  94.2 5.8 %copy-start.5 = (bf16[128,256]{0,1:T(8,128)(2,1)}, bf16[128,256]{0,1:T(8,128)(2,1)S(1)}, u32[]{:S(2)}) copy-start(bf16[128,256]{0,1:T(8,128)(2,1)S(1)} %copy.89) | copy-start | bytes 196612
  98.3 1.7 copy-start.12
  111.7 1.9 copy-start.2
  118.1 2.1 copy-start.3
  118.1 2.1 copy-start.6
  120.3 15.0 %copy-start.8 = (pred[1024]{0:T(1024)(128)(4,1)S(1)}, pred[1024]{0:T(1024)(128)(4,1)}, u32[]{:S(2)}) copy-start(pred[1024]{0:T(1024)(128)(4,1)} %broadcast_in_dim.116) | copy-start | bytes 3076
  120.5 15.1 %copy-start.14 = (bf16[256,1024]{1,0:T(8,128)(2,1)S(1)}, bf16[256,1024]{1,0:T(8,128)(2,1)}, u32[]{:S(2)}) copy-start(bf16[256,1024]{1,0:T(8,128)(2,1)} %param.28) | copy-start | bytes 1572868
  134.3 3.1 %copy-start.1 = (bf16[272,1024]{1,0:T(8,128)(2,1)}, bf16[272,1024]{1,0:T(8,128)(2,1)S(1)}, u32[]{:S(2)}) copy-start(bf16[272,1024]{1,0:T(8,128)(2,1)S(1)} %all_gather.7) | copy-start | bytes 1671172
  135.5 2.0 copy-start.7
  137.5 0.8 copy-start.4
  140.5 25.9 %all-to-all-start.2 = ((bf16[16,16,1024]{2,1,0:T(8,128)(2,1)}), bf16[16,16,1024]{2,1,0:T(8,128)(2,1)}, u32[]{:S(2)}, u32[]{:S(2)}) async-start(bf16[16,16,1024]{2,1,0:T(8,128)(2,1)} %broadcast_select_fusion.1), calls=%async_computation.2 | async-start | bytes 1048576 | tf_op jit(solution)/shard_map/all_to_all | solution.py:197
  173.0 5.4 %copy-start.11 = (bf16[128,2]{0,1:T(2,128)(2,1)S(1)}, bf16[128,2]{0,1:T(2,128)(2,1)}, u32[]{:S(2)}) copy-start(bf16[128,2]{0,1:T(2,128)(2,1)} %copy-done.10) | copy-start | bytes 1540
  174.9 11.6 %all-to-all-start.3 = ((bf16[16,16,4,256]{3,1,0,2:T(8,128)(2,1)}), bf16[16,16,4,256]{3,1,0,2:T(8,128)(2,1)S(1)}, u32[]{:S(2)}, u32[]{:S(2)}) async-start(bf16[16,16,4,256]{3,1,0,2:T(8,128)(2,1)} %copy.106), calls=%async_computation.3 | async-start | bytes 1048576 | tf_op jit(solution)/shard_map/all_to_all | solution.py:207
  181.6 26.0 %copy-start.13 = (pred[128]{0:T(512)(128)(4,1)S(1)}, pred[128]{0:T(512)(128)(4,1)}, u32[]{:S(2)}) copy-start(pred[128]{0:T(512)(128)(4,1)} %copy-done.12) | copy-start | bytes 388
  187.2 18.3 %all-to-all-start.4 = ((bf16[16,16,256]{2,1,0:T(8,128)(2,1)}), bf16[16,16,256]{2,1,0:T(8,128)(2,1)S(1)}, u32[]{:S(2)}, u32[]{:S(2)}) async-start(bf16[16,16,256]{2,1,0:T(8,128)(2,1)} %reduce_sum.65), calls=%async_computation.4 | async-start | bytes 262144 | tf_op jit(solution)/shard_map/all_to_all | solution.py:209
Sparse Core Ops, SparseCore 0:
  10.5 95.8 all-gather.1

commit v4 on v3

--- a/solution.py
+++ b/solution.py
@@ -115,15 +115,17 @@
     page_rows = key_cache.shape[1]
     group_pages = page_local * block_devices
     capacity = row_count * TOPK // expert_count
-    ring = [
-        lax.ppermute(
-            out_weight,
-            "head",
-            [(source, (source + shift) % head_count) for source in range(head_count)],
-        )
-        for shift in range(1, head_count)
-    ]
-    rotated_weight = jnp.concatenate([out_weight] + ring, axis=0)
+    def head_ring(block):
+        return [
+            lax.ppermute(
+                block,
+                "head",
+                [(source, (source + shift) % head_count) for source in range(head_count)],
+            )
+            for shift in range(1, head_count)
+        ]
+
+    rotated_weight = jnp.concatenate([out_weight] + head_ring(out_weight), axis=0)
     inverse = page_inverse(page_group, group_pages, GROUPS)
     inverse_destination = (
         jnp.zeros((seq_count,), jnp.int32)
@@ -162,15 +164,14 @@
     attended = attend_rows(
         queries, suffix_keys, suffix_values, prefix_keys, prefix_values, length, local_heads
     )
-    stacked = jnp.concatenate([attended, hidden, router_weight.T], axis=0)
-    gathered = lax.all_gather(stacked, "head", axis=1, tiled=True)
-    full_attended = gathered[:row_count]
-    full_hidden = gathered[row_count : 2 * row_count]
-    full_router = gathered[2 * row_count :].T
+    side = jnp.concatenate([hidden, router_weight.T], axis=0)
+    rotated_side = jnp.stack([side] + head_ring(side), axis=0)
     source_head = (head_index - jnp.arange(head_count, dtype=jnp.int32)) % head_count
-    rotated_attended = jnp.take(
-        full_attended.reshape(row_count, head_count, features), source_head, axis=1
-    ).reshape(row_count, head_count * features)
+    side_blocks = jnp.take(rotated_side, source_head, axis=0)
+    full_side = jnp.transpose(side_blocks, (1, 0, 2)).reshape(side.shape[0], head_count * features)
+    full_hidden = full_side[:row_count]
+    full_router = full_side[row_count:].T
+    rotated_attended = jnp.concatenate([attended] + head_ring(attended), axis=1)
     resid = full_hidden.astype(jnp.float32) + jnp.dot(
         rotated_attended, rotated_weight, preferred_element_type=jnp.float32
     )
@@ -201,12 +202,13 @@
     partial_out = jnp.einsum(
         "snf,df->snd", expert_hidden, down_weight[0], preferred_element_type=jnp.float32
     )
-    split_part = partial_out.reshape(
-        expert_count, capacity, head_count, column_width
+    split_part = jnp.transpose(
+        partial_out.reshape(expert_count, capacity, head_count, column_width), (0, 2, 1, 3)
     ).astype(jnp.bfloat16)
-    by_head = lax.all_to_all(split_part, "head", split_axis=2, concat_axis=2, tiled=True)
-    summed = jnp.sum(by_head.astype(jnp.float32), axis=2).astype(jnp.bfloat16)
-    returned = lax.all_to_all(summed, "ex", split_axis=0, concat_axis=0, tiled=True)
+    split_part = split_part.reshape(expert_count * head_count, capacity, column_width)
+    arrived = lax.all_to_all(split_part, ("ex", "head"), split_axis=0, concat_axis=0, tiled=True)
+    arrived = arrived.reshape(expert_count, head_count, capacity, column_width)
+    returned = jnp.sum(arrived.astype(jnp.float32), axis=1).astype(jnp.bfloat16)
     picked = (
         returned[expert_flat, slot_rank].astype(jnp.float32).reshape(row_count, TOPK, column_width)
     )

time: 217 us -> 214 us (0.986)
  starting transfers between devices: 51.2 us -> 66.8 us
  blocking collectives: 12.9 us -> 0 us
  local copies, waits for them, and re-layouts: 37 us -> 34.1 us
  waiting for transfers between devices: 67.7 us -> 65.4 us
    ppermute x3 -> x9, starting transfers between devices: 11.4 us -> 31.1 us  [head_ring(): lax.ppermute(block, 'head', [(source, (source + shift) % head_count) for...]
    all_gather x1 -> x0, blocking collectives: 12.9 us -> none  [on_device(): gathered = lax.all_gather(stacked, 'head', axis=1, tiled=True)]
    all_gather x1, waiting for transfers between devices: 6.37 us -> 0.01 us  [on_device(): lax.all_gather(local_pages, SEQ, axis=0, tiled=False)]
    all_to_all x1, starting transfers between devices: 7.64 us -> 4.55 us  [on_device(): lax.all_to_all(send_rows, 'ex', split_axis=0, concat_axis=0, tiled=True)]
    ppermute x3 -> x9, waiting for transfers between devices: 0.01 us -> 2.8 us  [head_ring(): lax.ppermute(block, 'head', [(source, (source + shift) % head_count) for...]
    unnamed x43 -> x42, local copies, waits for them, and re-layouts: 7.8 us -> 8.78 us
    all_to_all x2 -> x1, starting transfers between devices: 8.85 us -> 7.99 us  [on_device(): lax.all_to_all(split_part, ('ex', 'head'), split_axis=0, concat_axis=0, t...]
    all_to_all x2 -> x1, waiting for transfers between devices: 17.6 us -> 18.2 us  [on_device(): lax.all_to_all(split_part, ('ex', 'head'), split_axis=0, concat_axis=0, t...]
  transfers between devices with their start and end apart: 9 -> 14, of which waited for: 6 -> 5; matrix products, arithmetic and copies ran while one was open for 21% -> 21% of each run, Pallas kernels for 0% -> 0%
where the time goes in v4:
time: 214 us; the launch traced here: 212 us
  starting transfers between devices  66.8 us (31%)
  waiting for transfers between devices  65.4 us (31%)
  local copies, waits for them, and re-layouts  34.1 us (16%)
  between operations  18.6 us (9%)
  matrix products  14 us (7%)
  other arithmetic  13.5 us (6%)
    ppermute x9, starting transfers between devices, head_ring(): lax.ppermute(block, 'head', [(source, (source + shift) % head_count) for...  31.1 us
    all_to_all x1, waiting for transfers between devices, on_device(): lax.all_to_all(split_part, ('ex', 'head'), split_axis=0, concat_axis=0, t...  18.2 us
    all_to_all x1, starting transfers between devices, on_device(): lax.all_to_all(pieces, SEQ, split_axis=0, concat_axis=0, tiled=True)  17.4 us
    all_to_all x1, waiting for transfers between devices, on_device(): lax.all_to_all(send_rows, 'ex', split_axis=0, concat_axis=0, tiled=True)  16.3 us
    all_to_all x1, waiting for transfers between devices, on_device(): lax.all_to_all(pieces, SEQ, split_axis=0, concat_axis=0, tiled=True)  14.8 us
    all_to_all x1, waiting for transfers between devices, on_device(): lax.all_to_all(spread, SEQ, split_axis=0, concat_axis=0, tiled=True)  13.3 us
    unnamed x42, local copies, waits for them, and re-layouts  8.78 us
    all_to_all x1, starting transfers between devices, on_device(): lax.all_to_all(split_part, ('ex', 'head'), split_axis=0, concat_axis=0, t...  7.99 us
  transfers between devices with their start and end apart: 14, of which 5 were waited for; matrix products, arithmetic and copies ran while one was open for 21% of the time, Pallas kernels for 0%

profile of v4, /device:TPU:8, one launch (start us, length us, event | category | flops | bytes accessed | tf_op | source)
XLA Modules:
  0.0 212.4 jit_solution(5389241387103612977)
XLA Ops:
  6.5 1.5 pad_maximum_fusion.2
  8.0 3.4 %collective-permute-start.6 = (bf16[256,1024]{1,0:T(8,128)(2,1)}, bf16[256,1024]{1,0:T(8,128)(2,1)}, u32[]{:S(2)}, u32[]{:S(2)}) collective-permute-start(bf16[256,1024]{1,0:T(8,128)(2,1)} %param.28), channel_id=1, source_target_pairs={{0,1},{1,2},{2,3},{3,0},{4,5},{5,6},{6,7},{7,4},{8,9},{9,10},{10,1... | collective-permute-start | bytes 1572872 | tf_op jit(solution)/shard_map/ppermute | solution.py:120
  11.4 4.6 %collective-permute-start.7 = (bf16[256,1024]{1,0:T(8,128)(2,1)}, bf16[256,1024]{1,0:T(8,128)(2,1)}, u32[]{:S(2)}, u32[]{:S(2)}) collective-permute-start(bf16[256,1024]{1,0:T(8,128)(2,1)} %param.28), channel_id=1, source_target_pairs={{0,2},{1,3},{2,0},{3,1},{4,6},{5,7},{6,4},{7,5},{8,10},{9,11},{10,... | collective-permute-start | bytes 1572872 | tf_op jit(solution)/shard_map/ppermute | solution.py:120
  26.1 17.4 %all-to-all-start = ((bf16[128,2,576]{2,1,0:T(2,128)(2,1)}), bf16[128,2,576]{2,1,0:T(2,128)(2,1)S(1)}, u32[]{:S(2)}, u32[]{:S(2)}) async-start(bf16[128,2,576]{2,1,0:T(2,128)(2,1)} %reshape.445), calls=%async_computation | async-start | bytes 655360 | tf_op jit(solution)/shard_map/all_to_all | solution.py:148
  45.0 14.8 %all-to-all-done = bf16[128,2,576]{2,1,0:T(2,128)(2,1)S(1)} async-done(((bf16[128,2,576]{2,1,0:T(2,128)(2,1)}), bf16[128,2,576]{2,1,0:T(2,128)(2,1)S(1)}, u32[]{:S(2)}, u32[]{:S(2)}) %all-to-all-start) | async-done | bytes 294944 | tf_op jit(solution)/shard_map/all_to_all | solution.py:148
  63.2 5.9 %all-to-all-start.1 = ((bf16[128,2,576]{2,1,0:T(2,128)(2,1)}), bf16[128,2,576]{2,1,0:T(2,128)(2,1)S(1)}, u32[]{:S(2)}, u32[]{:S(2)}) async-start(bf16[128,2,576]{2,1,0:T(2,128)(2,1)} %reshape.447), calls=%async_computation.1 | async-start | bytes 655360 | tf_op jit(solution)/shard_map/all_to_all | solution.py:150
  73.4 13.3 %all-to-all-done.1 = bf16[128,2,576]{2,1,0:T(2,128)(2,1)S(1)} async-done(((bf16[128,2,576]{2,1,0:T(2,128)(2,1)}), bf16[128,2,576]{2,1,0:T(2,128)(2,1)S(1)}, u32[]{:S(2)}, u32[]{:S(2)}) %all-to-all-start.1) | async-done | bytes 294944 | tf_op jit(solution)/shard_map/all_to_all | solution.py:150
  87.8 1.9 collective-permute-start
  89.8 4.7 %collective-permute-start.1 = (bf16[144,256]{1,0:T(8,128)(2,1)S(1)}, bf16[144,256]{1,0:T(8,128)(2,1)S(1)}, u32[]{:S(2)}, u32[]{:S(2)}) collective-permute-start(bf16[144,256]{1,0:T(8,128)(2,1)S(1)} %get-tuple-element.42), channel_id=1, source_target_pairs={{0,2},{1,3},{2,0},{3,1},{4,6},{5,7},{6,4},{7,5},{8,10},{9,11},{10,... | collective-permute-start | bytes 221192 | tf_op jit(solution)/shard_map/ppermute | solution.py:120
  94.5 2.4 %collective-permute-start.2 = (bf16[144,256]{1,0:T(8,128)(2,1)S(1)}, bf16[144,256]{1,0:T(8,128)(2,1)S(1)}, u32[]{:S(2)}, u32[]{:S(2)}) collective-permute-start(bf16[144,256]{1,0:T(8,128)(2,1)S(1)} %get-tuple-element.42), channel_id=1, source_target_pairs={{0,3},{1,0},{2,1},{3,2},{4,7},{5,4},{6,5},{7,6},{8,11},{9,8},{10,9... | collective-permute-start | bytes 221192 | tf_op jit(solution)/shard_map/ppermute | solution.py:120
  100.5 1.4 scatter_custom_fusion.2
  103.7 2.9 %collective-permute-start.8 = (bf16[256,1024]{1,0:T(8,128)(2,1)}, bf16[256,1024]{1,0:T(8,128)(2,1)}, u32[]{:S(2)}, u32[]{:S(2)}) collective-permute-start(bf16[256,1024]{1,0:T(8,128)(2,1)} %param.28), channel_id=1, source_target_pairs={{0,3},{1,0},{2,1},{3,2},{4,7},{5,4},{6,5},{7,6},{8,11},{9,8},{10,9... | collective-permute-start | bytes 1572872 | tf_op jit(solution)/shard_map/ppermute | solution.py:120
  108.1 2.8 %gather_fusion.2 = bf16[32,32,512]{2,1,0:T(8,128)(2,1)S(1)} fusion(bf16[128,32,512]{2,1,0:T(8,128)(2,1)} %all-gather.2.cloned.1.call-done, s32[1024]{0:T(1024)S(1)} %pad_clamp_fusion.1), kind=kCustom, calls=%fused_computation.2 | custom fusion | bytes 2097280 | tf_op jit(solution)/shard_map/jit(_take)/gather | solution.py:161
  112.0 1.4 reshape_reshape.7
  113.4 1.9 multiply_reduce_fusion
  116.4 2.8 %reshape_reshape.6 = bf16[1024,4,64]{2,1,0:T(4,128)(2,1)} reshape(bf16[32,32,256]{2,1,0:T(8,128)(2,1)} %get-tuple-element.34) | data formatting | bytes 1048576 | tf_op jit(solution)/shard_map/reshape;reshape | solution.py:31
  119.9 2.1 fusion.33
  122.2 3.1 %collective-permute-start.3 = (bf16[128,256]{0,1:T(8,128)(2,1)S(1)}, bf16[128,256]{0,1:T(8,128)(2,1)S(1)}, u32[]{:S(2)}, u32[]{:S(2)}) collective-permute-start(bf16[128,256]{0,1:T(8,128)(2,1)S(1)} %bitcast.147), channel_id=1, source_target_pairs={{0,1},{1,2},{2,3},{3,0},{4,5},{5,6},{6,7},{7,4},{8,9},{9,10},{10,1... | collective-permute-start | bytes 196616 | tf_op jit(solution)/shard_map/ppermute | solution.py:120
  125.3 4.8 %collective-permute-start.4 = (bf16[128,256]{0,1:T(8,128)(2,1)S(1)}, bf16[128,256]{0,1:T(8,128)(2,1)S(1)}, u32[]{:S(2)}, u32[]{:S(2)}) collective-permute-start(bf16[128,256]{0,1:T(8,128)(2,1)S(1)} %bitcast.148), channel_id=1, source_target_pairs={{0,2},{1,3},{2,0},{3,1},{4,6},{5,7},{6,4},{7,5},{8,10},{9,11},{10,... | collective-permute-start | bytes 196616 | tf_op jit(solution)/shard_map/ppermute | solution.py:120
  130.1 3.2 %collective-permute-start.5 = (bf16[128,256]{0,1:T(8,128)(2,1)S(1)}, bf16[128,256]{0,1:T(8,128)(2,1)S(1)}, u32[]{:S(2)}, u32[]{:S(2)}) collective-permute-start(bf16[128,256]{0,1:T(8,128)(2,1)S(1)} %bitcast.149), channel_id=1, source_target_pairs={{0,3},{1,0},{2,1},{3,2},{4,7},{5,4},{6,5},{7,6},{8,11},{9,8},{10,9... | collective-permute-start | bytes 196616 | tf_op jit(solution)/shard_map/ppermute | solution.py:120
  133.5 2.8 %collective-permute-done.5 = bf16[128,256]{0,1:T(8,128)(2,1)S(1)} collective-permute-done((bf16[128,256]{0,1:T(8,128)(2,1)S(1)}, bf16[128,256]{0,1:T(8,128)(2,1)S(1)}, u32[]{:S(2)}, u32[]{:S(2)}) %collective-permute-start.5) | collective-permute-done | bytes 65568 | tf_op jit(solution)/shard_map/ppermute | solution.py:120
  136.3 2.1 multiply_reduce_fusion.1
  141.6 4.5 %all-to-all-start.2 = ((bf16[16,16,1024]{2,1,0:T(8,128)(2,1)}), bf16[16,16,1024]{2,1,0:T(8,128)(2,1)}, u32[]{:S(2)}, u32[]{:S(2)}) async-start(bf16[16,16,1024]{2,1,0:T(8,128)(2,1)} %broadcast_select_fusion.1), calls=%async_computation.2 | async-start | bytes 1048576 | tf_op jit(solution)/shard_map/all_to_all | solution.py:198
  146.1 3.1 %dot_general.37 = bf16[4,256,704]{1,0,2:T(4,128)(2,1)S(1)} reshape(bf16[1,1024,704]{1,2,0:T(8,128)(2,1)} %param.34) | data formatting | bytes 2883584 | tf_op jit(solution)/shard_map/snf,df->snd/dot_general | solution.py:202
  149.2 16.3 %all-to-all-done.2 = bf16[16,16,1024]{2,1,0:T(8,128)(2,1)} async-done(((bf16[16,16,1024]{2,1,0:T(8,128)(2,1)}), bf16[16,16,1024]{2,1,0:T(8,128)(2,1)}, u32[]{:S(2)}, u32[]{:S(2)}) %all-to-all-start.2) | async-done | bytes 524320 | tf_op jit(solution)/shard_map/all_to_all | solution.py:198
  165.5 3.2 %fusion.45 = f32[16,16,704]{2,1,0:T(8,128)} fusion(bf16[16,16,1024]{2,1,0:T(8,128)(2,1)} %all-to-all-done.2, bf16[1,1024,704]{1,2,0:T(8,128)(2,1)} %param.32), kind=kOutput, calls=%fused_computation.49 | convolution fusion | flops 370540544 | bytes 2686976 | tf_op jit(solution)/shard_map/snd,df->snf/dot_general | solution.py:199
  168.6 3.5 %fusion.19 = bf16[16,16,4,256]{3,1,2,0:T(8,128)(2,1)} fusion(bf16[4,256,704]{1,0,2:T(4,128)(2,1)S(1)} %dot_general.37, f32[16,16,704]{2,1,0:T(8,128)} %fusion.45, bf16[16,16,1024]{2,1,0:T(8,128)(2,1)} %all-to-all-done.2, bf16[1,1024,704]{1,2,0:T(8,128)(2,1)S(1)} %copy-done), kind=kOutput, calls=%fused_computation.29 | convolution fusion | flops 738820096 | bytes 4653056 | tf_op jit(solution)/shard_map/snf,df->snd/dot_general | solution.py:202
  172.1 8.0 %all-to-all-start.3 = ((bf16[64,16,256]{2,1,0:T(8,128)(2,1)}), bf16[64,16,256]{2,1,0:T(8,128)(2,1)S(1)}, u32[]{:S(2)}, u32[]{:S(2)}) async-start(bf16[64,16,256]{2,1,0:T(8,128)(2,1)} %bitcast.135), calls=%async_computation.3 | async-start | bytes 1048576 | tf_op jit(solution)/shard_map/all_to_all | solution.py:209
  181.3 2.0 gather_fusion.5
  183.6 18.2 %all-to-all-done.3 = bf16[64,16,256]{2,1,0:T(8,128)(2,1)S(1)} async-done(((bf16[64,16,256]{2,1,0:T(8,128)(2,1)}), bf16[64,16,256]{2,1,0:T(8,128)(2,1)S(1)}, u32[]{:S(2)}, u32[]{:S(2)}) %all-to-all-start.3) | async-done | bytes 524320 | tf_op jit(solution)/shard_map/all_to_all | solution.py:209
  201.8 1.7 gather_fusion.4
  203.9 1.7 fusion.63
  (139 shorter events, 30.7 us)
Async XLA Ops:
  6.5 162.1 %copy-start = (bf16[1,1024,704]{1,2,0:T(8,128)(2,1)S(1)}, bf16[1,1024,704]{1,2,0:T(8,128)(2,1)}, u32[]{:S(2)}) copy-start(bf16[1,1024,704]{1,2,0:T(8,128)(2,1)} %param.33) | copy-start | bytes 4325380
  6.5 37.0 %copy-start.9 = (s32[128]{0:T(128)S(1)}, s32[128]{0:T(128)}, u32[]{:S(2)}) copy-start(s32[128]{0:T(128)} %param.27) | copy-start | bytes 1540
  6.5 37.2 %copy-start.14 = (s32[128]{0:T(128)S(1)}, s32[128]{0:T(128)}, u32[]{:S(2)}) copy-start(s32[128]{0:T(128)} %param.35) | copy-start | bytes 1540
  6.5 101.5 %all-gather.2.cloned.1.call-start = ((), (), s32[]{:S(2)}) async-start(), calls=%async_computation.4 | async-start | bytes 4227072 | tf_op jit(solution)/shard_map/all_gather | solution.py:140
  8.0 122.1 %collective-permute-start.6 = (bf16[256,1024]{1,0:T(8,128)(2,1)}, bf16[256,1024]{1,0:T(8,128)(2,1)}, u32[]{:S(2)}, u32[]{:S(2)}) collective-permute-start(bf16[256,1024]{1,0:T(8,128)(2,1)} %param.28), channel_id=1, source_target_pairs={{0,1},{1,2},{2,3},{3,0},{4,5},{5,6},{6,7},{7,4},{8,9},{9,10},{10,1... | collective-permute-start | bytes 1572872 | tf_op jit(solution)/shard_map/ppermute | solution.py:120
  11.4 122.0 %collective-permute-start.7 = (bf16[256,1024]{1,0:T(8,128)(2,1)}, bf16[256,1024]{1,0:T(8,128)(2,1)}, u32[]{:S(2)}, u32[]{:S(2)}) collective-permute-start(bf16[256,1024]{1,0:T(8,128)(2,1)} %param.28), channel_id=1, source_target_pairs={{0,2},{1,3},{2,0},{3,1},{4,6},{5,7},{6,4},{7,5},{8,10},{9,11},{10,... | collective-permute-start | bytes 1572872 | tf_op jit(solution)/shard_map/ppermute | solution.py:120
  26.1 33.7 %all-to-all-start = ((bf16[128,2,576]{2,1,0:T(2,128)(2,1)}), bf16[128,2,576]{2,1,0:T(2,128)(2,1)S(1)}, u32[]{:S(2)}, u32[]{:S(2)}) async-start(bf16[128,2,576]{2,1,0:T(2,128)(2,1)} %reshape.445), calls=%async_computation | async-start | bytes 655360 | tf_op jit(solution)/shard_map/all_to_all | solution.py:148
  61.3 26.5 %copy-start.7 = (bf16[256,16]{0,1:T(8,128)(2,1)S(1)}, bf16[256,16]{0,1:T(8,128)(2,1)}, u32[]{:S(2)}) copy-start(bf16[256,16]{0,1:T(8,128)(2,1)} %param.30) | copy-start | bytes 24580
  63.2 23.5 %all-to-all-start.1 = ((bf16[128,2,576]{2,1,0:T(2,128)(2,1)}), bf16[128,2,576]{2,1,0:T(2,128)(2,1)S(1)}, u32[]{:S(2)}, u32[]{:S(2)}) async-start(bf16[128,2,576]{2,1,0:T(2,128)(2,1)} %reshape.447), calls=%async_computation.1 | async-start | bytes 655360 | tf_op jit(solution)/shard_map/all_to_all | solution.py:150
  87.8 15.8 %collective-permute-start = (bf16[144,256]{1,0:T(8,128)(2,1)S(1)}, bf16[144,256]{1,0:T(8,128)(2,1)S(1)}, u32[]{:S(2)}, u32[]{:S(2)}) collective-permute-start(bf16[144,256]{1,0:T(8,128)(2,1)S(1)} %get-tuple-element.42), channel_id=1, source_target_pairs={{0,1},{1,2},{2,3},{3,0},{4,5},{5,6},{6,7},{7,4},{8,9},{9,10},{10,1... | collective-permute-start | bytes 221192 | tf_op jit(solution)/shard_map/ppermute | solution.py:120
  89.8 16.8 %collective-permute-start.1 = (bf16[144,256]{1,0:T(8,128)(2,1)S(1)}, bf16[144,256]{1,0:T(8,128)(2,1)S(1)}, u32[]{:S(2)}, u32[]{:S(2)}) collective-permute-start(bf16[144,256]{1,0:T(8,128)(2,1)S(1)} %get-tuple-element.42), channel_id=1, source_target_pairs={{0,2},{1,3},{2,0},{3,1},{4,6},{5,7},{6,4},{7,5},{8,10},{9,11},{10,... | collective-permute-start | bytes 221192 | tf_op jit(solution)/shard_map/ppermute | solution.py:120
  94.5 12.1 %collective-permute-start.2 = (bf16[144,256]{1,0:T(8,128)(2,1)S(1)}, bf16[144,256]{1,0:T(8,128)(2,1)S(1)}, u32[]{:S(2)}, u32[]{:S(2)}) collective-permute-start(bf16[144,256]{1,0:T(8,128)(2,1)S(1)} %get-tuple-element.42), channel_id=1, source_target_pairs={{0,3},{1,0},{2,1},{3,2},{4,7},{5,4},{6,5},{7,6},{8,11},{9,8},{10,9... | collective-permute-start | bytes 221192 | tf_op jit(solution)/shard_map/ppermute | solution.py:120
  96.9 0.5 copy-start.10
  98.1 8.5 %copy-start.5 = (bf16[128,256]{0,1:T(8,128)(2,1)}, bf16[128,256]{0,1:T(8,128)(2,1)S(1)}, u32[]{:S(2)}) copy-start(bf16[128,256]{0,1:T(8,128)(2,1)S(1)} %copy.72) | copy-start | bytes 196612
  102.0 6.1 %copy-start.12 = (pred[128]{0:T(512)(128)(4,1)}, pred[128]{0:T(512)(128)(4,1)S(1)}, u32[]{:S(2)}) copy-start(pred[128]{0:T(512)(128)(4,1)S(1)} %iota_compare_fusion.4) | copy-start | bytes 388
  103.7 29.8 %collective-permute-start.8 = (bf16[256,1024]{1,0:T(8,128)(2,1)}, bf16[256,1024]{1,0:T(8,128)(2,1)}, u32[]{:S(2)}, u32[]{:S(2)}) collective-permute-start(bf16[256,1024]{1,0:T(8,128)(2,1)} %param.28), channel_id=1, source_target_pairs={{0,3},{1,0},{2,1},{3,2},{4,7},{5,4},{6,5},{7,6},{8,11},{9,8},{10,9... | collective-permute-start | bytes 1572872 | tf_op jit(solution)/shard_map/ppermute | solution.py:120
  113.4 1.9 copy-start.2
  119.9 2.1 copy-start.3
  119.9 2.1 %copy-start.6 = (bf16[128,256]{0,1:T(8,128)(2,1)S(1)}, bf16[128,256]{0,1:T(8,128)(2,1)}, u32[]{:S(2)}) copy-start(bf16[128,256]{0,1:T(8,128)(2,1)} %copy.76) | copy-start | bytes 196612
  119.9 13.5 %copy-start.1 = (bf16[144,4,256]{2,0,1:T(8,128)(2,1)S(1)}, bf16[144,4,256]{2,0,1:T(8,128)(2,1)}, u32[]{:S(2)}) copy-start(bf16[144,4,256]{2,0,1:T(8,128)(2,1)} %select_bitcast_fusion) | copy-start | bytes 884740
  122.2 11.3 %collective-permute-start.3 = (bf16[128,256]{0,1:T(8,128)(2,1)S(1)}, bf16[128,256]{0,1:T(8,128)(2,1)S(1)}, u32[]{:S(2)}, u32[]{:S(2)}) collective-permute-start(bf16[128,256]{0,1:T(8,128)(2,1)S(1)} %bitcast.147), channel_id=1, source_target_pairs={{0,1},{1,2},{2,3},{3,0},{4,5},{5,6},{6,7},{7,4},{8,9},{9,10},{10,1... | collective-permute-start | bytes 196616 | tf_op jit(solution)/shard_map/ppermute | solution.py:120
  125.3 8.2 %collective-permute-start.4 = (bf16[128,256]{0,1:T(8,128)(2,1)S(1)}, bf16[128,256]{0,1:T(8,128)(2,1)S(1)}, u32[]{:S(2)}, u32[]{:S(2)}) collective-permute-start(bf16[128,256]{0,1:T(8,128)(2,1)S(1)} %bitcast.148), channel_id=1, source_target_pairs={{0,2},{1,3},{2,0},{3,1},{4,6},{5,7},{6,4},{7,5},{8,10},{9,11},{10,... | collective-permute-start | bytes 196616 | tf_op jit(solution)/shard_map/ppermute | solution.py:120
  130.1 6.2 %collective-permute-start.5 = (bf16[128,256]{0,1:T(8,128)(2,1)S(1)}, bf16[128,256]{0,1:T(8,128)(2,1)S(1)}, u32[]{:S(2)}, u32[]{:S(2)}) collective-permute-start(bf16[128,256]{0,1:T(8,128)(2,1)S(1)} %bitcast.149), channel_id=1, source_target_pairs={{0,3},{1,0},{2,1},{3,2},{4,7},{5,4},{6,5},{7,6},{8,11},{9,8},{10,9... | collective-permute-start | bytes 196616 | tf_op jit(solution)/shard_map/ppermute | solution.py:120
  136.3 2.9 %copy-start.8 = (f32[1024]{0:T(1024)S(1)}, f32[1024]{0:T(1024)}, u32[]{:S(2)}) copy-start(f32[1024]{0:T(1024)} %param.29) | copy-start | bytes 12292
  138.4 0.8 copy-start.4
  141.6 23.9 %all-to-all-start.2 = ((bf16[16,16,1024]{2,1,0:T(8,128)(2,1)}), bf16[16,16,1024]{2,1,0:T(8,128)(2,1)}, u32[]{:S(2)}, u32[]{:S(2)}) async-start(bf16[16,16,1024]{2,1,0:T(8,128)(2,1)} %broadcast_select_fusion.1), calls=%async_computation.2 | async-start | bytes 1048576 | tf_op jit(solution)/shard_map/all_to_all | solution.py:198
  168.6 11.5 %copy-start.11 = (bf16[128,2]{0,1:T(2,128)(2,1)S(1)}, bf16[128,2]{0,1:T(2,128)(2,1)}, u32[]{:S(2)}) copy-start(bf16[128,2]{0,1:T(2,128)(2,1)} %copy-done.10) | copy-start | bytes 1540
  172.1 29.7 %all-to-all-start.3 = ((bf16[64,16,256]{2,1,0:T(8,128)(2,1)}), bf16[64,16,256]{2,1,0:T(8,128)(2,1)S(1)}, u32[]{:S(2)}, u32[]{:S(2)}) async-start(bf16[64,16,256]{2,1,0:T(8,128)(2,1)} %bitcast.135), calls=%async_computation.3 | async-start | bytes 1048576 | tf_op jit(solution)/shard_map/all_to_all | solution.py:209
  183.3 20.5 %copy-start.13 = (pred[128]{0:T(512)(128)(4,1)S(1)}, pred[128]{0:T(512)(128)(4,1)}, u32[]{:S(2)}) copy-start(pred[128]{0:T(512)(128)(4,1)} %copy-done.12) | copy-start | bytes 388
Sparse Core Ops, SparseCore 0:
  10.5 93.8 all-gather.1

commit v5 on v4

--- a/solution.py
+++ b/solution.py
@@ -171,7 +171,11 @@
     full_side = jnp.transpose(side_blocks, (1, 0, 2)).reshape(side.shape[0], head_count * features)
     full_hidden = full_side[:row_count]
     full_router = full_side[row_count:].T
-    rotated_attended = jnp.concatenate([attended] + head_ring(attended), axis=1)
+    spread_attended = jnp.broadcast_to(attended[None], (head_count,) + attended.shape)
+    by_source = lax.all_to_all(spread_attended, "head", split_axis=0, concat_axis=0, tiled=True)
+    rotated_attended = jnp.transpose(jnp.take(by_source, source_head, axis=0), (1, 0, 2)).reshape(
+        row_count, head_count * features
+    )
     resid = full_hidden.astype(jnp.float32) + jnp.dot(
         rotated_attended, rotated_weight, preferred_element_type=jnp.float32
     )

time: 214 us -> 211 us (0.986)
  starting transfers between devices: 66.8 us -> 59.3 us
  waiting for transfers between devices: 65.4 us -> 69.6 us
    ppermute x9 -> x6, starting transfers between devices: 31.1 us -> 20 us  [head_ring(): lax.ppermute(block, 'head', [(source, (source + shift) % head_count) for...]
    all_to_all x0 -> x1, waiting for transfers between devices: none -> 6.58 us  [on_device(): lax.all_to_all(spread_attended, 'head', split_axis=0, concat_axis=0, tile...]
    all_to_all x0 -> x1, starting transfers between devices: none -> 4.04 us  [on_device(): lax.all_to_all(spread_attended, 'head', split_axis=0, concat_axis=0, tile...]
    ppermute x9 -> x6, waiting for transfers between devices: 2.8 us -> 0.02 us  [head_ring(): lax.ppermute(block, 'head', [(source, (source + shift) % head_count) for...]
    unnamed x42 -> x48, local copies, waits for them, and re-layouts: 8.78 us -> 8.05 us
  transfers between devices with their start and end apart: 14 -> 12, of which waited for: 5 -> 5; matrix products, arithmetic and copies ran while one was open for 21% -> 21% of each run, Pallas kernels for 0% -> 0%
where the time goes in v5:
time: 211 us; the launch traced here: 210 us
  waiting for transfers between devices  69.6 us (33%)
  starting transfers between devices  59.3 us (28%)
  local copies, waits for them, and re-layouts  35.1 us (17%)
  between operations  18.7 us (9%)
  matrix products  13.9 us (7%)
  other arithmetic  13.5 us (6%)
    ppermute x6, starting transfers between devices, head_ring(): lax.ppermute(block, 'head', [(source, (source + shift) % head_count) for...  20 us
    all_to_all x1, waiting for transfers between devices, on_device(): lax.all_to_all(send_rows, 'ex', split_axis=0, concat_axis=0, tiled=True)  17.9 us
    all_to_all x1, starting transfers between devices, on_device(): lax.all_to_all(pieces, SEQ, split_axis=0, concat_axis=0, tiled=True)  17.4 us
    all_to_all x1, waiting for transfers between devices, on_device(): lax.all_to_all(split_part, ('ex', 'head'), split_axis=0, concat_axis=0, t...  17 us
    all_to_all x1, waiting for transfers between devices, on_device(): lax.all_to_all(pieces, SEQ, split_axis=0, concat_axis=0, tiled=True)  14.8 us
    all_to_all x1, waiting for transfers between devices, on_device(): lax.all_to_all(spread, SEQ, split_axis=0, concat_axis=0, tiled=True)  13.2 us
    unnamed x48, local copies, waits for them, and re-layouts  8.05 us
    all_to_all x1, starting transfers between devices, on_device(): lax.all_to_all(split_part, ('ex', 'head'), split_axis=0, concat_axis=0, t...  7.23 us
  transfers between devices with their start and end apart: 12, of which 5 were waited for; matrix products, arithmetic and copies ran while one was open for 21% of the time, Pallas kernels for 0%

profile of v5, /device:TPU:8, one launch (start us, length us, event | category | flops | bytes accessed | tf_op | source)
XLA Modules:
  0.0 210.2 jit_solution(11494283338524089561)
XLA Ops:
  6.5 1.5 pad_maximum_fusion.2
  8.0 3.4 %collective-permute-start.3 = (bf16[256,1024]{1,0:T(8,128)(2,1)}, bf16[256,1024]{1,0:T(8,128)(2,1)}, u32[]{:S(2)}, u32[]{:S(2)}) collective-permute-start(bf16[256,1024]{1,0:T(8,128)(2,1)} %param.28), channel_id=1, source_target_pairs={{0,1},{1,2},{2,3},{3,0},{4,5},{5,6},{6,7},{7,4},{8,9},{9,10},{10,1... | collective-permute-start | bytes 1572872 | tf_op jit(solution)/shard_map/ppermute | solution.py:120
  11.4 4.6 %collective-permute-start.4 = (bf16[256,1024]{1,0:T(8,128)(2,1)}, bf16[256,1024]{1,0:T(8,128)(2,1)}, u32[]{:S(2)}, u32[]{:S(2)}) collective-permute-start(bf16[256,1024]{1,0:T(8,128)(2,1)} %param.28), channel_id=1, source_target_pairs={{0,2},{1,3},{2,0},{3,1},{4,6},{5,7},{6,4},{7,5},{8,10},{9,11},{10,... | collective-permute-start | bytes 1572872 | tf_op jit(solution)/shard_map/ppermute | solution.py:120
  26.1 17.4 %all-to-all-start = ((bf16[128,2,576]{2,1,0:T(2,128)(2,1)}), bf16[128,2,576]{2,1,0:T(2,128)(2,1)S(1)}, u32[]{:S(2)}, u32[]{:S(2)}) async-start(bf16[128,2,576]{2,1,0:T(2,128)(2,1)} %reshape.462), calls=%async_computation | async-start | bytes 655360 | tf_op jit(solution)/shard_map/all_to_all | solution.py:148
  45.0 14.8 %all-to-all-done = bf16[128,2,576]{2,1,0:T(2,128)(2,1)S(1)} async-done(((bf16[128,2,576]{2,1,0:T(2,128)(2,1)}), bf16[128,2,576]{2,1,0:T(2,128)(2,1)S(1)}, u32[]{:S(2)}, u32[]{:S(2)}) %all-to-all-start) | async-done | bytes 294944 | tf_op jit(solution)/shard_map/all_to_all | solution.py:148
  63.2 5.9 %all-to-all-start.1 = ((bf16[128,2,576]{2,1,0:T(2,128)(2,1)}), bf16[128,2,576]{2,1,0:T(2,128)(2,1)S(1)}, u32[]{:S(2)}, u32[]{:S(2)}) async-start(bf16[128,2,576]{2,1,0:T(2,128)(2,1)} %reshape.464), calls=%async_computation.1 | async-start | bytes 655360 | tf_op jit(solution)/shard_map/all_to_all | solution.py:150
  73.5 13.2 %all-to-all-done.1 = bf16[128,2,576]{2,1,0:T(2,128)(2,1)S(1)} async-done(((bf16[128,2,576]{2,1,0:T(2,128)(2,1)}), bf16[128,2,576]{2,1,0:T(2,128)(2,1)S(1)}, u32[]{:S(2)}, u32[]{:S(2)}) %all-to-all-start.1) | async-done | bytes 294944 | tf_op jit(solution)/shard_map/all_to_all | solution.py:150
  87.9 1.9 collective-permute-start
  89.8 4.7 %collective-permute-start.1 = (bf16[144,256]{1,0:T(8,128)(2,1)S(1)}, bf16[144,256]{1,0:T(8,128)(2,1)S(1)}, u32[]{:S(2)}, u32[]{:S(2)}) collective-permute-start(bf16[144,256]{1,0:T(8,128)(2,1)S(1)} %get-tuple-element.42), channel_id=1, source_target_pairs={{0,2},{1,3},{2,0},{3,1},{4,6},{5,7},{6,4},{7,5},{8,10},{9,11},{10,... | collective-permute-start | bytes 221192 | tf_op jit(solution)/shard_map/ppermute | solution.py:120
  94.5 2.4 %collective-permute-start.2 = (bf16[144,256]{1,0:T(8,128)(2,1)S(1)}, bf16[144,256]{1,0:T(8,128)(2,1)S(1)}, u32[]{:S(2)}, u32[]{:S(2)}) collective-permute-start(bf16[144,256]{1,0:T(8,128)(2,1)S(1)} %get-tuple-element.42), channel_id=1, source_target_pairs={{0,3},{1,0},{2,1},{3,2},{4,7},{5,4},{6,5},{7,6},{8,11},{9,8},{10,9... | collective-permute-start | bytes 221192 | tf_op jit(solution)/shard_map/ppermute | solution.py:120
  100.6 1.4 scatter_custom_fusion.2
  103.8 2.9 %collective-permute-start.5 = (bf16[256,1024]{1,0:T(8,128)(2,1)}, bf16[256,1024]{1,0:T(8,128)(2,1)}, u32[]{:S(2)}, u32[]{:S(2)}) collective-permute-start(bf16[256,1024]{1,0:T(8,128)(2,1)} %param.28), channel_id=1, source_target_pairs={{0,3},{1,0},{2,1},{3,2},{4,7},{5,4},{6,5},{7,6},{8,11},{9,8},{10,9... | collective-permute-start | bytes 1572872 | tf_op jit(solution)/shard_map/ppermute | solution.py:120
  108.2 2.8 %gather_fusion.2 = bf16[32,32,512]{2,1,0:T(8,128)(2,1)S(1)} fusion(bf16[128,32,512]{2,1,0:T(8,128)(2,1)} %all-gather.2.cloned.1.call-done, s32[1024]{0:T(1024)S(1)} %pad_clamp_fusion.1), kind=kCustom, calls=%fused_computation.2 | custom fusion | bytes 2097280 | tf_op jit(solution)/shard_map/jit(_take)/gather | solution.py:161
  112.1 1.4 reshape_reshape.7
  113.5 1.9 multiply_reduce_fusion
  115.5 1.1 fusion.8
  116.6 2.8 %reshape_reshape.6 = bf16[1024,4,64]{2,1,0:T(4,128)(2,1)} reshape(bf16[32,32,256]{2,1,0:T(8,128)(2,1)} %get-tuple-element.34) | data formatting | bytes 1048576 | tf_op jit(solution)/shard_map/reshape;reshape | solution.py:31
  120.0 2.1 fusion.33
  123.2 4.0 %all-to-all-start.2 = ((bf16[4,128,256]{2,1,0:T(8,128)(2,1)}), bf16[4,128,256]{2,1,0:T(8,128)(2,1)S(1)}, u32[]{:S(2)}, u32[]{:S(2)}) async-start(bf16[4,128,256]{2,1,0:T(8,128)(2,1)} %broadcast_in_dim.130), calls=%async_computation.2 | async-start | bytes 524288 | tf_op jit(solution)/shard_map/all_to_all | solution.py:175
  127.3 6.6 %all-to-all-done.2 = bf16[4,128,256]{2,1,0:T(8,128)(2,1)S(1)} async-done(((bf16[4,128,256]{2,1,0:T(8,128)(2,1)}), bf16[4,128,256]{2,1,0:T(8,128)(2,1)S(1)}, u32[]{:S(2)}, u32[]{:S(2)}) %all-to-all-start.2) | async-done | bytes 262176 | tf_op jit(solution)/shard_map/all_to_all | solution.py:175
  134.9 2.1 multiply_reduce_fusion.1
  137.9 1.3 gather_fusion.4
  140.1 4.8 %all-to-all-start.3 = ((bf16[16,16,1024]{2,1,0:T(8,128)(2,1)}), bf16[16,16,1024]{2,1,0:T(8,128)(2,1)}, u32[]{:S(2)}, u32[]{:S(2)}) async-start(bf16[16,16,1024]{2,1,0:T(8,128)(2,1)} %broadcast_select_fusion.1), calls=%async_computation.3 | async-start | bytes 1048576 | tf_op jit(solution)/shard_map/all_to_all | solution.py:202
  145.0 3.1 %dot_general.37 = bf16[4,256,704]{1,0,2:T(4,128)(2,1)S(1)} reshape(bf16[1,1024,704]{1,2,0:T(8,128)(2,1)} %param.34) | data formatting | bytes 2883584 | tf_op jit(solution)/shard_map/snf,df->snd/dot_general | solution.py:206
  148.1 17.9 %all-to-all-done.3 = bf16[16,16,1024]{2,1,0:T(8,128)(2,1)} async-done(((bf16[16,16,1024]{2,1,0:T(8,128)(2,1)}), bf16[16,16,1024]{2,1,0:T(8,128)(2,1)}, u32[]{:S(2)}, u32[]{:S(2)}) %all-to-all-start.3) | async-done | bytes 524320 | tf_op jit(solution)/shard_map/all_to_all | solution.py:202
  166.0 3.2 %fusion.45 = f32[16,16,704]{2,1,0:T(8,128)} fusion(bf16[16,16,1024]{2,1,0:T(8,128)(2,1)} %all-to-all-done.3, bf16[1,1024,704]{1,2,0:T(8,128)(2,1)} %param.32), kind=kOutput, calls=%fused_computation.50 | convolution fusion | flops 370540544 | bytes 2686976 | tf_op jit(solution)/shard_map/snd,df->snf/dot_general | solution.py:203
  169.2 3.4 %fusion.19 = bf16[16,16,4,256]{3,1,2,0:T(8,128)(2,1)} fusion(bf16[4,256,704]{1,0,2:T(4,128)(2,1)S(1)} %dot_general.37, f32[16,16,704]{2,1,0:T(8,128)} %fusion.45, bf16[16,16,1024]{2,1,0:T(8,128)(2,1)} %all-to-all-done.3, bf16[1,1024,704]{1,2,0:T(8,128)(2,1)S(1)} %copy-done), kind=kOutput, calls=%fused_computation.30 | convolution fusion | flops 738820096 | bytes 4653056 | tf_op jit(solution)/shard_map/snf,df->snd/dot_general | solution.py:206
  172.6 7.2 %all-to-all-start.4 = ((bf16[64,16,256]{2,1,0:T(8,128)(2,1)}), bf16[64,16,256]{2,1,0:T(8,128)(2,1)S(1)}, u32[]{:S(2)}, u32[]{:S(2)}) async-start(bf16[64,16,256]{2,1,0:T(8,128)(2,1)} %bitcast.139), calls=%async_computation.4 | async-start | bytes 1048576 | tf_op jit(solution)/shard_map/all_to_all | solution.py:213
  180.3 2.0 gather_fusion.6
  182.6 17.0 %all-to-all-done.4 = bf16[64,16,256]{2,1,0:T(8,128)(2,1)S(1)} async-done(((bf16[64,16,256]{2,1,0:T(8,128)(2,1)}), bf16[64,16,256]{2,1,0:T(8,128)(2,1)S(1)}, u32[]{:S(2)}, u32[]{:S(2)}) %all-to-all-start.4) | async-done | bytes 524320 | tf_op jit(solution)/shard_map/all_to_all | solution.py:213
  199.6 1.7 gather_fusion.5
  201.6 1.7 fusion.56
  (146 shorter events, 29.4 us)
Async XLA Ops:
  6.5 162.6 %copy-start = (bf16[1,1024,704]{1,2,0:T(8,128)(2,1)S(1)}, bf16[1,1024,704]{1,2,0:T(8,128)(2,1)}, u32[]{:S(2)}) copy-start(bf16[1,1024,704]{1,2,0:T(8,128)(2,1)} %param.33) | copy-start | bytes 4325380
  6.5 37.0 %copy-start.10 = (s32[128]{0:T(128)S(1)}, s32[128]{0:T(128)}, u32[]{:S(2)}) copy-start(s32[128]{0:T(128)} %param.27) | copy-start | bytes 1540
  6.5 37.2 %copy-start.17 = (s32[128]{0:T(128)S(1)}, s32[128]{0:T(128)}, u32[]{:S(2)}) copy-start(s32[128]{0:T(128)} %param.35) | copy-start | bytes 1540
  6.5 101.7 %all-gather.2.cloned.1.call-start = ((), (), s32[]{:S(2)}) async-start(), calls=%async_computation.5 | async-start | bytes 4227072 | tf_op jit(solution)/shard_map/all_gather | solution.py:140
  8.0 126.9 %collective-permute-start.3 = (bf16[256,1024]{1,0:T(8,128)(2,1)}, bf16[256,1024]{1,0:T(8,128)(2,1)}, u32[]{:S(2)}, u32[]{:S(2)}) collective-permute-start(bf16[256,1024]{1,0:T(8,128)(2,1)} %param.28), channel_id=1, source_target_pairs={{0,1},{1,2},{2,3},{3,0},{4,5},{5,6},{6,7},{7,4},{8,9},{9,10},{10,1... | collective-permute-start | bytes 1572872 | tf_op jit(solution)/shard_map/ppermute | solution.py:120
  11.4 123.5 %collective-permute-start.4 = (bf16[256,1024]{1,0:T(8,128)(2,1)}, bf16[256,1024]{1,0:T(8,128)(2,1)}, u32[]{:S(2)}, u32[]{:S(2)}) collective-permute-start(bf16[256,1024]{1,0:T(8,128)(2,1)} %param.28), channel_id=1, source_target_pairs={{0,2},{1,3},{2,0},{3,1},{4,6},{5,7},{6,4},{7,5},{8,10},{9,11},{10,... | collective-permute-start | bytes 1572872 | tf_op jit(solution)/shard_map/ppermute | solution.py:120
  26.1 33.7 %all-to-all-start = ((bf16[128,2,576]{2,1,0:T(2,128)(2,1)}), bf16[128,2,576]{2,1,0:T(2,128)(2,1)S(1)}, u32[]{:S(2)}, u32[]{:S(2)}) async-start(bf16[128,2,576]{2,1,0:T(2,128)(2,1)} %reshape.462), calls=%async_computation | async-start | bytes 655360 | tf_op jit(solution)/shard_map/all_to_all | solution.py:148
  61.3 26.5 %copy-start.7 = (bf16[256,16]{0,1:T(8,128)(2,1)S(1)}, bf16[256,16]{0,1:T(8,128)(2,1)}, u32[]{:S(2)}) copy-start(bf16[256,16]{0,1:T(8,128)(2,1)} %param.30) | copy-start | bytes 24580
  63.2 23.5 %all-to-all-start.1 = ((bf16[128,2,576]{2,1,0:T(2,128)(2,1)}), bf16[128,2,576]{2,1,0:T(2,128)(2,1)S(1)}, u32[]{:S(2)}, u32[]{:S(2)}) async-start(bf16[128,2,576]{2,1,0:T(2,128)(2,1)} %reshape.464), calls=%async_computation.1 | async-start | bytes 655360 | tf_op jit(solution)/shard_map/all_to_all | solution.py:150
  73.3 34.1 %copy-start.15 = (pred[4]{0:T(512)(128)(4,1)}, pred[4]{0:T(512)(128)(4,1)S(1)}, u32[]{:S(2)}) copy-start(pred[4]{0:T(512)(128)(4,1)S(1)} %compare_and_fusion.2) | copy-start | bytes 16
  73.4 33.4 %copy-start.8 = (s32[1024]{0:T(1024)}, s32[1024]{0:T(1024)S(1)}, u32[]{:S(2)}) copy-start(s32[1024]{0:T(1024)S(1)} %pad_clamp_fusion.2) | copy-start | bytes 12292
  87.9 15.9 %collective-permute-start = (bf16[144,256]{1,0:T(8,128)(2,1)S(1)}, bf16[144,256]{1,0:T(8,128)(2,1)S(1)}, u32[]{:S(2)}, u32[]{:S(2)}) collective-permute-start(bf16[144,256]{1,0:T(8,128)(2,1)S(1)} %get-tuple-element.42), channel_id=1, source_target_pairs={{0,1},{1,2},{2,3},{3,0},{4,5},{5,6},{6,7},{7,4},{8,9},{9,10},{10,1... | collective-permute-start | bytes 221192 | tf_op jit(solution)/shard_map/ppermute | solution.py:120
  89.8 16.9 %collective-permute-start.1 = (bf16[144,256]{1,0:T(8,128)(2,1)S(1)}, bf16[144,256]{1,0:T(8,128)(2,1)S(1)}, u32[]{:S(2)}, u32[]{:S(2)}) collective-permute-start(bf16[144,256]{1,0:T(8,128)(2,1)S(1)} %get-tuple-element.42), channel_id=1, source_target_pairs={{0,2},{1,3},{2,0},{3,1},{4,6},{5,7},{6,4},{7,5},{8,10},{9,11},{10,... | collective-permute-start | bytes 221192 | tf_op jit(solution)/shard_map/ppermute | solution.py:120
  94.5 12.2 %collective-permute-start.2 = (bf16[144,256]{1,0:T(8,128)(2,1)S(1)}, bf16[144,256]{1,0:T(8,128)(2,1)S(1)}, u32[]{:S(2)}, u32[]{:S(2)}) collective-permute-start(bf16[144,256]{1,0:T(8,128)(2,1)S(1)} %get-tuple-element.42), channel_id=1, source_target_pairs={{0,3},{1,0},{2,1},{3,2},{4,7},{5,4},{6,5},{7,6},{8,11},{9,8},{10,9... | collective-permute-start | bytes 221192 | tf_op jit(solution)/shard_map/ppermute | solution.py:120
  97.0 0.6 copy-start.11
  98.2 8.6 %copy-start.5 = (bf16[128,256]{0,1:T(8,128)(2,1)}, bf16[128,256]{0,1:T(8,128)(2,1)S(1)}, u32[]{:S(2)}) copy-start(bf16[128,256]{0,1:T(8,128)(2,1)S(1)} %copy.93) | copy-start | bytes 196612
  102.1 6.1 %copy-start.13 = (pred[128]{0:T(512)(128)(4,1)}, pred[128]{0:T(512)(128)(4,1)S(1)}, u32[]{:S(2)}) copy-start(pred[128]{0:T(512)(128)(4,1)S(1)} %iota_compare_fusion.4) | copy-start | bytes 388
  103.8 31.1 %collective-permute-start.5 = (bf16[256,1024]{1,0:T(8,128)(2,1)}, bf16[256,1024]{1,0:T(8,128)(2,1)}, u32[]{:S(2)}, u32[]{:S(2)}) collective-permute-start(bf16[256,1024]{1,0:T(8,128)(2,1)} %param.28), channel_id=1, source_target_pairs={{0,3},{1,0},{2,1},{3,2},{4,7},{5,4},{6,5},{7,6},{8,11},{9,8},{10,9... | collective-permute-start | bytes 1572872 | tf_op jit(solution)/shard_map/ppermute | solution.py:120
  113.5 1.9 copy-start.2
  120.0 2.1 %copy-start.3 = (f32[4,128,128]{1,2,0:T(8,128)S(1)}, f32[4,128,128]{1,2,0:T(8,128)}, u32[]{:S(2)}) copy-start(f32[4,128,128]{1,2,0:T(8,128)} %get-tuple-element.50) | copy-start | bytes 786436
  120.0 2.1 %copy-start.6 = (bf16[128,256]{0,1:T(8,128)(2,1)S(1)}, bf16[128,256]{0,1:T(8,128)(2,1)}, u32[]{:S(2)}) copy-start(bf16[128,256]{0,1:T(8,128)(2,1)} %copy.97) | copy-start | bytes 196612
  122.1 5.1 %copy-start.1 = (bf16[144,4,256]{2,0,1:T(8,128)(2,1)S(1)}, bf16[144,4,256]{2,0,1:T(8,128)(2,1)}, u32[]{:S(2)}) copy-start(bf16[144,4,256]{2,0,1:T(8,128)(2,1)} %select_bitcast_fusion) | copy-start | bytes 884740
  122.2 12.4 %copy-start.16 = (pred[4]{0:T(512)(128)(4,1)S(1)}, pred[4]{0:T(512)(128)(4,1)}, u32[]{:S(2)}) copy-start(pred[4]{0:T(512)(128)(4,1)} %copy-done.15) | copy-start | bytes 16
  123.2 10.7 %all-to-all-start.2 = ((bf16[4,128,256]{2,1,0:T(8,128)(2,1)}), bf16[4,128,256]{2,1,0:T(8,128)(2,1)S(1)}, u32[]{:S(2)}, u32[]{:S(2)}) async-start(bf16[4,128,256]{2,1,0:T(8,128)(2,1)} %broadcast_in_dim.130), calls=%async_computation.2 | async-start | bytes 524288 | tf_op jit(solution)/shard_map/all_to_all | solution.py:175
  134.9 2.9 %copy-start.9 = (f32[1024]{0:T(1024)S(1)}, f32[1024]{0:T(1024)}, u32[]{:S(2)}) copy-start(f32[1024]{0:T(1024)} %param.29) | copy-start | bytes 12292
  137.0 0.8 copy-start.4
  140.1 25.9 %all-to-all-start.3 = ((bf16[16,16,1024]{2,1,0:T(8,128)(2,1)}), bf16[16,16,1024]{2,1,0:T(8,128)(2,1)}, u32[]{:S(2)}, u32[]{:S(2)}) async-start(bf16[16,16,1024]{2,1,0:T(8,128)(2,1)} %broadcast_select_fusion.1), calls=%async_computation.3 | async-start | bytes 1048576 | tf_op jit(solution)/shard_map/all_to_all | solution.py:202
  169.2 10.7 %copy-start.12 = (bf16[128,2]{0,1:T(2,128)(2,1)S(1)}, bf16[128,2]{0,1:T(2,128)(2,1)}, u32[]{:S(2)}) copy-start(bf16[128,2]{0,1:T(2,128)(2,1)} %copy-done.11) | copy-start | bytes 1540
  172.6 27.0 %all-to-all-start.4 = ((bf16[64,16,256]{2,1,0:T(8,128)(2,1)}), bf16[64,16,256]{2,1,0:T(8,128)(2,1)S(1)}, u32[]{:S(2)}, u32[]{:S(2)}) async-start(bf16[64,16,256]{2,1,0:T(8,128)(2,1)} %bitcast.139), calls=%async_computation.4 | async-start | bytes 1048576 | tf_op jit(solution)/shard_map/all_to_all | solution.py:213
  182.3 19.3 %copy-start.14 = (pred[128]{0:T(512)(128)(4,1)S(1)}, pred[128]{0:T(512)(128)(4,1)}, u32[]{:S(2)}) copy-start(pred[128]{0:T(512)(128)(4,1)} %copy-done.13) | copy-start | bytes 388
Sparse Core Ops, SparseCore 0:
  10.5 93.8 all-gather.1

commit v6 on v5

--- a/solution.py
+++ b/solution.py
@@ -24,30 +24,20 @@
 
 def attend_rows(query_rows, key_rows, value_rows, prefix_keys, prefix_values, length, head_total):
     row_count = query_rows.shape[0]
-    head_size = query_rows.shape[1] // head_total
+    features = query_rows.shape[1]
+    head_size = features // head_total
     scale = head_size ** (-0.5)
-
-    def heads_of(array):
-        return array.reshape(array.shape[0], head_total, head_size)
-
+    head_of_column = jnp.arange(features, dtype=jnp.int32) // head_size
+    own_head = head_of_column[None, :] == jnp.arange(head_total, dtype=jnp.int32)[:, None]
+    masked_queries = jnp.where(
+        own_head[:, None, :], query_rows[None], jnp.zeros_like(query_rows)[None]
+    ).reshape(head_total * row_count, features)
     prefix_scores = (
-        jnp.einsum(
-            "qhd,khd->hqk",
-            heads_of(query_rows),
-            heads_of(prefix_keys),
-            preferred_element_type=jnp.float32,
-        )
-        * scale
-    )
+        jnp.dot(masked_queries, prefix_keys.T, preferred_element_type=jnp.float32) * scale
+    ).reshape(head_total, row_count, -1)
     suffix_scores = (
-        jnp.einsum(
-            "qhd,khd->hqk",
-            heads_of(query_rows),
-            heads_of(key_rows),
-            preferred_element_type=jnp.float32,
-        )
-        * scale
-    )
+        jnp.dot(masked_queries, key_rows.T, preferred_element_type=jnp.float32) * scale
+    ).reshape(head_total, row_count, -1)
     query_pos = jnp.arange(row_count, dtype=jnp.int32)[:, None]
     key_pos = jnp.arange(row_count, dtype=jnp.int32)[None, :]
     allowed = (key_pos <= query_pos) & (key_pos < length)
@@ -60,13 +50,18 @@
     )
     prefix_probs = (prefix_exp / denominators).astype(jnp.bfloat16)
     suffix_probs = (suffix_exp / denominators).astype(jnp.bfloat16)
-    mixed_heads = jnp.einsum(
-        "hqk,khd->qhd", prefix_probs, heads_of(prefix_values), preferred_element_type=jnp.float32
-    )
-    mixed_heads = mixed_heads + jnp.einsum(
-        "hqk,khd->qhd", suffix_probs, heads_of(value_rows), preferred_element_type=jnp.float32
-    )
-    return mixed_heads.reshape(row_count, head_total * head_size).astype(jnp.bfloat16)
+    mixed = jnp.dot(
+        prefix_probs.reshape(head_total * row_count, -1),
+        prefix_values,
+        preferred_element_type=jnp.float32,
+    ) + jnp.dot(
+        suffix_probs.reshape(head_total * row_count, -1),
+        value_rows,
+        preferred_element_type=jnp.float32,
+    )
+    mixed = mixed.reshape(head_total, row_count, features)
+    picked = jnp.where(own_head[:, None, :], mixed, jnp.zeros_like(mixed))
+    return jnp.sum(picked, axis=0).astype(jnp.bfloat16)
 
 
 def slot_table(route_rows, replicas, per_device, experts):

time: 211 us -> 204 us (0.967)
  local copies, waits for them, and re-layouts: 35.1 us -> 28.7 us
  matrix products: 13.9 us -> 11.2 us
  other arithmetic: 13.5 us -> 11.3 us
    another operation x5 -> x3, local copies, waits for them, and re-layouts: 4.38 us -> 0.2 us  [the longest x2 4.19 us: heads_of(): return array.reshape(array.shape[0], head_total, head_size)]
    all_to_all x1, starting transfers between devices: 4.85 us -> 7.85 us  [on_device(): lax.all_to_all(send_rows, 'ex', split_axis=0, concat_axis=0, tiled=True)]
    dot_general x4, matrix products: 5.1 us -> 2.37 us  [the longest x1 0.94 us: attend_rows(): jnp.dot(masked_queries, key_rows.T, preferred_element_type=jnp.float32)]
    unnamed x48 -> x26, local copies, waits for them, and re-layouts: 8.05 us -> 7.76 us
  transfers between devices with their start and end apart: 12 -> 12, of which waited for: 5 -> 5; matrix products, arithmetic and copies ran while one was open for 21% -> 17% of each run, Pallas kernels for 0% -> 0%
where the time goes in v6:
time: 204 us; the launch traced here: 202 us
  waiting for transfers between devices  71.1 us (35%)
  starting transfers between devices  61.1 us (30%)
  local copies, waits for them, and re-layouts  28.7 us (14%)
  between operations  18.8 us (9%)
  other arithmetic  11.3 us (6%)
  matrix products  11.2 us (5%)
    ppermute x6, starting transfers between devices, head_ring(): lax.ppermute(block, 'head', [(source, (source + shift) % head_count) for...  20 us
    all_to_all x1, waiting for transfers between devices, on_device(): lax.all_to_all(send_rows, 'ex', split_axis=0, concat_axis=0, tiled=True)  18.7 us
    all_to_all x1, waiting for transfers between devices, on_device(): lax.all_to_all(split_part, ('ex', 'head'), split_axis=0, concat_axis=0, t...  18 us
    all_to_all x1, starting transfers between devices, on_device(): lax.all_to_all(pieces, SEQ, split_axis=0, concat_axis=0, tiled=True)  17.4 us
    all_to_all x1, waiting for transfers between devices, on_device(): lax.all_to_all(pieces, SEQ, split_axis=0, concat_axis=0, tiled=True)  14.8 us
    all_to_all x1, waiting for transfers between devices, on_device(): lax.all_to_all(spread, SEQ, split_axis=0, concat_axis=0, tiled=True)  13 us
    all_to_all x1, starting transfers between devices, on_device(): lax.all_to_all(send_rows, 'ex', split_axis=0, concat_axis=0, tiled=True)  7.85 us
    unnamed x26, local copies, waits for them, and re-layouts  7.76 us
  transfers between devices with their start and end apart: 12, of which 5 were waited for; matrix products, arithmetic and copies ran while one was open for 17% of the time, Pallas kernels for 0%

profile of v6, /device:TPU:8, one launch (start us, length us, event | category | flops | bytes accessed | tf_op | source)
XLA Modules:
  0.0 202.3 jit_solution(5439200362059518708)
XLA Ops:
  6.5 1.5 pad_maximum_fusion.2
  8.0 3.4 %collective-permute-start.3 = (bf16[256,1024]{1,0:T(8,128)(2,1)}, bf16[256,1024]{1,0:T(8,128)(2,1)}, u32[]{:S(2)}, u32[]{:S(2)}) collective-permute-start(bf16[256,1024]{1,0:T(8,128)(2,1)} %param.28), channel_id=1, source_target_pairs={{0,1},{1,2},{2,3},{3,0},{4,5},{5,6},{6,7},{7,4},{8,9},{9,10},{10,1... | collective-permute-start | bytes 1572872 | tf_op jit(solution)/shard_map/ppermute | solution.py:115
  11.4 4.6 %collective-permute-start.4 = (bf16[256,1024]{1,0:T(8,128)(2,1)}, bf16[256,1024]{1,0:T(8,128)(2,1)}, u32[]{:S(2)}, u32[]{:S(2)}) collective-permute-start(bf16[256,1024]{1,0:T(8,128)(2,1)} %param.28), channel_id=1, source_target_pairs={{0,2},{1,3},{2,0},{3,1},{4,6},{5,7},{6,4},{7,5},{8,10},{9,11},{10,... | collective-permute-start | bytes 1572872 | tf_op jit(solution)/shard_map/ppermute | solution.py:115
  25.3 1.1 reshape.535
  26.4 17.4 %all-to-all-start = ((bf16[128,2,576]{2,1,0:T(2,128)(2,1)}), bf16[128,2,576]{2,1,0:T(2,128)(2,1)S(1)}, u32[]{:S(2)}, u32[]{:S(2)}) async-start(bf16[128,2,576]{2,1,0:T(2,128)(2,1)} %reshape.535), calls=%async_computation | async-start | bytes 655360 | tf_op jit(solution)/shard_map/all_to_all | solution.py:143
  43.8 1.0 scatter_custom_fusion
  45.3 14.8 %all-to-all-done = bf16[128,2,576]{2,1,0:T(2,128)(2,1)S(1)} async-done(((bf16[128,2,576]{2,1,0:T(2,128)(2,1)}), bf16[128,2,576]{2,1,0:T(2,128)(2,1)S(1)}, u32[]{:S(2)}, u32[]{:S(2)}) %all-to-all-start) | async-done | bytes 294944 | tf_op jit(solution)/shard_map/all_to_all | solution.py:143
  62.5 1.1 reshape.537
  63.5 5.8 %all-to-all-start.1 = ((bf16[128,2,576]{2,1,0:T(2,128)(2,1)}), bf16[128,2,576]{2,1,0:T(2,128)(2,1)S(1)}, u32[]{:S(2)}, u32[]{:S(2)}) async-start(bf16[128,2,576]{2,1,0:T(2,128)(2,1)} %reshape.537), calls=%async_computation.1 | async-start | bytes 655360 | tf_op jit(solution)/shard_map/all_to_all | solution.py:145
  72.9 1.0 scatter_custom_fusion.1
  74.0 13.0 %all-to-all-done.1 = bf16[128,2,576]{2,1,0:T(2,128)(2,1)S(1)} async-done(((bf16[128,2,576]{2,1,0:T(2,128)(2,1)}), bf16[128,2,576]{2,1,0:T(2,128)(2,1)S(1)}, u32[]{:S(2)}, u32[]{:S(2)}) %all-to-all-start.1) | async-done | bytes 294944 | tf_op jit(solution)/shard_map/all_to_all | solution.py:145
  88.2 1.9 collective-permute-start
  90.1 4.5 %collective-permute-start.1 = (bf16[144,256]{1,0:T(8,128)(2,1)S(1)}, bf16[144,256]{1,0:T(8,128)(2,1)S(1)}, u32[]{:S(2)}, u32[]{:S(2)}) collective-permute-start(bf16[144,256]{1,0:T(8,128)(2,1)S(1)} %get-tuple-element.40), channel_id=1, source_target_pairs={{0,2},{1,3},{2,0},{3,1},{4,6},{5,7},{6,4},{7,5},{8,10},{9,11},{10,... | collective-permute-start | bytes 221192 | tf_op jit(solution)/shard_map/ppermute | solution.py:115
  94.7 2.5 %collective-permute-start.2 = (bf16[144,256]{1,0:T(8,128)(2,1)S(1)}, bf16[144,256]{1,0:T(8,128)(2,1)S(1)}, u32[]{:S(2)}, u32[]{:S(2)}) collective-permute-start(bf16[144,256]{1,0:T(8,128)(2,1)S(1)} %get-tuple-element.40), channel_id=1, source_target_pairs={{0,3},{1,0},{2,1},{3,2},{4,7},{5,4},{6,5},{7,6},{8,11},{9,8},{10,9... | collective-permute-start | bytes 221192 | tf_op jit(solution)/shard_map/ppermute | solution.py:115
  99.5 1.4 scatter_custom_fusion.2
  101.2 0.9 fusion.80
  102.1 2.9 %collective-permute-start.5 = (bf16[256,1024]{1,0:T(8,128)(2,1)}, bf16[256,1024]{1,0:T(8,128)(2,1)}, u32[]{:S(2)}, u32[]{:S(2)}) collective-permute-start(bf16[256,1024]{1,0:T(8,128)(2,1)} %param.28), channel_id=1, source_target_pairs={{0,3},{1,0},{2,1},{3,2},{4,7},{5,4},{6,5},{7,6},{8,11},{9,8},{10,9... | collective-permute-start | bytes 1572872 | tf_op jit(solution)/shard_map/ppermute | solution.py:115
  105.9 2.8 %gather_fusion.2 = bf16[32,32,512]{2,1,0:T(8,128)(2,1)S(1)} fusion(bf16[128,32,512]{2,1,0:T(8,128)(2,1)} %all-gather.2.cloned.1.call-done, s32[1024]{0:T(1024)S(1)} %pad_clamp_fusion.1), kind=kCustom, calls=%fused_computation.2 | custom fusion | bytes 2097280 | tf_op jit(solution)/shard_map/jit(_take)/gather | solution.py:156
  112.0 3.9 %all-to-all-start.2 = ((bf16[4,128,256]{2,1,0:T(8,128)(2,1)}), bf16[4,128,256]{2,1,0:T(8,128)(2,1)S(1)}, u32[]{:S(2)}, u32[]{:S(2)}) async-start(bf16[4,128,256]{2,1,0:T(8,128)(2,1)} %broadcast_in_dim.177), calls=%async_computation.2 | async-start | bytes 524288 | tf_op jit(solution)/shard_map/all_to_all | solution.py:170
  116.0 6.6 %all-to-all-done.2 = bf16[4,128,256]{2,1,0:T(8,128)(2,1)S(1)} async-done(((bf16[4,128,256]{2,1,0:T(8,128)(2,1)}), bf16[4,128,256]{2,1,0:T(8,128)(2,1)S(1)}, u32[]{:S(2)}, u32[]{:S(2)}) %all-to-all-start.2) | async-done | bytes 262176 | tf_op jit(solution)/shard_map/all_to_all | solution.py:170
  123.5 2.1 %multiply_reduce_fusion.1 = (f32[128]{0:T(128)S(1)}, f32[128,1024]{1,0:T(8,128)S(1)}) fusion(f32[128,1024]{1,0:T(8,128)S(1)} %bitcast.147, bf16[128,1024]{0,1:T(8,128)(2,1)S(1)} %bitcast.150, bf16[256,1024]{1,0:T(8,128)(2,1)} %collective-permute-done.5, bf16[256,1024]{1,0:T(8,128)(2,1)} %collective-permute-done.4, ...), kind=kOutput, calls=%fused_computation.49 | convolution fusion | flops 277217152 | bytes 3408384 | tf_op jit(solution)/shard_map/dot_general | solution.py:174
  126.5 1.2 gather_fusion.4
  128.6 7.9 %all-to-all-start.3 = ((bf16[16,16,1024]{2,1,0:T(8,128)(2,1)}), bf16[16,16,1024]{2,1,0:T(8,128)(2,1)}, u32[]{:S(2)}, u32[]{:S(2)}) async-start(bf16[16,16,1024]{2,1,0:T(8,128)(2,1)} %broadcast_select_fusion.1), calls=%async_computation.3 | async-start | bytes 1048576 | tf_op jit(solution)/shard_map/all_to_all | solution.py:197
  136.4 3.1 %dot_general.37 = bf16[4,256,704]{1,0,2:T(4,128)(2,1)S(1)} reshape(bf16[1,1024,704]{1,2,0:T(8,128)(2,1)} %param.34) | data formatting | bytes 2883584 | tf_op jit(solution)/shard_map/snf,df->snd/dot_general | solution.py:201
  139.5 18.7 %all-to-all-done.3 = bf16[16,16,1024]{2,1,0:T(8,128)(2,1)} async-done(((bf16[16,16,1024]{2,1,0:T(8,128)(2,1)}), bf16[16,16,1024]{2,1,0:T(8,128)(2,1)}, u32[]{:S(2)}, u32[]{:S(2)}) %all-to-all-start.3) | async-done | bytes 524320 | tf_op jit(solution)/shard_map/all_to_all | solution.py:197
  158.2 3.2 %fusion.40 = f32[16,16,704]{2,1,0:T(8,128)} fusion(bf16[16,16,1024]{2,1,0:T(8,128)(2,1)} %all-to-all-done.3, bf16[1,1024,704]{1,2,0:T(8,128)(2,1)} %param.32), kind=kOutput, calls=%fused_computation.45 | convolution fusion | flops 370540544 | bytes 2686976 | tf_op jit(solution)/shard_map/snd,df->snf/dot_general | solution.py:198
  161.4 3.4 %fusion.19 = bf16[16,16,4,256]{3,1,2,0:T(8,128)(2,1)} fusion(bf16[4,256,704]{1,0,2:T(4,128)(2,1)S(1)} %dot_general.37, f32[16,16,704]{2,1,0:T(8,128)} %fusion.40, bf16[16,16,1024]{2,1,0:T(8,128)(2,1)} %all-to-all-done.3, bf16[1,1024,704]{1,2,0:T(8,128)(2,1)S(1)} %copy-done), kind=kOutput, calls=%fused_computation.30 | convolution fusion | flops 738820096 | bytes 4653056 | tf_op jit(solution)/shard_map/snf,df->snd/dot_general | solution.py:201
  164.8 6.2 %all-to-all-start.4 = ((bf16[64,16,256]{2,1,0:T(8,128)(2,1)}), bf16[64,16,256]{2,1,0:T(8,128)(2,1)S(1)}, u32[]{:S(2)}, u32[]{:S(2)}) async-start(bf16[64,16,256]{2,1,0:T(8,128)(2,1)} %bitcast.146), calls=%async_computation.4 | async-start | bytes 1048576 | tf_op jit(solution)/shard_map/all_to_all | solution.py:208
  171.4 2.0 gather_fusion.6
  173.7 18.0 %all-to-all-done.4 = bf16[64,16,256]{2,1,0:T(8,128)(2,1)S(1)} async-done(((bf16[64,16,256]{2,1,0:T(8,128)(2,1)}), bf16[64,16,256]{2,1,0:T(8,128)(2,1)S(1)}, u32[]{:S(2)}, u32[]{:S(2)}) %all-to-all-start.4) | async-done | bytes 524320 | tf_op jit(solution)/shard_map/all_to_all | solution.py:208
  191.8 1.7 gather_fusion.5
  193.8 1.7 fusion.52
  (123 shorter events, 22.4 us)
Async XLA Ops:
  6.5 154.8 %copy-start = (bf16[1,1024,704]{1,2,0:T(8,128)(2,1)S(1)}, bf16[1,1024,704]{1,2,0:T(8,128)(2,1)}, u32[]{:S(2)}) copy-start(bf16[1,1024,704]{1,2,0:T(8,128)(2,1)} %param.33) | copy-start | bytes 4325380
  6.5 37.2 %copy-start.6 = (s32[128]{0:T(128)S(1)}, s32[128]{0:T(128)}, u32[]{:S(2)}) copy-start(s32[128]{0:T(128)} %param.35) | copy-start | bytes 1540
  6.5 38.3 %copy-start.5 = (s32[128]{0:T(128)S(1)}, s32[128]{0:T(128)}, u32[]{:S(2)}) copy-start(s32[128]{0:T(128)} %param.27) | copy-start | bytes 1540
  6.5 99.3 %all-gather.2.cloned.1.call-start = ((), (), s32[]{:S(2)}) async-start(), calls=%async_computation.5 | async-start | bytes 4227072 | tf_op jit(solution)/shard_map/all_gather | solution.py:135
  8.0 115.4 %collective-permute-start.3 = (bf16[256,1024]{1,0:T(8,128)(2,1)}, bf16[256,1024]{1,0:T(8,128)(2,1)}, u32[]{:S(2)}, u32[]{:S(2)}) collective-permute-start(bf16[256,1024]{1,0:T(8,128)(2,1)} %param.28), channel_id=1, source_target_pairs={{0,1},{1,2},{2,3},{3,0},{4,5},{5,6},{6,7},{7,4},{8,9},{9,10},{10,1... | collective-permute-start | bytes 1572872 | tf_op jit(solution)/shard_map/ppermute | solution.py:115
  11.4 112.0 %collective-permute-start.4 = (bf16[256,1024]{1,0:T(8,128)(2,1)}, bf16[256,1024]{1,0:T(8,128)(2,1)}, u32[]{:S(2)}, u32[]{:S(2)}) collective-permute-start(bf16[256,1024]{1,0:T(8,128)(2,1)} %param.28), channel_id=1, source_target_pairs={{0,2},{1,3},{2,0},{3,1},{4,6},{5,7},{6,4},{7,5},{8,10},{9,11},{10,... | collective-permute-start | bytes 1572872 | tf_op jit(solution)/shard_map/ppermute | solution.py:115
  26.4 33.7 %all-to-all-start = ((bf16[128,2,576]{2,1,0:T(2,128)(2,1)}), bf16[128,2,576]{2,1,0:T(2,128)(2,1)S(1)}, u32[]{:S(2)}, u32[]{:S(2)}) async-start(bf16[128,2,576]{2,1,0:T(2,128)(2,1)} %reshape.535), calls=%async_computation | async-start | bytes 655360 | tf_op jit(solution)/shard_map/all_to_all | solution.py:143
  61.6 26.6 %copy-start.3 = (bf16[256,16]{0,1:T(8,128)(2,1)S(1)}, bf16[256,16]{0,1:T(8,128)(2,1)}, u32[]{:S(2)}) copy-start(bf16[256,16]{0,1:T(8,128)(2,1)} %param.30) | copy-start | bytes 24580
  63.5 23.5 %all-to-all-start.1 = ((bf16[128,2,576]{2,1,0:T(2,128)(2,1)}), bf16[128,2,576]{2,1,0:T(2,128)(2,1)S(1)}, u32[]{:S(2)}, u32[]{:S(2)}) async-start(bf16[128,2,576]{2,1,0:T(2,128)(2,1)} %reshape.537), calls=%async_computation.1 | async-start | bytes 655360 | tf_op jit(solution)/shard_map/all_to_all | solution.py:145
  88.2 13.9 %collective-permute-start = (bf16[144,256]{1,0:T(8,128)(2,1)S(1)}, bf16[144,256]{1,0:T(8,128)(2,1)S(1)}, u32[]{:S(2)}, u32[]{:S(2)}) collective-permute-start(bf16[144,256]{1,0:T(8,128)(2,1)S(1)} %get-tuple-element.40), channel_id=1, source_target_pairs={{0,1},{1,2},{2,3},{3,0},{4,5},{5,6},{6,7},{7,4},{8,9},{9,10},{10,1... | collective-permute-start | bytes 221192 | tf_op jit(solution)/shard_map/ppermute | solution.py:115
  90.1 15.0 %collective-permute-start.1 = (bf16[144,256]{1,0:T(8,128)(2,1)S(1)}, bf16[144,256]{1,0:T(8,128)(2,1)S(1)}, u32[]{:S(2)}, u32[]{:S(2)}) collective-permute-start(bf16[144,256]{1,0:T(8,128)(2,1)S(1)} %get-tuple-element.40), channel_id=1, source_target_pairs={{0,2},{1,3},{2,0},{3,1},{4,6},{5,7},{6,4},{7,5},{8,10},{9,11},{10,... | collective-permute-start | bytes 221192 | tf_op jit(solution)/shard_map/ppermute | solution.py:115
  94.7 10.4 %collective-permute-start.2 = (bf16[144,256]{1,0:T(8,128)(2,1)S(1)}, bf16[144,256]{1,0:T(8,128)(2,1)S(1)}, u32[]{:S(2)}, u32[]{:S(2)}) collective-permute-start(bf16[144,256]{1,0:T(8,128)(2,1)S(1)} %get-tuple-element.40), channel_id=1, source_target_pairs={{0,3},{1,0},{2,1},{3,2},{4,7},{5,4},{6,5},{7,6},{8,11},{9,8},{10,9... | collective-permute-start | bytes 221192 | tf_op jit(solution)/shard_map/ppermute | solution.py:115
  102.1 21.3 %collective-permute-start.5 = (bf16[256,1024]{1,0:T(8,128)(2,1)}, bf16[256,1024]{1,0:T(8,128)(2,1)}, u32[]{:S(2)}, u32[]{:S(2)}) collective-permute-start(bf16[256,1024]{1,0:T(8,128)(2,1)} %param.28), channel_id=1, source_target_pairs={{0,3},{1,0},{2,1},{3,2},{4,7},{5,4},{6,5},{7,6},{8,11},{9,8},{10,9... | collective-permute-start | bytes 1572872 | tf_op jit(solution)/shard_map/ppermute | solution.py:115
  108.8 1.0 copy-start.2
  112.0 10.6 %all-to-all-start.2 = ((bf16[4,128,256]{2,1,0:T(8,128)(2,1)}), bf16[4,128,256]{2,1,0:T(8,128)(2,1)S(1)}, u32[]{:S(2)}, u32[]{:S(2)}) async-start(bf16[4,128,256]{2,1,0:T(8,128)(2,1)} %broadcast_in_dim.177), calls=%async_computation.2 | async-start | bytes 524288 | tf_op jit(solution)/shard_map/all_to_all | solution.py:170
  123.5 2.9 %copy-start.4 = (f32[1024]{0:T(1024)S(1)}, f32[1024]{0:T(1024)}, u32[]{:S(2)}) copy-start(f32[1024]{0:T(1024)} %param.29) | copy-start | bytes 12292
  125.5 0.8 copy-start.1
  128.6 29.6 %all-to-all-start.3 = ((bf16[16,16,1024]{2,1,0:T(8,128)(2,1)}), bf16[16,16,1024]{2,1,0:T(8,128)(2,1)}, u32[]{:S(2)}, u32[]{:S(2)}) async-start(bf16[16,16,1024]{2,1,0:T(8,128)(2,1)} %broadcast_select_fusion.1), calls=%async_computation.3 | async-start | bytes 1048576 | tf_op jit(solution)/shard_map/all_to_all | solution.py:197
  164.8 26.9 %all-to-all-start.4 = ((bf16[64,16,256]{2,1,0:T(8,128)(2,1)}), bf16[64,16,256]{2,1,0:T(8,128)(2,1)S(1)}, u32[]{:S(2)}, u32[]{:S(2)}) async-start(bf16[64,16,256]{2,1,0:T(8,128)(2,1)} %bitcast.146), calls=%async_computation.4 | async-start | bytes 1048576 | tf_op jit(solution)/shard_map/all_to_all | solution.py:208
Sparse Core Ops, SparseCore 0:
  10.5 94.4 all-gather.1

commit v7 on v6

--- a/solution.py
+++ b/solution.py
@@ -195,11 +195,15 @@
         expert_count, capacity, normed.shape[1]
     )
     slots = lax.all_to_all(send_rows, "ex", split_axis=0, concat_axis=0, tiled=True)
-    gate_act = jnp.einsum("snd,df->snf", slots, gate_weight[0], preferred_element_type=jnp.float32)
-    up_act = jnp.einsum("snd,df->snf", slots, up_weight[0], preferred_element_type=jnp.float32)
+    slot_rows = slots.reshape(expert_count * capacity, slots.shape[2])
+    gate_act = jnp.dot(slot_rows, gate_weight[0], preferred_element_type=jnp.float32)
+    up_act = jnp.dot(slot_rows, up_weight[0], preferred_element_type=jnp.float32)
     expert_hidden = (jax.nn.gelu(gate_act, approximate=True) * up_act).astype(jnp.bfloat16)
-    partial_out = jnp.einsum(
-        "snf,df->snd", expert_hidden, down_weight[0], preferred_element_type=jnp.float32
+    partial_out = lax.dot_general(
+        expert_hidden,
+        down_weight[0],
+        (((1,), (1,)), ((), ())),
+        preferred_element_type=jnp.float32,
     )
     split_part = jnp.transpose(
         partial_out.reshape(expert_count, capacity, head_count, column_width), (0, 2, 1, 3)

time: 204 us -> 200 us (0.980)
  matrix products: 11.2 us -> 8.59 us
    dot_general x2 -> x3, matrix products: 6.59 us -> 3.99 us  [the longest x1 2.74 us: on_device(): lax.dot_general(expert_hidden, down_weight[0], (((1,), (1,)), ((), ())),...]
  transfers between devices with their start and end apart: 12 -> 12, of which waited for: 5 -> 5; matrix products, arithmetic and copies ran while one was open for 17% -> 18% of each run, Pallas kernels for 0% -> 0%
where the time goes in v7:
time: 200 us; the launch traced here: 199 us
  waiting for transfers between devices  70.1 us (35%)
  starting transfers between devices  61.1 us (31%)
  local copies, waits for them, and re-layouts  29.7 us (15%)
  between operations  18.8 us (9%)
  other arithmetic  10.4 us (5%)
  matrix products  8.59 us (4%)
    ppermute x6, starting transfers between devices, head_ring(): lax.ppermute(block, 'head', [(source, (source + shift) % head_count) for...  20 us
    all_to_all x1, waiting for transfers between devices, on_device(): lax.all_to_all(split_part, ('ex', 'head'), split_axis=0, concat_axis=0, t...  18 us
    all_to_all x1, waiting for transfers between devices, on_device(): lax.all_to_all(send_rows, 'ex', split_axis=0, concat_axis=0, tiled=True)  17.8 us
    all_to_all x1, starting transfers between devices, on_device(): lax.all_to_all(pieces, SEQ, split_axis=0, concat_axis=0, tiled=True)  17.4 us
    all_to_all x1, waiting for transfers between devices, on_device(): lax.all_to_all(pieces, SEQ, split_axis=0, concat_axis=0, tiled=True)  14.6 us
    all_to_all x1, waiting for transfers between devices, on_device(): lax.all_to_all(spread, SEQ, split_axis=0, concat_axis=0, tiled=True)  13 us
    all_to_all x1, starting transfers between devices, on_device(): lax.all_to_all(send_rows, 'ex', split_axis=0, concat_axis=0, tiled=True)  7.81 us
    unnamed x26, local copies, waits for them, and re-layouts  7.64 us
  transfers between devices with their start and end apart: 12, of which 5 were waited for; matrix products, arithmetic and copies ran while one was open for 18% of the time, Pallas kernels for 0%

profile of v7, /device:TPU:8, one launch (start us, length us, event | category | flops | bytes accessed | tf_op | source)
XLA Modules:
  0.0 198.8 jit_solution(13802374533519856791)
XLA Ops:
  6.5 1.5 pad_maximum_fusion.2
  8.0 3.4 %collective-permute-start.3 = (bf16[256,1024]{1,0:T(8,128)(2,1)}, bf16[256,1024]{1,0:T(8,128)(2,1)}, u32[]{:S(2)}, u32[]{:S(2)}) collective-permute-start(bf16[256,1024]{1,0:T(8,128)(2,1)} %param.28), channel_id=1, source_target_pairs={{0,1},{1,2},{2,3},{3,0},{4,5},{5,6},{6,7},{7,4},{8,9},{9,10},{10,1... | collective-permute-start | bytes 1572872 | tf_op jit(solution)/shard_map/ppermute | solution.py:115
  11.4 4.6 %collective-permute-start.4 = (bf16[256,1024]{1,0:T(8,128)(2,1)}, bf16[256,1024]{1,0:T(8,128)(2,1)}, u32[]{:S(2)}, u32[]{:S(2)}) collective-permute-start(bf16[256,1024]{1,0:T(8,128)(2,1)} %param.28), channel_id=1, source_target_pairs={{0,2},{1,3},{2,0},{3,1},{4,6},{5,7},{6,4},{7,5},{8,10},{9,11},{10,... | collective-permute-start | bytes 1572872 | tf_op jit(solution)/shard_map/ppermute | solution.py:115
  25.3 1.1 reshape.538
  26.4 17.4 %all-to-all-start = ((bf16[128,2,576]{2,1,0:T(2,128)(2,1)}), bf16[128,2,576]{2,1,0:T(2,128)(2,1)S(1)}, u32[]{:S(2)}, u32[]{:S(2)}) async-start(bf16[128,2,576]{2,1,0:T(2,128)(2,1)} %reshape.538), calls=%async_computation | async-start | bytes 655360 | tf_op jit(solution)/shard_map/all_to_all | solution.py:143
  43.8 1.0 scatter_custom_fusion
  45.3 14.6 %all-to-all-done = bf16[128,2,576]{2,1,0:T(2,128)(2,1)S(1)} async-done(((bf16[128,2,576]{2,1,0:T(2,128)(2,1)}), bf16[128,2,576]{2,1,0:T(2,128)(2,1)S(1)}, u32[]{:S(2)}, u32[]{:S(2)}) %all-to-all-start) | async-done | bytes 294944 | tf_op jit(solution)/shard_map/all_to_all | solution.py:143
  60.5 0.9 gather_fusion
  62.3 1.1 reshape.540
  63.4 6.0 %all-to-all-start.1 = ((bf16[128,2,576]{2,1,0:T(2,128)(2,1)}), bf16[128,2,576]{2,1,0:T(2,128)(2,1)S(1)}, u32[]{:S(2)}, u32[]{:S(2)}) async-start(bf16[128,2,576]{2,1,0:T(2,128)(2,1)} %reshape.540), calls=%async_computation.1 | async-start | bytes 655360 | tf_op jit(solution)/shard_map/all_to_all | solution.py:145
  72.8 1.0 scatter_custom_fusion.1
  73.9 13.0 %all-to-all-done.1 = bf16[128,2,576]{2,1,0:T(2,128)(2,1)S(1)} async-done(((bf16[128,2,576]{2,1,0:T(2,128)(2,1)}), bf16[128,2,576]{2,1,0:T(2,128)(2,1)S(1)}, u32[]{:S(2)}, u32[]{:S(2)}) %all-to-all-start.1) | async-done | bytes 294944 | tf_op jit(solution)/shard_map/all_to_all | solution.py:145
  88.2 1.9 collective-permute-start
  90.1 4.5 %collective-permute-start.1 = (bf16[144,256]{1,0:T(8,128)(2,1)S(1)}, bf16[144,256]{1,0:T(8,128)(2,1)S(1)}, u32[]{:S(2)}, u32[]{:S(2)}) collective-permute-start(bf16[144,256]{1,0:T(8,128)(2,1)S(1)} %get-tuple-element.40), channel_id=1, source_target_pairs={{0,2},{1,3},{2,0},{3,1},{4,6},{5,7},{6,4},{7,5},{8,10},{9,11},{10,... | collective-permute-start | bytes 221192 | tf_op jit(solution)/shard_map/ppermute | solution.py:115
  94.6 2.6 %collective-permute-start.2 = (bf16[144,256]{1,0:T(8,128)(2,1)S(1)}, bf16[144,256]{1,0:T(8,128)(2,1)S(1)}, u32[]{:S(2)}, u32[]{:S(2)}) collective-permute-start(bf16[144,256]{1,0:T(8,128)(2,1)S(1)} %get-tuple-element.40), channel_id=1, source_target_pairs={{0,3},{1,0},{2,1},{3,2},{4,7},{5,4},{6,5},{7,6},{8,11},{9,8},{10,9... | collective-permute-start | bytes 221192 | tf_op jit(solution)/shard_map/ppermute | solution.py:115
  99.4 1.4 scatter_custom_fusion.2
  101.2 0.9 fusion.75
  102.1 2.9 %collective-permute-start.5 = (bf16[256,1024]{1,0:T(8,128)(2,1)}, bf16[256,1024]{1,0:T(8,128)(2,1)}, u32[]{:S(2)}, u32[]{:S(2)}) collective-permute-start(bf16[256,1024]{1,0:T(8,128)(2,1)} %param.28), channel_id=1, source_target_pairs={{0,3},{1,0},{2,1},{3,2},{4,7},{5,4},{6,5},{7,6},{8,11},{9,8},{10,9... | collective-permute-start | bytes 1572872 | tf_op jit(solution)/shard_map/ppermute | solution.py:115
  105.8 2.8 %gather_fusion.2 = bf16[32,32,512]{2,1,0:T(8,128)(2,1)S(1)} fusion(bf16[128,32,512]{2,1,0:T(8,128)(2,1)} %all-gather.2.cloned.1.call-done, s32[1024]{0:T(1024)S(1)} %pad_clamp_fusion.1), kind=kCustom, calls=%fused_computation.2 | custom fusion | bytes 2097280 | tf_op jit(solution)/shard_map/jit(_take)/gather | solution.py:156
  112.0 3.9 %all-to-all-start.2 = ((bf16[4,128,256]{2,1,0:T(8,128)(2,1)}), bf16[4,128,256]{2,1,0:T(8,128)(2,1)S(1)}, u32[]{:S(2)}, u32[]{:S(2)}) async-start(bf16[4,128,256]{2,1,0:T(8,128)(2,1)} %broadcast_in_dim.177), calls=%async_computation.2 | async-start | bytes 524288 | tf_op jit(solution)/shard_map/all_to_all | solution.py:170
  116.0 6.6 %all-to-all-done.2 = bf16[4,128,256]{2,1,0:T(8,128)(2,1)S(1)} async-done(((bf16[4,128,256]{2,1,0:T(8,128)(2,1)}), bf16[4,128,256]{2,1,0:T(8,128)(2,1)S(1)}, u32[]{:S(2)}, u32[]{:S(2)}) %all-to-all-start.2) | async-done | bytes 262176 | tf_op jit(solution)/shard_map/all_to_all | solution.py:170
  123.5 2.1 %multiply_reduce_fusion.1 = (f32[128]{0:T(128)S(1)}, f32[128,1024]{1,0:T(8,128)S(1)}) fusion(f32[128,1024]{1,0:T(8,128)S(1)} %bitcast.144, bf16[128,1024]{0,1:T(8,128)(2,1)S(1)} %bitcast.148, bf16[256,1024]{1,0:T(8,128)(2,1)} %collective-permute-done.5, bf16[256,1024]{1,0:T(8,128)(2,1)} %collective-permute-done.4, ...), kind=kOutput, calls=%fused_computation.48 | convolution fusion | flops 277217152 | bytes 3408384 | tf_op jit(solution)/shard_map/dot_general | solution.py:174
  125.7 1.2 gather_fusion.4
  126.9 0.9 broadcast_select_fusion.1
  127.8 7.8 %all-to-all-start.3 = ((bf16[16,16,1024]{2,1,0:T(8,128)(2,1)}), bf16[16,16,1024]{2,1,0:T(8,128)(2,1)S(1)}, u32[]{:S(2)}, u32[]{:S(2)}) async-start(bf16[16,16,1024]{2,1,0:T(8,128)(2,1)} %broadcast_select_fusion.1), calls=%async_computation.3 | async-start | bytes 1048576 | tf_op jit(solution)/shard_map/all_to_all | solution.py:197
  135.6 4.0 %dot_general.40 = bf16[4,256,704]{1,0,2:T(4,128)(2,1)} reshape(bf16[1,1024,704]{1,2,0:T(8,128)(2,1)} %param.34) | data formatting | bytes 2883584 | tf_op jit(solution)/shard_map/dot_general | solution.py:202
  139.6 17.8 %all-to-all-done.3 = bf16[16,16,1024]{2,1,0:T(8,128)(2,1)S(1)} async-done(((bf16[16,16,1024]{2,1,0:T(8,128)(2,1)}), bf16[16,16,1024]{2,1,0:T(8,128)(2,1)S(1)}, u32[]{:S(2)}, u32[]{:S(2)}) %all-to-all-start.3) | async-done | bytes 524320 | tf_op jit(solution)/shard_map/all_to_all | solution.py:197
  159.5 2.7 %fusion.16 = bf16[16,16,4,256]{3,1,2,0:T(8,128)(2,1)} fusion(bf16[16,16,704,1]{2,1,3,0:T(8,128)(2,1)S(1)} %bitcast.147, bf16[4,256,704]{1,0,2:T(4,128)(2,1)} %dot_general.40), kind=kOutput, calls=%fused_computation.29 | convolution fusion | flops 369360896 | bytes 2326528 | tf_op jit(solution)/shard_map/dot_general | solution.py:202
  162.2 6.1 %all-to-all-start.4 = ((bf16[64,16,256]{2,1,0:T(8,128)(2,1)}), bf16[64,16,256]{2,1,0:T(8,128)(2,1)S(1)}, u32[]{:S(2)}, u32[]{:S(2)}) async-start(bf16[64,16,256]{2,1,0:T(8,128)(2,1)} %bitcast.143), calls=%async_computation.4 | async-start | bytes 1048576 | tf_op jit(solution)/shard_map/all_to_all | solution.py:212
  168.8 2.0 gather_fusion.6
  171.1 18.0 %all-to-all-done.4 = bf16[64,16,256]{2,1,0:T(8,128)(2,1)S(1)} async-done(((bf16[64,16,256]{2,1,0:T(8,128)(2,1)}), bf16[64,16,256]{2,1,0:T(8,128)(2,1)S(1)}, u32[]{:S(2)}, u32[]{:S(2)}) %all-to-all-start.4) | async-done | bytes 524320 | tf_op jit(solution)/shard_map/all_to_all | solution.py:212
  189.2 1.7 gather_fusion.5
  (125 shorter events, 22.7 us)
Async XLA Ops:
  6.5 150.8 %copy-start = (bf16[1,1024,704]{1,2,0:T(8,128)(2,1)S(1)}, bf16[1,1024,704]{1,2,0:T(8,128)(2,1)}, u32[]{:S(2)}) copy-start(bf16[1,1024,704]{1,2,0:T(8,128)(2,1)} %param.32) | copy-start | bytes 4325380
  6.5 37.2 %copy-start.6 = (s32[128]{0:T(128)S(1)}, s32[128]{0:T(128)}, u32[]{:S(2)}) copy-start(s32[128]{0:T(128)} %param.35) | copy-start | bytes 1540
  6.5 38.3 %copy-start.5 = (s32[128]{0:T(128)S(1)}, s32[128]{0:T(128)}, u32[]{:S(2)}) copy-start(s32[128]{0:T(128)} %param.27) | copy-start | bytes 1540
  6.5 99.3 %all-gather.2.cloned.1.call-start = ((), (), s32[]{:S(2)}) async-start(), calls=%async_computation.5 | async-start | bytes 4227072 | tf_op jit(solution)/shard_map/all_gather | solution.py:135
  8.0 115.4 %collective-permute-start.3 = (bf16[256,1024]{1,0:T(8,128)(2,1)}, bf16[256,1024]{1,0:T(8,128)(2,1)}, u32[]{:S(2)}, u32[]{:S(2)}) collective-permute-start(bf16[256,1024]{1,0:T(8,128)(2,1)} %param.28), channel_id=1, source_target_pairs={{0,1},{1,2},{2,3},{3,0},{4,5},{5,6},{6,7},{7,4},{8,9},{9,10},{10,1... | collective-permute-start | bytes 1572872 | tf_op jit(solution)/shard_map/ppermute | solution.py:115
  11.4 112.0 %collective-permute-start.4 = (bf16[256,1024]{1,0:T(8,128)(2,1)}, bf16[256,1024]{1,0:T(8,128)(2,1)}, u32[]{:S(2)}, u32[]{:S(2)}) collective-permute-start(bf16[256,1024]{1,0:T(8,128)(2,1)} %param.28), channel_id=1, source_target_pairs={{0,2},{1,3},{2,0},{3,1},{4,6},{5,7},{6,4},{7,5},{8,10},{9,11},{10,... | collective-permute-start | bytes 1572872 | tf_op jit(solution)/shard_map/ppermute | solution.py:115
  26.4 33.6 %all-to-all-start = ((bf16[128,2,576]{2,1,0:T(2,128)(2,1)}), bf16[128,2,576]{2,1,0:T(2,128)(2,1)S(1)}, u32[]{:S(2)}, u32[]{:S(2)}) async-start(bf16[128,2,576]{2,1,0:T(2,128)(2,1)} %reshape.538), calls=%async_computation | async-start | bytes 655360 | tf_op jit(solution)/shard_map/all_to_all | solution.py:143
  61.5 26.7 %copy-start.3 = (bf16[256,16]{0,1:T(8,128)(2,1)S(1)}, bf16[256,16]{0,1:T(8,128)(2,1)}, u32[]{:S(2)}) copy-start(bf16[256,16]{0,1:T(8,128)(2,1)} %param.30) | copy-start | bytes 24580
  63.4 23.6 %all-to-all-start.1 = ((bf16[128,2,576]{2,1,0:T(2,128)(2,1)}), bf16[128,2,576]{2,1,0:T(2,128)(2,1)S(1)}, u32[]{:S(2)}, u32[]{:S(2)}) async-start(bf16[128,2,576]{2,1,0:T(2,128)(2,1)} %reshape.540), calls=%async_computation.1 | async-start | bytes 655360 | tf_op jit(solution)/shard_map/all_to_all | solution.py:145
  88.2 13.9 %collective-permute-start = (bf16[144,256]{1,0:T(8,128)(2,1)S(1)}, bf16[144,256]{1,0:T(8,128)(2,1)S(1)}, u32[]{:S(2)}, u32[]{:S(2)}) collective-permute-start(bf16[144,256]{1,0:T(8,128)(2,1)S(1)} %get-tuple-element.40), channel_id=1, source_target_pairs={{0,1},{1,2},{2,3},{3,0},{4,5},{5,6},{6,7},{7,4},{8,9},{9,10},{10,1... | collective-permute-start | bytes 221192 | tf_op jit(solution)/shard_map/ppermute | solution.py:115
  90.1 15.0 %collective-permute-start.1 = (bf16[144,256]{1,0:T(8,128)(2,1)S(1)}, bf16[144,256]{1,0:T(8,128)(2,1)S(1)}, u32[]{:S(2)}, u32[]{:S(2)}) collective-permute-start(bf16[144,256]{1,0:T(8,128)(2,1)S(1)} %get-tuple-element.40), channel_id=1, source_target_pairs={{0,2},{1,3},{2,0},{3,1},{4,6},{5,7},{6,4},{7,5},{8,10},{9,11},{10,... | collective-permute-start | bytes 221192 | tf_op jit(solution)/shard_map/ppermute | solution.py:115
  94.6 10.5 %collective-permute-start.2 = (bf16[144,256]{1,0:T(8,128)(2,1)S(1)}, bf16[144,256]{1,0:T(8,128)(2,1)S(1)}, u32[]{:S(2)}, u32[]{:S(2)}) collective-permute-start(bf16[144,256]{1,0:T(8,128)(2,1)S(1)} %get-tuple-element.40), channel_id=1, source_target_pairs={{0,3},{1,0},{2,1},{3,2},{4,7},{5,4},{6,5},{7,6},{8,11},{9,8},{10,9... | collective-permute-start | bytes 221192 | tf_op jit(solution)/shard_map/ppermute | solution.py:115
  102.1 21.3 %collective-permute-start.5 = (bf16[256,1024]{1,0:T(8,128)(2,1)}, bf16[256,1024]{1,0:T(8,128)(2,1)}, u32[]{:S(2)}, u32[]{:S(2)}) collective-permute-start(bf16[256,1024]{1,0:T(8,128)(2,1)} %param.28), channel_id=1, source_target_pairs={{0,3},{1,0},{2,1},{3,2},{4,7},{5,4},{6,5},{7,6},{8,11},{9,8},{10,9... | collective-permute-start | bytes 1572872 | tf_op jit(solution)/shard_map/ppermute | solution.py:115
  108.8 1.0 copy-start.2
  112.0 10.6 %all-to-all-start.2 = ((bf16[4,128,256]{2,1,0:T(8,128)(2,1)}), bf16[4,128,256]{2,1,0:T(8,128)(2,1)S(1)}, u32[]{:S(2)}, u32[]{:S(2)}) async-start(bf16[4,128,256]{2,1,0:T(8,128)(2,1)} %broadcast_in_dim.177), calls=%async_computation.2 | async-start | bytes 524288 | tf_op jit(solution)/shard_map/all_to_all | solution.py:170
  123.5 2.1 %copy-start.4 = (f32[1024]{0:T(1024)S(1)}, f32[1024]{0:T(1024)}, u32[]{:S(2)}) copy-start(f32[1024]{0:T(1024)} %param.29) | copy-start | bytes 12292
  127.8 29.6 %all-to-all-start.3 = ((bf16[16,16,1024]{2,1,0:T(8,128)(2,1)}), bf16[16,16,1024]{2,1,0:T(8,128)(2,1)S(1)}, u32[]{:S(2)}, u32[]{:S(2)}) async-start(bf16[16,16,1024]{2,1,0:T(8,128)(2,1)} %broadcast_select_fusion.1), calls=%async_computation.3 | async-start | bytes 1048576 | tf_op jit(solution)/shard_map/all_to_all | solution.py:197
  157.4 1.4 copy-start.1
  162.2 26.9 %all-to-all-start.4 = ((bf16[64,16,256]{2,1,0:T(8,128)(2,1)}), bf16[64,16,256]{2,1,0:T(8,128)(2,1)S(1)}, u32[]{:S(2)}, u32[]{:S(2)}) async-start(bf16[64,16,256]{2,1,0:T(8,128)(2,1)} %bitcast.143), calls=%async_computation.4 | async-start | bytes 1048576 | tf_op jit(solution)/shard_map/all_to_all | solution.py:212
Sparse Core Ops, SparseCore 0:
  10.5 94.3 all-gather.1

commit v8 on v7

--- a/solution.py
+++ b/solution.py
@@ -191,8 +191,13 @@
         .at[slot_flat]
         .set(jnp.arange(pair_count, dtype=jnp.int32), mode="drop")
     )
-    send_rows = jnp.take(normed, slot_pair // TOPK, axis=0).reshape(
-        expert_count, capacity, normed.shape[1]
+    send_pick = (
+        (slot_pair // TOPK)[:, None] == jnp.arange(row_count, dtype=jnp.int32)[None, :]
+    ).astype(jnp.bfloat16)
+    send_rows = (
+        jnp.dot(send_pick, normed, preferred_element_type=jnp.float32)
+        .astype(jnp.bfloat16)
+        .reshape(expert_count, capacity, normed.shape[1])
     )
     slots = lax.all_to_all(send_rows, "ex", split_axis=0, concat_axis=0, tiled=True)
     slot_rows = slots.reshape(expert_count * capacity, slots.shape[2])
@@ -212,9 +217,14 @@
     arrived = lax.all_to_all(split_part, ("ex", "head"), split_axis=0, concat_axis=0, tiled=True)
     arrived = arrived.reshape(expert_count, head_count, capacity, column_width)
     returned = jnp.sum(arrived.astype(jnp.float32), axis=1).astype(jnp.bfloat16)
-    picked = (
-        returned[expert_flat, slot_rank].astype(jnp.float32).reshape(row_count, TOPK, column_width)
-    )
+    return_pick = (
+        slot_flat[:, None] == jnp.arange(expert_count * capacity, dtype=jnp.int32)[None, :]
+    ).astype(jnp.bfloat16)
+    picked = jnp.dot(
+        return_pick,
+        returned.reshape(expert_count * capacity, column_width),
+        preferred_element_type=jnp.float32,
+    ).reshape(row_count, TOPK, column_width)
     resid_columns = lax.dynamic_slice_in_dim(resid, head_index * column_width, column_width, 1)
     layer = resid_columns + gate_first[:, None] * picked[:, 0] + gate_second[:, None] * picked[:, 1]
     layer = layer.astype(jnp.bfloat16)

time: 200 us -> 197 us (0.985)
  local copies, waits for them, and re-layouts: 29.7 us -> 26.8 us
    gather x2 -> x0, local copies, waits for them, and re-layouts: 2.83 us -> none  [the longest x1 1.66 us: on_device(): returned[expert_flat, slot_rank].astype(jnp.float32)]
where the time goes in v8:
time: 197 us; the launch traced here: 196 us
  waiting for transfers between devices  70 us (36%)
  starting transfers between devices  60.8 us (31%)
  local copies, waits for them, and re-layouts  26.8 us (14%)
  between operations  18.8 us (10%)
  matrix products  10 us (5%)
  other arithmetic  9.38 us (5%)
    ppermute x6, starting transfers between devices, head_ring(): lax.ppermute(block, 'head', [(source, (source + shift) % head_count) for...  20 us
    all_to_all x1, waiting for transfers between devices, on_device(): lax.all_to_all(split_part, ('ex', 'head'), split_axis=0, concat_axis=0, t...  17.9 us
    all_to_all x1, waiting for transfers between devices, on_device(): lax.all_to_all(send_rows, 'ex', split_axis=0, concat_axis=0, tiled=True)  17.8 us
    all_to_all x1, starting transfers between devices, on_device(): lax.all_to_all(pieces, SEQ, split_axis=0, concat_axis=0, tiled=True)  17.4 us
    all_to_all x1, waiting for transfers between devices, on_device(): lax.all_to_all(pieces, SEQ, split_axis=0, concat_axis=0, tiled=True)  14.6 us
    all_to_all x1, waiting for transfers between devices, on_device(): lax.all_to_all(spread, SEQ, split_axis=0, concat_axis=0, tiled=True)  13 us
    unnamed x26, local copies, waits for them, and re-layouts  7.65 us
    all_to_all x1, starting transfers between devices, on_device(): lax.all_to_all(send_rows, 'ex', split_axis=0, concat_axis=0, tiled=True)  7.51 us
  transfers between devices with their start and end apart: 12, of which 5 were waited for; matrix products, arithmetic and copies ran while one was open for 18% of the time, Pallas kernels for 0%

profile of v8, /device:TPU:8, one launch (start us, length us, event | category | flops | bytes accessed | tf_op | source)
XLA Modules:
  0.0 195.9 jit_solution(16335075992545849184)
XLA Ops:
  6.5 1.5 pad_maximum_fusion.2
  8.0 3.4 %collective-permute-start.3 = (bf16[256,1024]{1,0:T(8,128)(2,1)}, bf16[256,1024]{1,0:T(8,128)(2,1)}, u32[]{:S(2)}, u32[]{:S(2)}) collective-permute-start(bf16[256,1024]{1,0:T(8,128)(2,1)} %param.28), channel_id=1, source_target_pairs={{0,1},{1,2},{2,3},{3,0},{4,5},{5,6},{6,7},{7,4},{8,9},{9,10},{10,1... | collective-permute-start | bytes 1572872 | tf_op jit(solution)/shard_map/ppermute | solution.py:115
  11.4 4.6 %collective-permute-start.4 = (bf16[256,1024]{1,0:T(8,128)(2,1)}, bf16[256,1024]{1,0:T(8,128)(2,1)}, u32[]{:S(2)}, u32[]{:S(2)}) collective-permute-start(bf16[256,1024]{1,0:T(8,128)(2,1)} %param.28), channel_id=1, source_target_pairs={{0,2},{1,3},{2,0},{3,1},{4,6},{5,7},{6,4},{7,5},{8,10},{9,11},{10,... | collective-permute-start | bytes 1572872 | tf_op jit(solution)/shard_map/ppermute | solution.py:115
  20.5 0.8 constant_dynamic-update-slice_fusion.4
  22.2 0.8 constant_dynamic-update-slice_fusion.2
  25.3 1.1 reshape.503
  26.4 17.4 %all-to-all-start = ((bf16[128,2,576]{2,1,0:T(2,128)(2,1)}), bf16[128,2,576]{2,1,0:T(2,128)(2,1)S(1)}, u32[]{:S(2)}, u32[]{:S(2)}) async-start(bf16[128,2,576]{2,1,0:T(2,128)(2,1)} %reshape.503), calls=%async_computation | async-start | bytes 655360 | tf_op jit(solution)/shard_map/all_to_all | solution.py:143
  43.8 1.0 scatter_custom_fusion
  45.3 14.6 %all-to-all-done = bf16[128,2,576]{2,1,0:T(2,128)(2,1)S(1)} async-done(((bf16[128,2,576]{2,1,0:T(2,128)(2,1)}), bf16[128,2,576]{2,1,0:T(2,128)(2,1)S(1)}, u32[]{:S(2)}, u32[]{:S(2)}) %all-to-all-start) | async-done | bytes 294944 | tf_op jit(solution)/shard_map/all_to_all | solution.py:143
  60.5 0.9 gather_fusion
  62.3 1.1 reshape.505
  63.4 6.0 %all-to-all-start.1 = ((bf16[128,2,576]{2,1,0:T(2,128)(2,1)}), bf16[128,2,576]{2,1,0:T(2,128)(2,1)S(1)}, u32[]{:S(2)}, u32[]{:S(2)}) async-start(bf16[128,2,576]{2,1,0:T(2,128)(2,1)} %reshape.505), calls=%async_computation.1 | async-start | bytes 655360 | tf_op jit(solution)/shard_map/all_to_all | solution.py:145
  72.8 1.0 scatter_custom_fusion.1
  73.9 13.0 %all-to-all-done.1 = bf16[128,2,576]{2,1,0:T(2,128)(2,1)S(1)} async-done(((bf16[128,2,576]{2,1,0:T(2,128)(2,1)}), bf16[128,2,576]{2,1,0:T(2,128)(2,1)S(1)}, u32[]{:S(2)}, u32[]{:S(2)}) %all-to-all-start.1) | async-done | bytes 294944 | tf_op jit(solution)/shard_map/all_to_all | solution.py:145
  88.2 1.9 collective-permute-start
  90.1 4.5 %collective-permute-start.1 = (bf16[144,256]{1,0:T(8,128)(2,1)S(1)}, bf16[144,256]{1,0:T(8,128)(2,1)S(1)}, u32[]{:S(2)}, u32[]{:S(2)}) collective-permute-start(bf16[144,256]{1,0:T(8,128)(2,1)S(1)} %get-tuple-element.36), channel_id=1, source_target_pairs={{0,2},{1,3},{2,0},{3,1},{4,6},{5,7},{6,4},{7,5},{8,10},{9,11},{10,... | collective-permute-start | bytes 221192 | tf_op jit(solution)/shard_map/ppermute | solution.py:115
  94.6 2.6 %collective-permute-start.2 = (bf16[144,256]{1,0:T(8,128)(2,1)S(1)}, bf16[144,256]{1,0:T(8,128)(2,1)S(1)}, u32[]{:S(2)}, u32[]{:S(2)}) collective-permute-start(bf16[144,256]{1,0:T(8,128)(2,1)S(1)} %get-tuple-element.36), channel_id=1, source_target_pairs={{0,3},{1,0},{2,1},{3,2},{4,7},{5,4},{6,5},{7,6},{8,11},{9,8},{10,9... | collective-permute-start | bytes 221192 | tf_op jit(solution)/shard_map/ppermute | solution.py:115
  99.8 1.4 scatter_custom_fusion.2
  101.4 0.9 fusion.76
  102.4 2.9 %collective-permute-start.5 = (bf16[256,1024]{1,0:T(8,128)(2,1)}, bf16[256,1024]{1,0:T(8,128)(2,1)}, u32[]{:S(2)}, u32[]{:S(2)}) collective-permute-start(bf16[256,1024]{1,0:T(8,128)(2,1)} %param.28), channel_id=1, source_target_pairs={{0,3},{1,0},{2,1},{3,2},{4,7},{5,4},{6,5},{7,6},{8,11},{9,8},{10,9... | collective-permute-start | bytes 1572872 | tf_op jit(solution)/shard_map/ppermute | solution.py:115
  106.1 2.8 %gather_fusion.2 = bf16[32,32,512]{2,1,0:T(8,128)(2,1)S(1)} fusion(bf16[128,32,512]{2,1,0:T(8,128)(2,1)} %all-gather.2.cloned.1.call-done, s32[1024]{0:T(1024)S(1)} %pad_clamp_fusion), kind=kCustom, calls=%fused_computation.2 | custom fusion | bytes 2097280 | tf_op jit(solution)/shard_map/jit(_take)/gather | solution.py:156
  112.3 3.9 %all-to-all-start.2 = ((bf16[4,128,256]{2,1,0:T(8,128)(2,1)}), bf16[4,128,256]{2,1,0:T(8,128)(2,1)S(1)}, u32[]{:S(2)}, u32[]{:S(2)}) async-start(bf16[4,128,256]{2,1,0:T(8,128)(2,1)} %broadcast_in_dim.165), calls=%async_computation.2 | async-start | bytes 524288 | tf_op jit(solution)/shard_map/all_to_all | solution.py:170
  116.3 6.6 %all-to-all-done.2 = bf16[4,128,256]{2,1,0:T(8,128)(2,1)S(1)} async-done(((bf16[4,128,256]{2,1,0:T(8,128)(2,1)}), bf16[4,128,256]{2,1,0:T(8,128)(2,1)S(1)}, u32[]{:S(2)}, u32[]{:S(2)}) %all-to-all-start.2) | async-done | bytes 262176 | tf_op jit(solution)/shard_map/all_to_all | solution.py:170
  123.7 2.1 %multiply_reduce_fusion.1 = (f32[128]{0:T(128)S(1)}, f32[128,1024]{1,0:T(8,128)S(1)}) fusion(f32[128,1024]{1,0:T(8,128)S(1)} %bitcast.148, bf16[128,1024]{0,1:T(8,128)(2,1)S(1)} %bitcast.152, bf16[256,1024]{1,0:T(8,128)(2,1)} %collective-permute-done.5, bf16[256,1024]{1,0:T(8,128)(2,1)} %collective-permute-done.4, ...), kind=kOutput, calls=%fused_computation.47 | convolution fusion | flops 277217152 | bytes 3408384 | tf_op jit(solution)/shard_map/dot_general | solution.py:174
  125.8 1.2 convolution_convert_fusion
  127.0 7.5 %all-to-all-start.3 = ((bf16[16,16,1024]{2,1,0:T(8,128)(2,1)}), bf16[16,16,1024]{2,1,0:T(8,128)(2,1)S(1)}, u32[]{:S(2)}, u32[]{:S(2)}) async-start(bf16[16,16,1024]{2,1,0:T(8,128)(2,1)} %bitcast.24), calls=%async_computation.3 | async-start | bytes 1048576 | tf_op jit(solution)/shard_map/all_to_all | solution.py:202
  134.5 4.0 %dot_general.47 = bf16[4,256,704]{1,0,2:T(4,128)(2,1)} reshape(bf16[1,1024,704]{1,2,0:T(8,128)(2,1)} %param.34) | data formatting | bytes 2883584 | tf_op jit(solution)/shard_map/dot_general | solution.py:207
  138.5 17.8 %all-to-all-done.3 = bf16[16,16,1024]{2,1,0:T(8,128)(2,1)S(1)} async-done(((bf16[16,16,1024]{2,1,0:T(8,128)(2,1)}), bf16[16,16,1024]{2,1,0:T(8,128)(2,1)S(1)}, u32[]{:S(2)}, u32[]{:S(2)}) %all-to-all-start.3) | async-done | bytes 524320 | tf_op jit(solution)/shard_map/all_to_all | solution.py:202
  158.4 2.7 %fusion.16 = bf16[16,16,4,256]{3,1,2,0:T(8,128)(2,1)} fusion(bf16[16,16,704,1]{2,1,3,0:T(8,128)(2,1)S(1)} %bitcast.151, bf16[4,256,704]{1,0,2:T(4,128)(2,1)} %dot_general.47), kind=kOutput, calls=%fused_computation.27 | convolution fusion | flops 369360896 | bytes 2326528 | tf_op jit(solution)/shard_map/dot_general | solution.py:207
  161.1 6.2 %all-to-all-start.4 = ((bf16[64,16,256]{2,1,0:T(8,128)(2,1)}), bf16[64,16,256]{2,1,0:T(8,128)(2,1)S(1)}, u32[]{:S(2)}, u32[]{:S(2)}) async-start(bf16[64,16,256]{2,1,0:T(8,128)(2,1)} %bitcast.147), calls=%async_computation.4 | async-start | bytes 1048576 | tf_op jit(solution)/shard_map/all_to_all | solution.py:217
  167.8 2.0 %gather_fusion.4 = f32[256]{0:T(256)S(1)} fusion(f32[128,16]{0,1:T(8,128)S(1)} %fusion.73, s32[256]{0:T(256)S(1)} %reshape.454), kind=kCustom, calls=%fused_computation.4 | custom fusion | bytes 4096 | tf_op jit(solution)/shard_map/jit(take_along_axis)/gather | solution.py:181
  170.1 17.9 %all-to-all-done.4 = bf16[64,16,256]{2,1,0:T(8,128)(2,1)S(1)} async-done(((bf16[64,16,256]{2,1,0:T(8,128)(2,1)}), bf16[64,16,256]{2,1,0:T(8,128)(2,1)S(1)}, u32[]{:S(2)}, u32[]{:S(2)}) %all-to-all-start.4) | async-done | bytes 524320 | tf_op jit(solution)/shard_map/all_to_all | solution.py:217
  (123 shorter events, 21.1 us)
Async XLA Ops:
  6.5 149.7 %copy-start = (bf16[1,1024,704]{1,2,0:T(8,128)(2,1)S(1)}, bf16[1,1024,704]{1,2,0:T(8,128)(2,1)}, u32[]{:S(2)}) copy-start(bf16[1,1024,704]{1,2,0:T(8,128)(2,1)} %param.32) | copy-start | bytes 4325380
  6.5 37.2 %copy-start.6 = (s32[128]{0:T(128)S(1)}, s32[128]{0:T(128)}, u32[]{:S(2)}) copy-start(s32[128]{0:T(128)} %param.35) | copy-start | bytes 1540
  6.5 38.3 %copy-start.5 = (s32[128]{0:T(128)S(1)}, s32[128]{0:T(128)}, u32[]{:S(2)}) copy-start(s32[128]{0:T(128)} %param.27) | copy-start | bytes 1540
  6.5 99.6 %all-gather.2.cloned.1.call-start = ((), (), s32[]{:S(2)}) async-start(), calls=%async_computation.5 | async-start | bytes 4227072 | tf_op jit(solution)/shard_map/all_gather | solution.py:135
  8.0 115.7 %collective-permute-start.3 = (bf16[256,1024]{1,0:T(8,128)(2,1)}, bf16[256,1024]{1,0:T(8,128)(2,1)}, u32[]{:S(2)}, u32[]{:S(2)}) collective-permute-start(bf16[256,1024]{1,0:T(8,128)(2,1)} %param.28), channel_id=1, source_target_pairs={{0,1},{1,2},{2,3},{3,0},{4,5},{5,6},{6,7},{7,4},{8,9},{9,10},{10,1... | collective-permute-start | bytes 1572872 | tf_op jit(solution)/shard_map/ppermute | solution.py:115
  11.4 112.3 %collective-permute-start.4 = (bf16[256,1024]{1,0:T(8,128)(2,1)}, bf16[256,1024]{1,0:T(8,128)(2,1)}, u32[]{:S(2)}, u32[]{:S(2)}) collective-permute-start(bf16[256,1024]{1,0:T(8,128)(2,1)} %param.28), channel_id=1, source_target_pairs={{0,2},{1,3},{2,0},{3,1},{4,6},{5,7},{6,4},{7,5},{8,10},{9,11},{10,... | collective-permute-start | bytes 1572872 | tf_op jit(solution)/shard_map/ppermute | solution.py:115
  26.4 33.6 %all-to-all-start = ((bf16[128,2,576]{2,1,0:T(2,128)(2,1)}), bf16[128,2,576]{2,1,0:T(2,128)(2,1)S(1)}, u32[]{:S(2)}, u32[]{:S(2)}) async-start(bf16[128,2,576]{2,1,0:T(2,128)(2,1)} %reshape.503), calls=%async_computation | async-start | bytes 655360 | tf_op jit(solution)/shard_map/all_to_all | solution.py:143
  61.5 26.7 %copy-start.4 = (bf16[256,16]{0,1:T(8,128)(2,1)S(1)}, bf16[256,16]{0,1:T(8,128)(2,1)}, u32[]{:S(2)}) copy-start(bf16[256,16]{0,1:T(8,128)(2,1)} %param.30) | copy-start | bytes 24580
  63.4 23.6 %all-to-all-start.1 = ((bf16[128,2,576]{2,1,0:T(2,128)(2,1)}), bf16[128,2,576]{2,1,0:T(2,128)(2,1)S(1)}, u32[]{:S(2)}, u32[]{:S(2)}) async-start(bf16[128,2,576]{2,1,0:T(2,128)(2,1)} %reshape.505), calls=%async_computation.1 | async-start | bytes 655360 | tf_op jit(solution)/shard_map/all_to_all | solution.py:145
  88.2 14.2 %collective-permute-start = (bf16[144,256]{1,0:T(8,128)(2,1)S(1)}, bf16[144,256]{1,0:T(8,128)(2,1)S(1)}, u32[]{:S(2)}, u32[]{:S(2)}) collective-permute-start(bf16[144,256]{1,0:T(8,128)(2,1)S(1)} %get-tuple-element.36), channel_id=1, source_target_pairs={{0,1},{1,2},{2,3},{3,0},{4,5},{5,6},{6,7},{7,4},{8,9},{9,10},{10,1... | collective-permute-start | bytes 221192 | tf_op jit(solution)/shard_map/ppermute | solution.py:115
  90.1 15.2 %collective-permute-start.1 = (bf16[144,256]{1,0:T(8,128)(2,1)S(1)}, bf16[144,256]{1,0:T(8,128)(2,1)S(1)}, u32[]{:S(2)}, u32[]{:S(2)}) collective-permute-start(bf16[144,256]{1,0:T(8,128)(2,1)S(1)} %get-tuple-element.36), channel_id=1, source_target_pairs={{0,2},{1,3},{2,0},{3,1},{4,6},{5,7},{6,4},{7,5},{8,10},{9,11},{10,... | collective-permute-start | bytes 221192 | tf_op jit(solution)/shard_map/ppermute | solution.py:115
  94.6 10.7 %collective-permute-start.2 = (bf16[144,256]{1,0:T(8,128)(2,1)S(1)}, bf16[144,256]{1,0:T(8,128)(2,1)S(1)}, u32[]{:S(2)}, u32[]{:S(2)}) collective-permute-start(bf16[144,256]{1,0:T(8,128)(2,1)S(1)} %get-tuple-element.36), channel_id=1, source_target_pairs={{0,3},{1,0},{2,1},{3,2},{4,7},{5,4},{6,5},{7,6},{8,11},{9,8},{10,9... | collective-permute-start | bytes 221192 | tf_op jit(solution)/shard_map/ppermute | solution.py:115
  102.4 21.3 %collective-permute-start.5 = (bf16[256,1024]{1,0:T(8,128)(2,1)}, bf16[256,1024]{1,0:T(8,128)(2,1)}, u32[]{:S(2)}, u32[]{:S(2)}) collective-permute-start(bf16[256,1024]{1,0:T(8,128)(2,1)} %param.28), channel_id=1, source_target_pairs={{0,3},{1,0},{2,1},{3,2},{4,7},{5,4},{6,5},{7,6},{8,11},{9,8},{10,9... | collective-permute-start | bytes 1572872 | tf_op jit(solution)/shard_map/ppermute | solution.py:115
  109.1 1.0 copy-start.2
  112.3 10.6 %all-to-all-start.2 = ((bf16[4,128,256]{2,1,0:T(8,128)(2,1)}), bf16[4,128,256]{2,1,0:T(8,128)(2,1)S(1)}, u32[]{:S(2)}, u32[]{:S(2)}) async-start(bf16[4,128,256]{2,1,0:T(8,128)(2,1)} %broadcast_in_dim.165), calls=%async_computation.2 | async-start | bytes 524288 | tf_op jit(solution)/shard_map/all_to_all | solution.py:170
  123.7 2.1 %copy-start.3 = (f32[1024]{0:T(1024)S(1)}, f32[1024]{0:T(1024)}, u32[]{:S(2)}) copy-start(f32[1024]{0:T(1024)} %param.29) | copy-start | bytes 12292
  127.0 29.3 %all-to-all-start.3 = ((bf16[16,16,1024]{2,1,0:T(8,128)(2,1)}), bf16[16,16,1024]{2,1,0:T(8,128)(2,1)S(1)}, u32[]{:S(2)}, u32[]{:S(2)}) async-start(bf16[16,16,1024]{2,1,0:T(8,128)(2,1)} %bitcast.24), calls=%async_computation.3 | async-start | bytes 1048576 | tf_op jit(solution)/shard_map/all_to_all | solution.py:202
  156.3 1.4 copy-start.1
  161.1 26.9 %all-to-all-start.4 = ((bf16[64,16,256]{2,1,0:T(8,128)(2,1)}), bf16[64,16,256]{2,1,0:T(8,128)(2,1)S(1)}, u32[]{:S(2)}, u32[]{:S(2)}) async-start(bf16[64,16,256]{2,1,0:T(8,128)(2,1)} %bitcast.147), calls=%async_computation.4 | async-start | bytes 1048576 | tf_op jit(solution)/shard_map/all_to_all | solution.py:217
Sparse Core Ops, SparseCore 0:
  10.5 94.3 all-gather.1

commit v9 on v8

--- a/solution.py
+++ b/solution.py
@@ -153,7 +153,14 @@
     routes = moved[:, tail : tail + TOPK].astype(jnp.int32)
     length = moved[0, tail + TOPK].astype(jnp.int32)
     chosen = lax.dynamic_slice_in_dim(inverse, group_index * group_pages, group_pages, 0)
-    held_pages = jnp.take(all_pages, chosen, axis=0)
+    page_pick = (
+        chosen[:, None] == jnp.arange(all_pages.shape[0], dtype=jnp.int32)[None, :]
+    ).astype(jnp.bfloat16)
+    held_pages = (
+        jnp.dot(page_pick, all_pages.reshape(all_pages.shape[0], -1), preferred_element_type=jnp.float32)
+        .astype(jnp.bfloat16)
+        .reshape(group_pages, page_rows, all_pages.shape[2])
+    )
     prefix_keys = held_pages[:, :, :features].reshape(group_pages * page_rows, features)
     prefix_values = held_pages[:, :, features:].reshape(group_pages * page_rows, features)
     attended = attend_rows(

time: 197 us -> 200 us (1.015)
  local copies, waits for them, and re-layouts: 26.8 us -> 29.2 us
    unnamed x26, local copies, waits for them, and re-layouts: 7.65 us -> 12.8 us
    gather x1 -> x0, local copies, waits for them, and re-layouts: 2.8 us -> none  [on_device(): held_pages = jnp.take(all_pages, chosen, axis=0)]
  transfers between devices with their start and end apart: 12 -> 12, of which waited for: 5 -> 5; matrix products, arithmetic and copies ran while one was open for 18% -> 19% of each run, Pallas kernels for 0% -> 0%
where the time goes in v9:
time: 200 us; the launch traced here: 199 us
  waiting for transfers between devices  70.2 us (35%)
  starting transfers between devices  61.4 us (31%)
  local copies, waits for them, and re-layouts  29.2 us (15%)
  between operations  18.8 us (9%)
  matrix products  10.1 us (5%)
  other arithmetic  9.13 us (5%)
    ppermute x6, starting transfers between devices, head_ring(): lax.ppermute(block, 'head', [(source, (source + shift) % head_count) for...  20 us
    all_to_all x1, waiting for transfers between devices, on_device(): lax.all_to_all(split_part, ('ex', 'head'), split_axis=0, concat_axis=0, t...  18.2 us
    all_to_all x1, waiting for transfers between devices, on_device(): lax.all_to_all(send_rows, 'ex', split_axis=0, concat_axis=0, tiled=True)  17.6 us
    all_to_all x1, starting transfers between devices, on_device(): lax.all_to_all(pieces, SEQ, split_axis=0, concat_axis=0, tiled=True)  17.4 us
    all_to_all x1, waiting for transfers between devices, on_device(): lax.all_to_all(pieces, SEQ, split_axis=0, concat_axis=0, tiled=True)  14.8 us
    all_to_all x1, waiting for transfers between devices, on_device(): lax.all_to_all(spread, SEQ, split_axis=0, concat_axis=0, tiled=True)  13 us
    unnamed x26, local copies, waits for them, and re-layouts  12.8 us
    all_to_all x1, starting transfers between devices, on_device(): lax.all_to_all(send_rows, 'ex', split_axis=0, concat_axis=0, tiled=True)  8.17 us
  transfers between devices with their start and end apart: 12, of which 5 were waited for; matrix products, arithmetic and copies ran while one was open for 19% of the time, Pallas kernels for 0%

profile of v9, /device:TPU:8, one launch (start us, length us, event | category | flops | bytes accessed | tf_op | source)
XLA Modules:
  0.0 198.8 jit_solution(16620345777408166909)
XLA Ops:
  6.5 1.5 pad_maximum_fusion.2
  8.0 3.4 %collective-permute-start.3 = (bf16[256,1024]{1,0:T(8,128)(2,1)}, bf16[256,1024]{1,0:T(8,128)(2,1)}, u32[]{:S(2)}, u32[]{:S(2)}) collective-permute-start(bf16[256,1024]{1,0:T(8,128)(2,1)} %param.28), channel_id=1, source_target_pairs={{0,1},{1,2},{2,3},{3,0},{4,5},{5,6},{6,7},{7,4},{8,9},{9,10},{10,1... | collective-permute-start | bytes 1572872 | tf_op jit(solution)/shard_map/ppermute | solution.py:115
  11.4 4.6 %collective-permute-start.4 = (bf16[256,1024]{1,0:T(8,128)(2,1)}, bf16[256,1024]{1,0:T(8,128)(2,1)}, u32[]{:S(2)}, u32[]{:S(2)}) collective-permute-start(bf16[256,1024]{1,0:T(8,128)(2,1)} %param.28), channel_id=1, source_target_pairs={{0,2},{1,3},{2,0},{3,1},{4,6},{5,7},{6,4},{7,5},{8,10},{9,11},{10,... | collective-permute-start | bytes 1572872 | tf_op jit(solution)/shard_map/ppermute | solution.py:115
  20.5 0.8 constant_dynamic-update-slice_fusion.4
  21.3 0.8 constant_dynamic-update-slice_fusion.3
  22.2 0.8 constant_dynamic-update-slice_fusion.2
  25.3 1.1 reshape.498
  26.4 17.4 %all-to-all-start = ((bf16[128,2,576]{2,1,0:T(2,128)(2,1)}), bf16[128,2,576]{2,1,0:T(2,128)(2,1)S(1)}, u32[]{:S(2)}, u32[]{:S(2)}) async-start(bf16[128,2,576]{2,1,0:T(2,128)(2,1)} %reshape.498), calls=%async_computation | async-start | bytes 655360 | tf_op jit(solution)/shard_map/all_to_all | solution.py:143
  43.8 1.0 scatter_custom_fusion
  45.3 14.8 %all-to-all-done = bf16[128,2,576]{2,1,0:T(2,128)(2,1)S(1)} async-done(((bf16[128,2,576]{2,1,0:T(2,128)(2,1)}), bf16[128,2,576]{2,1,0:T(2,128)(2,1)S(1)}, u32[]{:S(2)}, u32[]{:S(2)}) %all-to-all-start) | async-done | bytes 294944 | tf_op jit(solution)/shard_map/all_to_all | solution.py:143
  60.6 0.9 gather_fusion
  62.5 1.1 reshape.500
  63.5 5.8 %all-to-all-start.1 = ((bf16[128,2,576]{2,1,0:T(2,128)(2,1)}), bf16[128,2,576]{2,1,0:T(2,128)(2,1)S(1)}, u32[]{:S(2)}, u32[]{:S(2)}) async-start(bf16[128,2,576]{2,1,0:T(2,128)(2,1)} %reshape.500), calls=%async_computation.1 | async-start | bytes 655360 | tf_op jit(solution)/shard_map/all_to_all | solution.py:145
  72.9 1.0 scatter_custom_fusion.1
  74.0 13.0 %all-to-all-done.1 = bf16[128,2,576]{2,1,0:T(2,128)(2,1)S(1)} async-done(((bf16[128,2,576]{2,1,0:T(2,128)(2,1)}), bf16[128,2,576]{2,1,0:T(2,128)(2,1)S(1)}, u32[]{:S(2)}, u32[]{:S(2)}) %all-to-all-start.1) | async-done | bytes 294944 | tf_op jit(solution)/shard_map/all_to_all | solution.py:145
  88.2 1.9 collective-permute-start
  90.2 4.5 %collective-permute-start.1 = (bf16[144,256]{1,0:T(8,128)(2,1)S(1)}, bf16[144,256]{1,0:T(8,128)(2,1)S(1)}, u32[]{:S(2)}, u32[]{:S(2)}) collective-permute-start(bf16[144,256]{1,0:T(8,128)(2,1)S(1)} %get-tuple-element.34), channel_id=1, source_target_pairs={{0,2},{1,3},{2,0},{3,1},{4,6},{5,7},{6,4},{7,5},{8,10},{9,11},{10,... | collective-permute-start | bytes 221192 | tf_op jit(solution)/shard_map/ppermute | solution.py:115
  94.7 2.5 %collective-permute-start.2 = (bf16[144,256]{1,0:T(8,128)(2,1)S(1)}, bf16[144,256]{1,0:T(8,128)(2,1)S(1)}, u32[]{:S(2)}, u32[]{:S(2)}) collective-permute-start(bf16[144,256]{1,0:T(8,128)(2,1)S(1)} %get-tuple-element.34), channel_id=1, source_target_pairs={{0,3},{1,0},{2,1},{3,2},{4,7},{5,4},{6,5},{7,6},{8,11},{9,8},{10,9... | collective-permute-start | bytes 221192 | tf_op jit(solution)/shard_map/ppermute | solution.py:115
  99.8 1.4 scatter_custom_fusion.2
  101.7 2.9 %collective-permute-start.5 = (bf16[256,1024]{1,0:T(8,128)(2,1)}, bf16[256,1024]{1,0:T(8,128)(2,1)}, u32[]{:S(2)}, u32[]{:S(2)}) collective-permute-start(bf16[256,1024]{1,0:T(8,128)(2,1)} %param.28), channel_id=1, source_target_pairs={{0,3},{1,0},{2,1},{3,2},{4,7},{5,4},{6,5},{7,6},{8,11},{9,8},{10,9... | collective-permute-start | bytes 1572872 | tf_op jit(solution)/shard_map/ppermute | solution.py:115
  105.4 5.1 %copy.80 = bf16[16,8,32,512]{3,1,2,0:T(8,128)(2,1)S(1)} copy(bf16[16,8,32,512]{3,2,1,0:T(8,128)(2,1)} %bitcast.141) | data formatting | bytes 8388608
  114.5 3.9 %all-to-all-start.2 = ((bf16[4,128,256]{2,1,0:T(8,128)(2,1)}), bf16[4,128,256]{2,1,0:T(8,128)(2,1)S(1)}, u32[]{:S(2)}, u32[]{:S(2)}) async-start(bf16[4,128,256]{2,1,0:T(8,128)(2,1)} %broadcast_in_dim.152), calls=%async_computation.2 | async-start | bytes 524288 | tf_op jit(solution)/shard_map/all_to_all | solution.py:177
  118.5 6.6 %all-to-all-done.2 = bf16[4,128,256]{2,1,0:T(8,128)(2,1)S(1)} async-done(((bf16[4,128,256]{2,1,0:T(8,128)(2,1)}), bf16[4,128,256]{2,1,0:T(8,128)(2,1)S(1)}, u32[]{:S(2)}, u32[]{:S(2)}) %all-to-all-start.2) | async-done | bytes 262176 | tf_op jit(solution)/shard_map/all_to_all | solution.py:177
  125.9 2.1 %multiply_reduce_fusion.1 = (f32[128]{0:T(128)S(1)}, f32[128,1024]{1,0:T(8,128)S(1)}) fusion(f32[128,1024]{1,0:T(8,128)S(1)} %bitcast.157, bf16[128,1024]{0,1:T(8,128)(2,1)S(1)} %bitcast.161, bf16[256,1024]{1,0:T(8,128)(2,1)} %collective-permute-done.5, bf16[256,1024]{1,0:T(8,128)(2,1)} %collective-permute-done.4, ...), kind=kOutput, calls=%fused_computation.46 | convolution fusion | flops 277217152 | bytes 3408384 | tf_op jit(solution)/shard_map/dot_general | solution.py:181
  128.0 1.2 convolution_convert_fusion.1
  129.2 8.2 %all-to-all-start.3 = ((bf16[16,16,1024]{2,1,0:T(8,128)(2,1)}), bf16[16,16,1024]{2,1,0:T(8,128)(2,1)S(1)}, u32[]{:S(2)}, u32[]{:S(2)}) async-start(bf16[16,16,1024]{2,1,0:T(8,128)(2,1)} %bitcast.24), calls=%async_computation.3 | async-start | bytes 1048576 | tf_op jit(solution)/shard_map/all_to_all | solution.py:209
  137.4 4.0 %dot_general.51 = bf16[4,256,704]{1,0,2:T(4,128)(2,1)} reshape(bf16[1,1024,704]{1,2,0:T(8,128)(2,1)} %param.34) | data formatting | bytes 2883584 | tf_op jit(solution)/shard_map/dot_general | solution.py:214
  141.4 17.6 %all-to-all-done.3 = bf16[16,16,1024]{2,1,0:T(8,128)(2,1)S(1)} async-done(((bf16[16,16,1024]{2,1,0:T(8,128)(2,1)}), bf16[16,16,1024]{2,1,0:T(8,128)(2,1)S(1)}, u32[]{:S(2)}, u32[]{:S(2)}) %all-to-all-start.3) | async-done | bytes 524320 | tf_op jit(solution)/shard_map/all_to_all | solution.py:209
  161.1 2.7 %fusion.16 = bf16[16,16,4,256]{3,1,2,0:T(8,128)(2,1)} fusion(bf16[16,16,704,1]{2,1,3,0:T(8,128)(2,1)S(1)} %bitcast.160, bf16[4,256,704]{1,0,2:T(4,128)(2,1)} %dot_general.51), kind=kOutput, calls=%fused_computation.27 | convolution fusion | flops 369360896 | bytes 2326528 | tf_op jit(solution)/shard_map/dot_general | solution.py:214
  163.8 6.2 %all-to-all-start.4 = ((bf16[64,16,256]{2,1,0:T(8,128)(2,1)}), bf16[64,16,256]{2,1,0:T(8,128)(2,1)S(1)}, u32[]{:S(2)}, u32[]{:S(2)}) async-start(bf16[64,16,256]{2,1,0:T(8,128)(2,1)} %bitcast.156), calls=%async_computation.4 | async-start | bytes 1048576 | tf_op jit(solution)/shard_map/all_to_all | solution.py:224
  170.5 2.0 gather_fusion.3
  172.8 18.2 %all-to-all-done.4 = bf16[64,16,256]{2,1,0:T(8,128)(2,1)S(1)} async-done(((bf16[64,16,256]{2,1,0:T(8,128)(2,1)}), bf16[64,16,256]{2,1,0:T(8,128)(2,1)S(1)}, u32[]{:S(2)}, u32[]{:S(2)}) %all-to-all-start.4) | async-done | bytes 524320 | tf_op jit(solution)/shard_map/all_to_all | solution.py:224
  (121 shorter events, 21.0 us)
Async XLA Ops:
  6.5 152.4 %copy-start = (bf16[1,1024,704]{1,2,0:T(8,128)(2,1)S(1)}, bf16[1,1024,704]{1,2,0:T(8,128)(2,1)}, u32[]{:S(2)}) copy-start(bf16[1,1024,704]{1,2,0:T(8,128)(2,1)} %param.32) | copy-start | bytes 4325380
  6.5 37.2 %copy-start.5 = (s32[128]{0:T(128)S(1)}, s32[128]{0:T(128)}, u32[]{:S(2)}) copy-start(s32[128]{0:T(128)} %param.35) | copy-start | bytes 1540
  6.5 38.2 %copy-start.4 = (s32[128]{0:T(128)S(1)}, s32[128]{0:T(128)}, u32[]{:S(2)}) copy-start(s32[128]{0:T(128)} %param.27) | copy-start | bytes 1540
  6.5 98.9 %all-gather.2.cloned.1.call-start = ((), (), s32[]{:S(2)}) async-start(), calls=%async_computation.5 | async-start | bytes 4227072 | tf_op jit(solution)/shard_map/all_gather | solution.py:135
  8.0 117.9 %collective-permute-start.3 = (bf16[256,1024]{1,0:T(8,128)(2,1)}, bf16[256,1024]{1,0:T(8,128)(2,1)}, u32[]{:S(2)}, u32[]{:S(2)}) collective-permute-start(bf16[256,1024]{1,0:T(8,128)(2,1)} %param.28), channel_id=1, source_target_pairs={{0,1},{1,2},{2,3},{3,0},{4,5},{5,6},{6,7},{7,4},{8,9},{9,10},{10,1... | collective-permute-start | bytes 1572872 | tf_op jit(solution)/shard_map/ppermute | solution.py:115
  11.4 114.5 %collective-permute-start.4 = (bf16[256,1024]{1,0:T(8,128)(2,1)}, bf16[256,1024]{1,0:T(8,128)(2,1)}, u32[]{:S(2)}, u32[]{:S(2)}) collective-permute-start(bf16[256,1024]{1,0:T(8,128)(2,1)} %param.28), channel_id=1, source_target_pairs={{0,2},{1,3},{2,0},{3,1},{4,6},{5,7},{6,4},{7,5},{8,10},{9,11},{10,... | collective-permute-start | bytes 1572872 | tf_op jit(solution)/shard_map/ppermute | solution.py:115
  26.4 33.7 %all-to-all-start = ((bf16[128,2,576]{2,1,0:T(2,128)(2,1)}), bf16[128,2,576]{2,1,0:T(2,128)(2,1)S(1)}, u32[]{:S(2)}, u32[]{:S(2)}) async-start(bf16[128,2,576]{2,1,0:T(2,128)(2,1)} %reshape.498), calls=%async_computation | async-start | bytes 655360 | tf_op jit(solution)/shard_map/all_to_all | solution.py:143
  61.6 26.6 %copy-start.3 = (bf16[256,16]{0,1:T(8,128)(2,1)S(1)}, bf16[256,16]{0,1:T(8,128)(2,1)}, u32[]{:S(2)}) copy-start(bf16[256,16]{0,1:T(8,128)(2,1)} %param.30) | copy-start | bytes 24580
  63.5 23.5 %all-to-all-start.1 = ((bf16[128,2,576]{2,1,0:T(2,128)(2,1)}), bf16[128,2,576]{2,1,0:T(2,128)(2,1)S(1)}, u32[]{:S(2)}, u32[]{:S(2)}) async-start(bf16[128,2,576]{2,1,0:T(2,128)(2,1)} %reshape.500), calls=%async_computation.1 | async-start | bytes 655360 | tf_op jit(solution)/shard_map/all_to_all | solution.py:145
  88.2 13.5 %collective-permute-start = (bf16[144,256]{1,0:T(8,128)(2,1)S(1)}, bf16[144,256]{1,0:T(8,128)(2,1)S(1)}, u32[]{:S(2)}, u32[]{:S(2)}) collective-permute-start(bf16[144,256]{1,0:T(8,128)(2,1)S(1)} %get-tuple-element.34), channel_id=1, source_target_pairs={{0,1},{1,2},{2,3},{3,0},{4,5},{5,6},{6,7},{7,4},{8,9},{9,10},{10,1... | collective-permute-start | bytes 221192 | tf_op jit(solution)/shard_map/ppermute | solution.py:115
  90.2 14.5 %collective-permute-start.1 = (bf16[144,256]{1,0:T(8,128)(2,1)S(1)}, bf16[144,256]{1,0:T(8,128)(2,1)S(1)}, u32[]{:S(2)}, u32[]{:S(2)}) collective-permute-start(bf16[144,256]{1,0:T(8,128)(2,1)S(1)} %get-tuple-element.34), channel_id=1, source_target_pairs={{0,2},{1,3},{2,0},{3,1},{4,6},{5,7},{6,4},{7,5},{8,10},{9,11},{10,... | collective-permute-start | bytes 221192 | tf_op jit(solution)/shard_map/ppermute | solution.py:115
  94.7 10.0 %collective-permute-start.2 = (bf16[144,256]{1,0:T(8,128)(2,1)S(1)}, bf16[144,256]{1,0:T(8,128)(2,1)S(1)}, u32[]{:S(2)}, u32[]{:S(2)}) collective-permute-start(bf16[144,256]{1,0:T(8,128)(2,1)S(1)} %get-tuple-element.34), channel_id=1, source_target_pairs={{0,3},{1,0},{2,1},{3,2},{4,7},{5,4},{6,5},{7,6},{8,11},{9,8},{10,9... | collective-permute-start | bytes 221192 | tf_op jit(solution)/shard_map/ppermute | solution.py:115
  101.7 24.2 %collective-permute-start.5 = (bf16[256,1024]{1,0:T(8,128)(2,1)}, bf16[256,1024]{1,0:T(8,128)(2,1)}, u32[]{:S(2)}, u32[]{:S(2)}) collective-permute-start(bf16[256,1024]{1,0:T(8,128)(2,1)} %param.28), channel_id=1, source_target_pairs={{0,3},{1,0},{2,1},{3,2},{4,7},{5,4},{6,5},{7,6},{8,11},{9,8},{10,9... | collective-permute-start | bytes 1572872 | tf_op jit(solution)/shard_map/ppermute | solution.py:115
  114.5 10.6 %all-to-all-start.2 = ((bf16[4,128,256]{2,1,0:T(8,128)(2,1)}), bf16[4,128,256]{2,1,0:T(8,128)(2,1)S(1)}, u32[]{:S(2)}, u32[]{:S(2)}) async-start(bf16[4,128,256]{2,1,0:T(8,128)(2,1)} %broadcast_in_dim.152), calls=%async_computation.2 | async-start | bytes 524288 | tf_op jit(solution)/shard_map/all_to_all | solution.py:177
  125.9 2.1 %copy-start.2 = (f32[1024]{0:T(1024)S(1)}, f32[1024]{0:T(1024)}, u32[]{:S(2)}) copy-start(f32[1024]{0:T(1024)} %param.29) | copy-start | bytes 12292
  129.2 29.7 %all-to-all-start.3 = ((bf16[16,16,1024]{2,1,0:T(8,128)(2,1)}), bf16[16,16,1024]{2,1,0:T(8,128)(2,1)S(1)}, u32[]{:S(2)}, u32[]{:S(2)}) async-start(bf16[16,16,1024]{2,1,0:T(8,128)(2,1)} %bitcast.24), calls=%async_computation.3 | async-start | bytes 1048576 | tf_op jit(solution)/shard_map/all_to_all | solution.py:209
  159.0 1.4 copy-start.1
  163.8 27.1 %all-to-all-start.4 = ((bf16[64,16,256]{2,1,0:T(8,128)(2,1)}), bf16[64,16,256]{2,1,0:T(8,128)(2,1)S(1)}, u32[]{:S(2)}, u32[]{:S(2)}) async-start(bf16[64,16,256]{2,1,0:T(8,128)(2,1)} %bitcast.156), calls=%async_computation.4 | async-start | bytes 1048576 | tf_op jit(solution)/shard_map/all_to_all | solution.py:224
Sparse Core Ops, SparseCore 0:
  10.5 94.4 all-gather.1
